TPU v7x, 128 devices: a whole 4x4x4 slice. The times are simulated.
128 devices in a mesh: ctx: 16 (over x, z_lo, core), tp: 8 (over z_hi, y).
Axes of the slice: x: 4, y: 4, z: 4 (z_hi: 2, z_lo: 2; z = z_hi * 2 + z_lo), core: 2. Of those that a mesh axis runs over, the one named last changes fastest.
Arguments:
- queries: bfloat16 [16384, 8192], P(('ctx', 'tp')), may hold values from -48 to 48
- key_rows: bfloat16 [16384, 1024], P('ctx', 'tp'), may hold values from -8 to 8
- value_rows: bfloat16 [16384, 1024], P('ctx', 'tp'), may hold values from -6 to 6
- out_grad: bfloat16 [16384, 8192], P(('ctx', 'tp')), may hold values from -6 to 6
- doc_ids: int32 [16384], replicated, may hold values from 0 to 31, never falling along the last dimension, each value on 1 to 1408 neighbouring positions
- block_owner: int32 [128], replicated, may hold values from 0 to 15, as said below
Outputs:
- attended: bfloat16 [16384, 8192], P('ctx', 'tp')
- query_grad: bfloat16 [16384, 8192], P('ctx', 'tp')
- key_grad: bfloat16 [16384, 1024], P('ctx', 'tp')
- value_grad: bfloat16 [16384, 1024], P('ctx', 'tp')
Inputs may be any that keep to these rules, and one draw needn't show every extreme that they name: `doc_ids`: ids never fall along the sequence; every document has 1 to 1408 tokens and one has exactly 1408. `block_owner`: every context shard takes exactly 8 blocks, and at most one of the blocks s * 8 to (s + 1) * 8 - 1 of any index s.
All inputs are finite; a program needn't handle non-finite values.
Results may differ from a plain program's by a relative error of at most 0.012.
The roundings to bfloat16 on the way count: a program that leaves them out, or rounds other values in their place, can miss the bound.
Values may be sent and summed in bfloat16 or wider, within the bound.
No kernel may reach another device: no remote copies, remote signals or barrier semaphores. Data moves between devices by JAX's collectives and lax.ppermute only.
A program may use at most 128 MiB of HBM per device.

v0:
```python
import jax
import jax.numpy as jnp
from jax import lax
from jax.sharding import PartitionSpec as P

HEADS = 64
KV_HEADS = 8
HEAD_DIM = 128
BLOCK = 128
BAND = 12


def routing(block_owner, ctx_count, ctx_rank, blocks_here):
    owner_grid = block_owner.reshape(ctx_count, blocks_here)
    own_targets = lax.dynamic_index_in_dim(owner_grid, ctx_rank, 0, keepdims=False)
    targets = jnp.arange(ctx_count, dtype=jnp.int32)
    send_pick = (own_targets[None, :] == targets[:, None]).astype(jnp.bfloat16)
    arrivals = (owner_grid == ctx_rank).astype(jnp.int32)
    present = jnp.sum(arrivals, axis=1)
    arrival_rank = jnp.cumsum(present) - 1
    slot_index = jnp.arange(blocks_here, dtype=jnp.int32)
    chosen = (present[None, :] == 1) & (arrival_rank[None, :] == slot_index[:, None])
    source_block = targets * blocks_here + jnp.sum(arrivals * slot_index[None, :], axis=1)
    held_ids = jnp.sum(chosen.astype(jnp.int32) * source_block[None, :], axis=1)
    return (send_pick, chosen.astype(jnp.bfloat16), held_ids)


def select_rows(selector, blocks):
    picked = jnp.einsum("ab,brh->arh", selector, blocks, preferred_element_type=jnp.float32)
    return picked.astype(jnp.bfloat16)


def windows(key_src, value_src, block_id):
    window_rows = BAND * BLOCK
    kv_local = key_src.shape[1] // HEAD_DIM
    window_start = jnp.maximum(block_id - BAND + 1, 0) * BLOCK
    key_window = lax.dynamic_slice_in_dim(key_src, window_start, window_rows, 0)
    value_window = lax.dynamic_slice_in_dim(value_src, window_start, window_rows, 0)
    key_window = key_window.reshape(window_rows, kv_local, HEAD_DIM)
    value_window = value_window.reshape(window_rows, kv_local, HEAD_DIM)
    return (window_start, key_window, value_window)


def masked_scores(query_block, key_window, block_id, window_start, doc_ids):
    window_rows = key_window.shape[0]
    kv_local = key_window.shape[1]
    query_heads = query_block.reshape(BLOCK, kv_local, HEADS // KV_HEADS, HEAD_DIM)
    raw_scores = jnp.einsum(
        "qkgd,wkd->kgqw", query_heads, key_window, preferred_element_type=jnp.float32
    ) * HEAD_DIM ** (-0.5)
    query_pos = block_id * BLOCK + jnp.arange(BLOCK, dtype=jnp.int32)
    key_pos = window_start + jnp.arange(window_rows, dtype=jnp.int32)
    query_doc = lax.dynamic_slice_in_dim(doc_ids, block_id * BLOCK, BLOCK, 0)
    key_doc = lax.dynamic_slice_in_dim(doc_ids, window_start, window_rows, 0)
    allowed = (query_doc[:, None] == key_doc[None, :]) & (key_pos[None, :] <= query_pos[:, None])
    return (jnp.where(allowed[None, None], raw_scores, -1e30), query_heads)


def attend_forward(held_query, block_ids, key_src, value_src, doc_ids):

    def advance(running, inputs):
        query_block, block_id = inputs
        window_start, key_window, value_window = windows(key_src, value_src, block_id)
        scores, _ = masked_scores(query_block, key_window, block_id, window_start, doc_ids)
        row_max = jnp.max(scores, axis=-1, keepdims=True)
        log_total = row_max + jnp.log(jnp.sum(jnp.exp(scores - row_max), axis=-1, keepdims=True))
        soft_low = jnp.exp(scores - log_total).astype(jnp.bfloat16)
        natural_out = jnp.einsum(
            "kgqw,wkd->qkgd", soft_low, value_window, preferred_element_type=jnp.float32
        )
        return (running, (natural_out.reshape(BLOCK, -1).astype(jnp.bfloat16), log_total))

    _, (out_blocks, log_totals) = lax.scan(
        advance, jnp.zeros((), jnp.float32), (held_query, block_ids)
    )
    return (out_blocks, log_totals)


def attend_backward(
    held_query, held_grad, out_blocks, log_totals, block_ids, key_src, value_src, doc_ids
):
    window_rows = BAND * BLOCK
    inv_root = HEAD_DIM ** (-0.5)

    def advance(running, inputs):
        key_grad, value_grad = running
        query_block, grad_block, out_block, log_total, block_id = inputs
        window_start, key_window, value_window = windows(key_src, value_src, block_id)
        scores, query_heads = masked_scores(
            query_block, key_window, block_id, window_start, doc_ids
        )
        grad_heads = grad_block.reshape(query_heads.shape)
        out_heads = out_block.reshape(query_heads.shape)
        weights = jnp.exp(scores - log_total)
        soft_low = weights.astype(jnp.bfloat16)
        row_dot = jnp.sum(grad_heads.astype(jnp.float32) * out_heads.astype(jnp.float32), axis=-1)
        row_dot = jnp.transpose(row_dot, (1, 2, 0))[..., None]
        prob_grad = jnp.einsum(
            "qkgd,wkd->kgqw", grad_heads, value_window, preferred_element_type=jnp.float32
        )
        score_grad = (weights * (prob_grad - row_dot)).astype(jnp.bfloat16)
        query_part = (
            jnp.einsum("kgqw,wkd->qkgd", score_grad, key_window, preferred_element_type=jnp.float32)
            * inv_root
        )
        key_part = (
            jnp.einsum(
                "kgqw,qkgd->wkd", score_grad, query_heads, preferred_element_type=jnp.float32
            )
            * inv_root
        )
        value_part = jnp.einsum(
            "kgqw,qkgd->wkd", soft_low, grad_heads, preferred_element_type=jnp.float32
        )
        old_keys = lax.dynamic_slice_in_dim(key_grad, window_start, window_rows, 0)
        old_values = lax.dynamic_slice_in_dim(value_grad, window_start, window_rows, 0)
        key_grad = lax.dynamic_update_slice_in_dim(
            key_grad, old_keys + key_part.reshape(window_rows, -1), window_start, 0
        )
        value_grad = lax.dynamic_update_slice_in_dim(
            value_grad, old_values + value_part.reshape(window_rows, -1), window_start, 0
        )
        return ((key_grad, value_grad), query_part.reshape(BLOCK, -1).astype(jnp.bfloat16))

    zero_grads = (jnp.zeros(key_src.shape, jnp.float32), jnp.zeros(value_src.shape, jnp.float32))
    (key_grad, value_grad), dq_blocks = lax.scan(
        advance, zero_grads, (held_query, held_grad, out_blocks, log_totals, block_ids)
    )
    return (dq_blocks, key_grad, value_grad)


def on_device(queries, key_rows, value_rows, out_grad, doc_ids, block_owner):
    ctx_count = lax.axis_size("ctx")
    tp_count = lax.axis_size("tp")
    ctx_rank = lax.axis_index("ctx")
    local_rows, width = queries.shape
    head_cols = width // tp_count
    tok_dev = key_rows.shape[0]
    blocks_here = tok_dev // BLOCK
    send_pick, recv_pick, held_ids = routing(block_owner, ctx_count, ctx_rank, blocks_here)
    query_split, grad_split = (
        lax.all_to_all(
            queries.reshape(local_rows, tp_count, head_cols),
            "tp",
            split_axis=1,
            concat_axis=0,
            tiled=True,
        ),
        lax.all_to_all(
            out_grad.reshape(local_rows, tp_count, head_cols),
            "tp",
            split_axis=1,
            concat_axis=0,
            tiled=True,
        ),
    )
    query_blocks = query_split.reshape(blocks_here, BLOCK, head_cols)
    grad_blocks = grad_split.reshape(blocks_here, BLOCK, head_cols)
    arrived_query, arrived_grad = (
        lax.all_to_all(
            select_rows(send_pick, query_blocks), "ctx", split_axis=0, concat_axis=0, tiled=True
        ),
        lax.all_to_all(
            select_rows(send_pick, grad_blocks), "ctx", split_axis=0, concat_axis=0, tiled=True
        ),
    )
    held_query = select_rows(recv_pick, arrived_query)
    held_grad = select_rows(recv_pick, arrived_grad)
    key_src, value_src = (
        lax.all_gather(key_rows, "ctx", axis=0, tiled=True),
        lax.all_gather(value_rows, "ctx", axis=0, tiled=True),
    )
    out_blocks, log_totals = attend_forward(held_query, held_ids, key_src, value_src, doc_ids)
    dq_blocks, key_grad, value_grad = attend_backward(
        held_query, held_grad, out_blocks, log_totals, held_ids, key_src, value_src, doc_ids
    )
    key_total, value_total = (
        lax.psum_scatter(key_grad, "ctx", scatter_dimension=0, tiled=True),
        lax.psum_scatter(value_grad, "ctx", scatter_dimension=0, tiled=True),
    )
    return (
        out_blocks.reshape(tok_dev, head_cols),
        dq_blocks.reshape(tok_dev, head_cols),
        key_total.astype(jnp.bfloat16),
        value_total.astype(jnp.bfloat16),
    )


def solution(mesh):
    return jax.shard_map(
        on_device,
        mesh=mesh,
        in_specs=(
            P(("ctx", "tp"), None),
            P("ctx", "tp"),
            P("ctx", "tp"),
            P(("ctx", "tp"), None),
            P(),
            P(),
        ),
        out_specs=(P("ctx", "tp"), P("ctx", "tp"), P("ctx", "tp"), P("ctx", "tp")),
        check_vma=False,
    )
```

profile of v0, /device:TPU:60, one launch (start us, length us, event | category | flops | bytes accessed | tf_op | source)
XLA Modules:
  0.0 739.5 jit_solution(2950701493769142610)
XLA Ops:
  7.9 3.2 copy.76
  13.7 7.1 all-to-all-start
  20.8 4.1 copy.84
  24.9 4.0 copy.85
  28.9 19.6 %all-to-all-done = bf16[128,8,1024]{2,0,1:T(8,128)(2,1)S(1)} async-done(((bf16[128,8,1024]{2,0,1:T(8,128)(2,1)}), bf16[128,8,1024]{2,0,1:T(8,128)(2,1)S(1)}, u32[]{:S(2)}, u32[]{:S(2)}) %all-to-all-start) | async-done | bytes 2097184 | tf_op jit(solution)/shard_map/all_to_all | solution.py:142
  49.7 6.9 all-to-all-start.2
  56.8 3.2 convolution_convert_fusion.1
  59.9 4.3 copy.79
  64.2 17.0 %all-to-all-done.2 = bf16[128,8,1024]{2,0,1:T(8,128)(2,1)S(1)} async-done(((bf16[128,8,1024]{2,0,1:T(8,128)(2,1)}), bf16[128,8,1024]{2,0,1:T(8,128)(2,1)S(1)}, u32[]{:S(2)}, u32[]{:S(2)}) %all-to-all-start.2) | async-done | bytes 2097184 | tf_op jit(solution)/shard_map/all_to_all | solution.py:149
  81.2 12.9 %all-to-all-start.1 = ((bf16[16,128,1024]{2,1,0:T(8,128)(2,1)}), bf16[16,128,1024]{2,1,0:T(8,128)(2,1)}, u32[]{:S(2)}, u32[]{:S(2)}) async-start(bf16[16,128,1024]{2,1,0:T(8,128)(2,1)} %copy.79), calls=%async_computation.1 | async-start | bytes 8388608 | tf_op jit(solution)/shard_map/all_to_all | solution.py:160
  96.7 4.3 copy.87
  101.0 60.3 %all-to-all-done.1 = bf16[16,128,1024]{2,1,0:T(8,128)(2,1)} async-done(((bf16[16,128,1024]{2,1,0:T(8,128)(2,1)}), bf16[16,128,1024]{2,1,0:T(8,128)(2,1)}, u32[]{:S(2)}, u32[]{:S(2)}) %all-to-all-start.1) | async-done | bytes 4194336 | tf_op jit(solution)/shard_map/all_to_all | solution.py:160
  161.3 11.3 %all-to-all-start.3 = ((bf16[16,128,1024]{2,1,0:T(8,128)(2,1)}), bf16[16,128,1024]{2,1,0:T(8,128)(2,1)}, u32[]{:S(2)}, u32[]{:S(2)}) async-start(bf16[16,128,1024]{2,1,0:T(8,128)(2,1)} %copy.87), calls=%async_computation.3 | async-start | bytes 8388608 | tf_op jit(solution)/shard_map/all_to_all | solution.py:163
  173.3 4.6 fusion.57
  177.9 3.0 copy.82
  180.9 50.9 %all-to-all-done.3 = bf16[16,128,1024]{2,1,0:T(8,128)(2,1)} async-done(((bf16[16,128,1024]{2,1,0:T(8,128)(2,1)}), bf16[16,128,1024]{2,1,0:T(8,128)(2,1)}, u32[]{:S(2)}, u32[]{:S(2)}) %all-to-all-start.3) | async-done | bytes 4194336 | tf_op jit(solution)/shard_map/all_to_all | solution.py:163
  231.7 4.6 fusion.60
  236.3 2.8 copy.90
  239.2 96.6 %while.34 = (s32[]{:T(128)}, bf16[8,128,1024]{1,2,0:T(8,128)(2,1)}, f32[8,1,8,128,1]{3,2,4,1,0:T(8,128)S(1)}, s32[8]{0:T(128)S(1)}, bf16[16384,128]{1,0:T(8,128)...) while((s32[]{:T(128)}, bf16[8,128,1024]{1,2,0:T(8,128)(2,1)}, ...), condition=%wide.region_7.8_spmd, body=%wide.region_4.7_spmd.sunk | while | flops 823329408 | bytes 22086448 | solution.py:73
  335.8 3.5 broadcast.264.clone2
  339.3 3.5 broadcast.264.clone
  342.8 187.9 %while.35 = (s32[]{:T(128)}, f32[16384,128]{1,0:T(8,128)}, f32[16384,128]{1,0:T(8,128)}, bf16[8,128,1024]{2,1,0:T(8,128)(2,1)}, s32[8]{0:T(128)S(1)}, /*index=5*...) while((s32[]{:T(128)}, f32[16384,128]{1,0:T(8,128)}, ...), condition=%wide.region_10.11_spmd, body=%wide.region_8.10_spmd.sunk | while | flops 2030961280 | bytes 53994384 | solution.py:126
  357.9 2.9 fusion.120
  381.4 2.9 fusion.120
  404.8 2.9 fusion.120
  428.3 2.9 fusion.120
  451.8 2.9 fusion.120
  475.3 2.9 fusion.120
  498.8 2.9 fusion.120
  522.3 2.9 fusion.120
  534.9 96.2 %reduce-scatter.3.cloned.1.call-done = f32[1024,128]{1,0:T(8,128)} async-done(((f32[16384,128]{1,0:T(8,128)}), f32[1024,128]{1,0:T(8,128)}) %reduce-scatter.3.cloned.1.call-update) | async-done | bytes 524304 | tf_op jit(solution)/shard_map/reduce_scatter | solution.py:178
  632.9 98.3 %reduce-scatter.5.cloned.1.call-done = f32[1024,128]{1,0:T(8,128)} async-done(((f32[16384,128]{1,0:T(8,128)}), f32[1024,128]{1,0:T(8,128)}) %reduce-scatter.5.cloned.1.call-update) | async-done | bytes 524304 | tf_op jit(solution)/shard_map/reduce_scatter | solution.py:179
  (337 shorter events, 254.7 us)
Async XLA Ops:
  7.2 232.0 %all-gather.5.cloned.1.call-start = ((), (), s32[]{:S(2)}) async-start(), calls=%async_computation.7 | async-start | bytes 4456448 | tf_op jit(solution)/shard_map/all_gather | solution.py:170
  13.7 34.7 %all-to-all-start = ((bf16[128,8,1024]{2,0,1:T(8,128)(2,1)}), bf16[128,8,1024]{2,0,1:T(8,128)(2,1)S(1)}, u32[]{:S(2)}, u32[]{:S(2)}) async-start(bf16[128,8,1024]{2,0,1:T(8,128)(2,1)} %copy.77), calls=%async_computation | async-start | bytes 4194304 | tf_op jit(solution)/shard_map/all_to_all | solution.py:142
  24.9 31.8 %copy-start.3 = (s32[128]{0:T(128)S(1)}, s32[128]{0:T(128)}, u32[]{:S(2)}) copy-start(s32[128]{0:T(128)} %param.15) | copy-start | bytes 1540
  48.4 1.3 copy-start.1
  49.7 31.5 %all-to-all-start.2 = ((bf16[128,8,1024]{2,0,1:T(8,128)(2,1)}), bf16[128,8,1024]{2,0,1:T(8,128)(2,1)S(1)}, u32[]{:S(2)}, u32[]{:S(2)}) async-start(bf16[128,8,1024]{2,0,1:T(8,128)(2,1)} %copy.85), calls=%async_computation.2 | async-start | bytes 4194304 | tf_op jit(solution)/shard_map/all_to_all | solution.py:149
  81.2 80.1 %all-to-all-start.1 = ((bf16[16,128,1024]{2,1,0:T(8,128)(2,1)}), bf16[16,128,1024]{2,1,0:T(8,128)(2,1)}, u32[]{:S(2)}, u32[]{:S(2)}) async-start(bf16[16,128,1024]{2,1,0:T(8,128)(2,1)} %copy.79), calls=%async_computation.1 | async-start | bytes 8388608 | tf_op jit(solution)/shard_map/all_to_all | solution.py:160
  94.1 145.1 %all-gather.3.cloned.1.call-start = ((), (), s32[]{:S(2)}) async-start(), calls=%async_computation.6 | async-start | bytes 4456448 | tf_op jit(solution)/shard_map/all_gather | solution.py:171
  161.3 70.4 %all-to-all-start.3 = ((bf16[16,128,1024]{2,1,0:T(8,128)(2,1)}), bf16[16,128,1024]{2,1,0:T(8,128)(2,1)}, u32[]{:S(2)}, u32[]{:S(2)}) async-start(bf16[16,128,1024]{2,1,0:T(8,128)(2,1)} %copy.87), calls=%async_computation.3 | async-start | bytes 8388608 | tf_op jit(solution)/shard_map/all_to_all | solution.py:163
  172.5 458.6 %reduce-scatter.3.cloned.1.call-start = ((), (), s32[]{:S(2)}) async-start(), calls=%async_computation.8 | async-start | bytes 8912896 | tf_op jit(solution)/shard_map/reduce_scatter | solution.py:178
  354.1 2.0 copy-start
  377.6 2.0 copy-start
  401.1 2.0 copy-start
  424.6 2.0 copy-start
  448.1 2.0 copy-start
  471.6 2.0 copy-start
  495.1 2.0 copy-start
  518.6 2.0 copy-start
  530.7 200.5 %reduce-scatter.5.cloned.1.call-start = ((), (), s32[]{:S(2)}) async-start(), calls=%async_computation.9 | async-start | bytes 8912896 | tf_op jit(solution)/shard_map/reduce_scatter | solution.py:179
  530.8 1.6 copy-start.2
Sparse Core Ops, SparseCore 0:
  9.7 67.6 all-gather.4
  96.6 75.1 all-gather.2
  530.8 100.2 reduce-scatter.2
  633.4 97.7 reduce-scatter.4
where the time goes:
time: 747 us; the launch traced here: 739 us
  waiting for transfers between devices  344 us (46%)
  local copies, waits for them, and re-layouts  156 us (21%)
  matrix products  127 us (17%)
  other arithmetic  38.6 us (5%)
  starting transfers between devices  38.5 us (5%)
  loops' own time  22.1 us (3%)
  between operations  13.9 us (2%)
    reduce_scatter x1, waiting for transfers between devices, on_device(): lax.psum_scatter(value_grad, 'ctx', scatter_dimension=0, tiled=True)  98.3 us
    reduce_scatter x1, waiting for transfers between devices, on_device(): lax.psum_scatter(key_grad, 'ctx', scatter_dimension=0, tiled=True)  96.2 us
    all_to_all x1, waiting for transfers between devices, on_device(): lax.all_to_all(select_rows(send_pick, query_blocks), 'ctx', split_axis=0,...  60.3 us
    all_to_all x1, waiting for transfers between devices, on_device(): lax.all_to_all(select_rows(send_pick, grad_blocks), 'ctx', split_axis=0,...  50.9 us
    dynamic_slice x40, local copies, waits for them, and re-layouts, attend_forward(): lax.scan(advance, jnp.zeros((), jnp.float32), (held_query, block_ids))  32.9 us
    dot_general x16, matrix products, masked_scores(): jnp.einsum('qkgd,wkd->kgqw', query_heads, key_window, preferred_element_t...  32.4 us
    dot_general x8, matrix products, advance(): jnp.einsum('qkgd,wkd->kgqw', grad_heads, value_window, preferred_element_...  23.4 us
    dot_general x8, matrix products, advance(): jnp.einsum('kgqw,wkd->qkgd', soft_low, value_window, preferred_element_ty...  20.9 us
  transfers between devices with their start and end apart: 8, of which 6 were waited for; matrix products, arithmetic and copies ran while one was open for 6% of the time, Pallas kernels for 0%

commit v1 on v0

v1 whole, which is shorter than its diff:
```python
import jax
import jax.numpy as jnp
from jax import lax
from jax.sharding import PartitionSpec as P

HEADS = 64
KV_HEADS = 8
HEAD_DIM = 128
BLOCK = 128
BAND = 12


def routing(block_owner, ctx_count, ctx_rank, blocks_here):
    owner_grid = block_owner.reshape(ctx_count, blocks_here)
    own_targets = lax.dynamic_index_in_dim(owner_grid, ctx_rank, 0, keepdims=False)
    targets = jnp.arange(ctx_count, dtype=jnp.int32)
    send_pick = (own_targets[None, :] == targets[:, None]).astype(jnp.bfloat16)
    arrivals = (owner_grid == ctx_rank).astype(jnp.int32)
    present = jnp.sum(arrivals, axis=1)
    arrival_rank = jnp.cumsum(present) - 1
    slot_index = jnp.arange(blocks_here, dtype=jnp.int32)
    chosen = (present[None, :] == 1) & (arrival_rank[None, :] == slot_index[:, None])
    source_block = targets * blocks_here + jnp.sum(arrivals * slot_index[None, :], axis=1)
    held_ids = jnp.sum(chosen.astype(jnp.int32) * source_block[None, :], axis=1)
    return (send_pick, chosen.astype(jnp.bfloat16), held_ids)


def select_rows(selector, blocks):
    picked = jnp.einsum("ab,brh->arh", selector, blocks, preferred_element_type=jnp.float32)
    return picked.astype(jnp.bfloat16)


def halo_docs(doc_ids, first_row, halo_rows):
    positions = first_row + jnp.arange(halo_rows, dtype=jnp.int32)
    picked = jnp.take(doc_ids, jnp.clip(positions, 0, doc_ids.shape[0] - 1), axis=0)
    return jnp.where(positions >= 0, picked, -1)


def masked_scores(query_block, key_window, query_doc, key_doc, local_block):
    window_rows = key_window.shape[0]
    kv_local = key_window.shape[1]
    query_heads = query_block.reshape(BLOCK, kv_local, HEADS // KV_HEADS, HEAD_DIM)
    raw_scores = jnp.einsum(
        "qkgd,wkd->kgqw", query_heads, key_window, preferred_element_type=jnp.float32
    ) * HEAD_DIM ** (-0.5)
    query_pos = (BAND - 1) * BLOCK + jnp.arange(BLOCK, dtype=jnp.int32)
    key_pos = jnp.arange(window_rows, dtype=jnp.int32)
    allowed = (query_doc[:, None] == key_doc[None, :]) & (key_pos[None, :] <= query_pos[:, None])
    return (jnp.where(allowed[None, None], raw_scores, -1e30), query_heads)


def window_of(halo_key, halo_value, halo_doc, local_block):
    window_rows = BAND * BLOCK
    kv_local = halo_key.shape[1] // HEAD_DIM
    start = local_block * BLOCK
    key_window = lax.dynamic_slice_in_dim(halo_key, start, window_rows, 0)
    value_window = lax.dynamic_slice_in_dim(halo_value, start, window_rows, 0)
    key_doc = lax.dynamic_slice_in_dim(halo_doc, start, window_rows, 0)
    query_doc = lax.dynamic_slice_in_dim(halo_doc, start + (BAND - 1) * BLOCK, BLOCK, 0)
    return (
        key_window.reshape(window_rows, kv_local, HEAD_DIM),
        value_window.reshape(window_rows, kv_local, HEAD_DIM),
        query_doc,
        key_doc,
    )


def attend_forward(query_blocks, halo_key, halo_value, halo_doc):

    def advance(running, inputs):
        query_block, local_block = inputs
        key_window, value_window, query_doc, key_doc = window_of(
            halo_key, halo_value, halo_doc, local_block
        )
        scores, _ = masked_scores(query_block, key_window, query_doc, key_doc, local_block)
        row_max = jnp.max(scores, axis=-1, keepdims=True)
        log_total = row_max + jnp.log(jnp.sum(jnp.exp(scores - row_max), axis=-1, keepdims=True))
        soft_low = jnp.exp(scores - log_total).astype(jnp.bfloat16)
        natural_out = jnp.einsum(
            "kgqw,wkd->qkgd", soft_low, value_window, preferred_element_type=jnp.float32
        )
        return (running, (natural_out.reshape(BLOCK, -1).astype(jnp.bfloat16), log_total))

    local_ids = jnp.arange(query_blocks.shape[0], dtype=jnp.int32)
    _, (out_blocks, log_totals) = lax.scan(
        advance, jnp.zeros((), jnp.float32), (query_blocks, local_ids)
    )
    return (out_blocks, log_totals)


def attend_backward(query_blocks, grad_blocks, out_blocks, log_totals, halo_key, halo_value, halo_doc):
    window_rows = BAND * BLOCK
    inv_root = HEAD_DIM ** (-0.5)

    def advance(running, inputs):
        key_grad, value_grad = running
        query_block, grad_block, out_block, log_total, local_block = inputs
        key_window, value_window, query_doc, key_doc = window_of(
            halo_key, halo_value, halo_doc, local_block
        )
        scores, query_heads = masked_scores(
            query_block, key_window, query_doc, key_doc, local_block
        )
        grad_heads = grad_block.reshape(query_heads.shape)
        out_heads = out_block.reshape(query_heads.shape)
        weights = jnp.exp(scores - log_total)
        soft_low = weights.astype(jnp.bfloat16)
        row_dot = jnp.sum(grad_heads.astype(jnp.float32) * out_heads.astype(jnp.float32), axis=-1)
        row_dot = jnp.transpose(row_dot, (1, 2, 0))[..., None]
        prob_grad = jnp.einsum(
            "qkgd,wkd->kgqw", grad_heads, value_window, preferred_element_type=jnp.float32
        )
        score_grad = (weights * (prob_grad - row_dot)).astype(jnp.bfloat16)
        query_part = (
            jnp.einsum("kgqw,wkd->qkgd", score_grad, key_window, preferred_element_type=jnp.float32)
            * inv_root
        )
        key_part = (
            jnp.einsum(
                "kgqw,qkgd->wkd", score_grad, query_heads, preferred_element_type=jnp.float32
            )
            * inv_root
        )
        value_part = jnp.einsum(
            "kgqw,qkgd->wkd", soft_low, grad_heads, preferred_element_type=jnp.float32
        )
        start = local_block * BLOCK
        old_keys = lax.dynamic_slice_in_dim(key_grad, start, window_rows, 0)
        old_values = lax.dynamic_slice_in_dim(value_grad, start, window_rows, 0)
        key_grad = lax.dynamic_update_slice_in_dim(
            key_grad, old_keys + key_part.reshape(window_rows, -1), start, 0
        )
        value_grad = lax.dynamic_update_slice_in_dim(
            value_grad, old_values + value_part.reshape(window_rows, -1), start, 0
        )
        return ((key_grad, value_grad), query_part.reshape(BLOCK, -1).astype(jnp.bfloat16))

    zero_grads = (
        jnp.zeros(halo_key.shape, jnp.float32),
        jnp.zeros(halo_value.shape, jnp.float32),
    )
    local_ids = jnp.arange(query_blocks.shape[0], dtype=jnp.int32)
    (key_grad, value_grad), dq_blocks = lax.scan(
        advance, zero_grads, (query_blocks, grad_blocks, out_blocks, log_totals, local_ids)
    )
    return (dq_blocks, key_grad, value_grad)


def shift_from_below(x, ctx_count, distance):
    pairs = [(s, s + distance) for s in range(ctx_count - distance)]
    return lax.ppermute(x, "ctx", pairs)


def shift_to_below(x, ctx_count, distance):
    pairs = [(s + distance, s) for s in range(ctx_count - distance)]
    return lax.ppermute(x, "ctx", pairs)


def on_device(queries, key_rows, value_rows, out_grad, doc_ids, block_owner):
    ctx_count = lax.axis_size("ctx")
    tp_count = lax.axis_size("tp")
    ctx_rank = lax.axis_index("ctx")
    local_rows, width = queries.shape
    head_cols = width // tp_count
    tok_dev = key_rows.shape[0]
    kv_cols = key_rows.shape[1]
    blocks_here = tok_dev // BLOCK
    reach = (BAND - 1) * BLOCK
    far = reach - tok_dev
    send_pick, recv_pick, _ = routing(block_owner, ctx_count, ctx_rank, blocks_here)
    query_split, grad_split = (
        lax.all_to_all(
            queries.reshape(local_rows, tp_count, head_cols),
            "tp",
            split_axis=1,
            concat_axis=0,
            tiled=True,
        ),
        lax.all_to_all(
            out_grad.reshape(local_rows, tp_count, head_cols),
            "tp",
            split_axis=1,
            concat_axis=0,
            tiled=True,
        ),
    )
    query_blocks = query_split.reshape(blocks_here, BLOCK, head_cols)
    grad_blocks = grad_split.reshape(blocks_here, BLOCK, head_cols)
    kv_here = jnp.concatenate([key_rows, value_rows], axis=1)
    kv_near = shift_from_below(kv_here, ctx_count, 1)
    kv_far = shift_from_below(kv_here[tok_dev - far :], ctx_count, 2)
    halo = jnp.concatenate([kv_far, kv_near, kv_here], axis=0)
    halo_key = halo[:, :kv_cols]
    halo_value = halo[:, kv_cols:]
    halo_doc = halo_docs(doc_ids, ctx_rank * tok_dev - reach, reach + tok_dev)
    out_blocks, log_totals = attend_forward(query_blocks, halo_key, halo_value, halo_doc)
    dq_blocks, key_grad, value_grad = attend_backward(
        query_blocks, grad_blocks, out_blocks, log_totals, halo_key, halo_value, halo_doc
    )
    kv_grad = jnp.concatenate([key_grad, value_grad], axis=1)
    grad_near = shift_to_below(kv_grad[far:reach], ctx_count, 1)
    grad_far = shift_to_below(kv_grad[:far], ctx_count, 2)
    kv_total = kv_grad[reach:] + grad_near
    kv_total = kv_total.at[tok_dev - far :].add(grad_far)
    sent_out, sent_dq = (
        lax.all_to_all(
            select_rows(send_pick, out_blocks), "ctx", split_axis=0, concat_axis=0, tiled=True
        ),
        lax.all_to_all(
            select_rows(send_pick, dq_blocks), "ctx", split_axis=0, concat_axis=0, tiled=True
        ),
    )
    held_out = select_rows(recv_pick, sent_out)
    held_dq = select_rows(recv_pick, sent_dq)
    return (
        held_out.reshape(tok_dev, head_cols),
        held_dq.reshape(tok_dev, head_cols),
        kv_total[:, :kv_cols].astype(jnp.bfloat16),
        kv_total[:, kv_cols:].astype(jnp.bfloat16),
    )


def solution(mesh):
    return jax.shard_map(
        on_device,
        mesh=mesh,
        in_specs=(
            P(("ctx", "tp"), None),
            P("ctx", "tp"),
            P("ctx", "tp"),
            P(("ctx", "tp"), None),
            P(),
            P(),
        ),
        out_specs=(P("ctx", "tp"), P("ctx", "tp"), P("ctx", "tp"), P("ctx", "tp")),
        check_vma=False,
    )
```

time: 747 us -> 643 us (0.86)
  waiting for transfers between devices: 344 us -> 130 us
  matrix products: 127 us -> 209 us
  local copies, waits for them, and re-layouts: 156 us -> 220 us
  between operations: 13.9 us -> 0.88 us
  loops' own time: 22.1 us -> 11.5 us
    reduce_scatter x2 -> x0, waiting for transfers between devices: 194 us -> none  [the longest x1 98.3 us: on_device(): lax.psum_scatter(value_grad, 'ctx', scatter_dimension=0, tiled=True)]
    ppermute x0 -> x4, waiting for transfers between devices: none -> 77.1 us  [the longest x2 67.8 us: shift_to_below(): return lax.ppermute(x, 'ctx', pairs)]
    all_to_all x2, waiting for transfers between devices: 111 us -> 49.8 us  [the longest x1 49.8 us: on_device(): lax.all_to_all(select_rows(send_pick, dq_blocks), 'ctx', split_axis=0, co...]
    dot_general x8, matrix products: 13.5 us -> 45.1 us  [advance(): jnp.einsum('kgqw,qkgd->wkd', soft_low, grad_heads, preferred_element_type...]
    dynamic_update_slice x16, local copies, waits for them, and re-layouts: 12.1 us -> 39.9 us  [advance(): lax.dynamic_update_slice_in_dim(value_grad, old_values + value_part.resha...]
    dot_general x16, matrix products: 32.4 us -> 53.3 us  [masked_scores(): jnp.einsum('qkgd,wkd->kgqw', query_heads, key_window, preferred_element_t...]
    dynamic_update_slice x8, local copies, waits for them, and re-layouts: 2.05 us -> 19.2 us  [advance(): lax.dynamic_update_slice_in_dim(key_grad, old_keys + key_part.reshape(win...]
    all_to_all x1, waiting for transfers between devices: 17 us -> 0.01 us  [on_device(): lax.all_to_all(out_grad.reshape(local_rows, tp_count, head_cols), 'tp', s...]
  transfers between devices with their start and end apart: 8 -> 8, of which waited for: 6 -> 6; matrix products, arithmetic and copies ran while one was open for 6% -> 17% of each run, Pallas kernels for 0% -> 0%
where the time goes in v1:
time: 643 us; the launch traced here: 638 us
  local copies, waits for them, and re-layouts  220 us (34%)
  matrix products  209 us (33%)
  waiting for transfers between devices  130 us (20%)
  starting transfers between devices  35 us (5%)
  other arithmetic  31.2 us (5%)
  loops' own time  11.5 us (2%)
    ppermute x2, waiting for transfers between devices, shift_to_below(): return lax.ppermute(x, 'ctx', pairs)  67.8 us
    dot_general x16, matrix products, masked_scores(): jnp.einsum('qkgd,wkd->kgqw', query_heads, key_window, preferred_element_t...  53.3 us
    all_to_all x1, waiting for transfers between devices, on_device(): lax.all_to_all(select_rows(send_pick, dq_blocks), 'ctx', split_axis=0, co...  49.8 us
    dot_general x8, matrix products, advance(): jnp.einsum('kgqw,qkgd->wkd', soft_low, grad_heads, preferred_element_type...  45.1 us
    dynamic_update_slice x16, local copies, waits for them, and re-layouts, advance(): lax.dynamic_update_slice_in_dim(value_grad, old_values + value_part.resha...  39.9 us
    dot_general x8, matrix products, advance(): jnp.einsum('qkgd,wkd->kgqw', grad_heads, value_window, preferred_element_...  38.9 us
    dynamic_slice x16, local copies, waits for them, and re-layouts, advance(): old_values = lax.dynamic_slice_in_dim(value_grad, start, window_rows, 0)  35.2 us
    dynamic_slice x40, local copies, waits for them, and re-layouts, attend_forward(): lax.scan(advance, jnp.zeros((), jnp.float32), (query_blocks, local_ids))  32.6 us
  transfers between devices with their start and end apart: 8, of which 6 were waited for; matrix products, arithmetic and copies ran while one was open for 17% of the time, Pallas kernels for 0%

profile of v1, /device:TPU:60, one launch (start us, length us, event | category | flops | bytes accessed | tf_op | source)
XLA Modules:
  0.0 637.8 jit_solution(14774243730302712836)
XLA Ops:
  4.8 7.4 %all-to-all-start = ((bf16[128,8,1024]{0,2,1:T(8,128)(2,1)}), bf16[128,8,1024]{0,2,1:T(8,128)(2,1)}, u32[]{:S(2)}, u32[]{:S(2)}) async-start(bf16[128,8,1024]{0,2,1:T(8,128)(2,1)} %bitcast.43), calls=%async_computation | async-start | bytes 4194304 | tf_op jit(solution)/shard_map/all_to_all | solution.py:172
  21.1 13.0 %gather_fusion = s32[2432]{0:T(1024)S(1)} fusion(s32[16384]{0:T(1024)S(1)} %copy-done, s32[3072]{0:T(1024)S(1)} %pad_clamp_fusion), kind=kCustom, calls=%fused_computation | custom fusion | bytes 29184 | tf_op jit(solution)/shard_map/jit(_take)/gather | solution.py:35
  34.1 5.8 collective-permute-done
  47.8 4.8 all-to-all-start.2
  54.2 74.8 %while.31 = (s32[]{:T(128)}, bf16[8,128,1024]{1,2,0:T(8,128)(2,1)}, f32[8,1,8,128,1]{3,2,4,1,0:T(8,128)S(1)}, s32[8]{0:T(128)S(1)}, bf16[2432,128]{1,0:T(8,128)(...) while((s32[]{:T(128)}, bf16[8,128,1024]{1,2,0:T(8,128)(2,1)}, ...), condition=%wide.region_5.6_spmd, body=%wide.region_2.5_spmd.sunk | while | flops 823327872 | bytes 22074628 | solution.py:85
  132.9 330.2 %while.32 = (s32[]{:T(128)}, f32[2432,128]{1,0:T(8,128)}, f32[2432,128]{1,0:T(8,128)}, bf16[8,128,1024]{1,2,0:T(8,128)(2,1)}, s32[8]{0:T(128)S(1)}, /*index=5*/b...) while((s32[]{:T(128)}, f32[2432,128]{1,0:T(8,128)}, ...), condition=%wide.region_8.9_spmd, body=%wide.region_6.8_spmd.sunk | while | flops 2030959744 | bytes 57390492 | solution.py:143
  136.3 4.6 fusion.129
  143.1 4.9 fusion.132
  161.2 5.6 fusion.131
  184.3 4.9 fusion.132
  202.5 5.6 fusion.131
  225.6 4.9 fusion.132
  243.7 5.6 fusion.131
  260.1 4.6 fusion.129
  266.9 4.9 fusion.132
  285.1 5.6 fusion.131
  301.3 4.7 fusion.129
  308.1 4.9 fusion.132
  326.3 5.6 fusion.131
  349.4 4.9 fusion.132
  367.6 5.6 fusion.131
  383.9 4.6 fusion.129
  390.7 4.9 fusion.132
  408.9 5.6 fusion.131
  425.2 4.7 fusion.129
  432.0 4.9 fusion.132
  450.2 5.6 fusion.131
  472.5 5.8 all-to-all-start.3
  487.7 49.8 %all-to-all-done.3 = bf16[16,128,1024]{2,1,0:T(8,128)(2,1)} async-done(((bf16[16,128,1024]{2,1,0:T(8,128)(2,1)}), bf16[16,128,1024]{2,1,0:T(8,128)(2,1)}, u32[]{:S(2)}, u32[]{:S(2)}) %all-to-all-start.3) | async-done | bytes 4194336 | tf_op jit(solution)/shard_map/all_to_all | solution.py:209
  537.5 5.7 all-to-all-start.1
  553.4 51.0 %collective-permute-done.2 = f32[1024,256]{1,0:T(8,128)S(1)} collective-permute-done((f32[1024,256]{1,0:T(8,128)S(1)}, f32[1024,256]{1,0:T(8,128)S(1)}, u32[]{:S(2)}, u32[]{:S(2)}) %collective-permute-start.2) | collective-permute-done | bytes 1048608 | tf_op jit(solution)/shard_map/ppermute | solution.py:156
  605.7 16.9 %collective-permute-done.3 = f32[384,256]{1,0:T(8,128)S(1)} collective-permute-done((f32[384,256]{1,0:T(8,128)S(1)}, f32[384,256]{1,0:T(8,128)S(1)}, u32[]{:S(2)}, u32[]{:S(2)}) %collective-permute-start.3) | collective-permute-done | bytes 393248 | tf_op jit(solution)/shard_map/ppermute | solution.py:156
  (367 shorter events, 358.0 us)
Async XLA Ops:
  0.6 20.4 %copy-start = (s32[16384]{0:T(1024)S(1)}, s32[16384]{0:T(1024)}, u32[]{:S(2)}) copy-start(s32[16384]{0:T(1024)} %param.16) | copy-start | bytes 196612
  4.7 7.4 %copy-start.9 = (bf16[1024,128]{1,0:T(8,128)(2,1)S(1)}, bf16[1024,128]{1,0:T(8,128)(2,1)}, u32[]{:S(2)}) copy-start(bf16[1024,128]{1,0:T(8,128)(2,1)} %param.13) | copy-start | bytes 786436
  4.8 7.4 %copy-start.10 = (bf16[1024,128]{1,0:T(8,128)(2,1)S(1)}, bf16[1024,128]{1,0:T(8,128)(2,1)}, u32[]{:S(2)}) copy-start(bf16[1024,128]{1,0:T(8,128)(2,1)} %param.14) | copy-start | bytes 786436
  4.8 13.7 %copy-start.8 = (bf16[128,8192]{1,0:T(8,128)(2,1)S(1)}, bf16[128,8192]{1,0:T(8,128)(2,1)}, u32[]{:S(2)}) copy-start(bf16[128,8192]{1,0:T(8,128)(2,1)} %param.15) | copy-start | bytes 6291460
  4.8 43.1 %all-to-all-start = ((bf16[128,8,1024]{0,2,1:T(8,128)(2,1)}), bf16[128,8,1024]{0,2,1:T(8,128)(2,1)}, u32[]{:S(2)}, u32[]{:S(2)}) async-start(bf16[128,8,1024]{0,2,1:T(8,128)(2,1)} %bitcast.43), calls=%async_computation | async-start | bytes 4194304 | tf_op jit(solution)/shard_map/all_to_all | solution.py:172
  12.2 8.7 %copy-start.11 = (s32[128]{0:T(128)S(1)}, s32[128]{0:T(128)}, u32[]{:S(2)}) copy-start(s32[128]{0:T(128)} %param.17) | copy-start | bytes 1540
  12.3 31.1 %collective-permute-start.1 = (bf16[1024,256]{1,0:T(8,128)(2,1)S(1)}, bf16[1024,256]{1,0:T(8,128)(2,1)S(1)}, u32[]{:S(2)}, u32[]{:S(2)}) collective-permute-start(bf16[1024,256]{1,0:T(8,128)(2,1)S(1)} %constant_dynamic-update-slice_fusion.4), channel_id=1, source_target_pairs={{0,8},{8,16},{16,24},{24,32},{32,40},{40,48},{48,56},{56,64},{64,7... | collective-permute-start | bytes 1572872 | tf_op jit(solution)/shard_map/ppermute | solution.py:151
  14.9 25.1 %collective-permute-start = (bf16[384,256]{1,0:T(8,128)(2,1)}, bf16[384,256]{1,0:T(8,128)(2,1)S(1)}, u32[]{:S(2)}, u32[]{:S(2)}) collective-permute-start(bf16[384,256]{1,0:T(8,128)(2,1)} %slice.56), channel_id=1, source_target_pairs={{0,16},{8,24},{16,32},{24,40},{32,48},{40,56},{48,64},{56,72},{64,... | collective-permute-start | bytes 589832 | tf_op jit(solution)/shard_map/ppermute | solution.py:151
  47.8 81.2 %all-to-all-start.2 = ((bf16[128,8,1024]{0,2,1:T(8,128)(2,1)}), bf16[128,8,1024]{0,2,1:T(8,128)(2,1)}, u32[]{:S(2)}, u32[]{:S(2)}) async-start(bf16[128,8,1024]{0,2,1:T(8,128)(2,1)} %bitcast.50), calls=%async_computation.2 | async-start | bytes 4194304 | tf_op jit(solution)/shard_map/all_to_all | solution.py:179
  143.0 4.9 copy-start.5
  154.4 6.8 %copy-start.6 = (bf16[1,128,1024]{1,2,0:T(8,128)(2,1)S(1)}, bf16[1,128,1024]{1,2,0:T(8,128)(2,1)}, u32[]{:S(2)}) copy-start(bf16[1,128,1024]{1,2,0:T(8,128)(2,1)} %copy-done.5) | copy-start | bytes 786436 | tf_op jit(solution)/shard_map/while
  184.3 4.9 copy-start.5
  195.7 6.8 %copy-start.6 = (bf16[1,128,1024]{1,2,0:T(8,128)(2,1)S(1)}, bf16[1,128,1024]{1,2,0:T(8,128)(2,1)}, u32[]{:S(2)}) copy-start(bf16[1,128,1024]{1,2,0:T(8,128)(2,1)} %copy-done.5) | copy-start | bytes 786436 | tf_op jit(solution)/shard_map/while
  225.5 4.9 copy-start.5
  236.9 6.8 %copy-start.6 = (bf16[1,128,1024]{1,2,0:T(8,128)(2,1)S(1)}, bf16[1,128,1024]{1,2,0:T(8,128)(2,1)}, u32[]{:S(2)}) copy-start(bf16[1,128,1024]{1,2,0:T(8,128)(2,1)} %copy-done.5) | copy-start | bytes 786436 | tf_op jit(solution)/shard_map/while
  266.8 4.9 copy-start.5
  266.8 4.9 copy-start.2
  278.2 6.8 %copy-start.6 = (bf16[1,128,1024]{1,2,0:T(8,128)(2,1)S(1)}, bf16[1,128,1024]{1,2,0:T(8,128)(2,1)}, u32[]{:S(2)}) copy-start(bf16[1,128,1024]{1,2,0:T(8,128)(2,1)} %copy-done.5) | copy-start | bytes 786436 | tf_op jit(solution)/shard_map/while
  308.1 4.9 copy-start.5
  319.5 6.8 %copy-start.6 = (bf16[1,128,1024]{1,2,0:T(8,128)(2,1)S(1)}, bf16[1,128,1024]{1,2,0:T(8,128)(2,1)}, u32[]{:S(2)}) copy-start(bf16[1,128,1024]{1,2,0:T(8,128)(2,1)} %copy-done.5) | copy-start | bytes 786436 | tf_op jit(solution)/shard_map/while
  349.4 4.9 copy-start.5
  360.8 6.8 %copy-start.6 = (bf16[1,128,1024]{1,2,0:T(8,128)(2,1)S(1)}, bf16[1,128,1024]{1,2,0:T(8,128)(2,1)}, u32[]{:S(2)}) copy-start(bf16[1,128,1024]{1,2,0:T(8,128)(2,1)} %copy-done.5) | copy-start | bytes 786436 | tf_op jit(solution)/shard_map/while
  390.7 4.9 copy-start.5
  402.1 6.8 %copy-start.6 = (bf16[1,128,1024]{1,2,0:T(8,128)(2,1)S(1)}, bf16[1,128,1024]{1,2,0:T(8,128)(2,1)}, u32[]{:S(2)}) copy-start(bf16[1,128,1024]{1,2,0:T(8,128)(2,1)} %copy-done.5) | copy-start | bytes 786436 | tf_op jit(solution)/shard_map/while
  432.0 4.9 copy-start.5
  443.4 6.8 %copy-start.6 = (bf16[1,128,1024]{1,2,0:T(8,128)(2,1)S(1)}, bf16[1,128,1024]{1,2,0:T(8,128)(2,1)}, u32[]{:S(2)}) copy-start(bf16[1,128,1024]{1,2,0:T(8,128)(2,1)} %copy-done.5) | copy-start | bytes 786436 | tf_op jit(solution)/shard_map/while
  472.5 65.0 %all-to-all-start.3 = ((bf16[16,128,1024]{2,1,0:T(8,128)(2,1)}), bf16[16,128,1024]{2,1,0:T(8,128)(2,1)}, u32[]{:S(2)}, u32[]{:S(2)}) async-start(bf16[16,128,1024]{2,1,0:T(8,128)(2,1)} %copy.55), calls=%async_computation.3 | async-start | bytes 8388608 | tf_op jit(solution)/shard_map/all_to_all | solution.py:209
  487.7 55.5 %copy-start.3 = (f32[2432,128]{1,0:T(8,128)S(1)}, f32[2432,128]{1,0:T(8,128)}, u32[]{:S(2)}) copy-start(f32[2432,128]{1,0:T(8,128)} %get-tuple-element.272) | copy-start | bytes 3735556
  537.5 93.1 %all-to-all-start.1 = ((bf16[16,128,1024]{2,1,0:T(8,128)(2,1)}), bf16[16,128,1024]{2,1,0:T(8,128)(2,1)}, u32[]{:S(2)}, u32[]{:S(2)}) async-start(bf16[16,128,1024]{2,1,0:T(8,128)(2,1)} %copy.50), calls=%async_computation.1 | async-start | bytes 8388608 | tf_op jit(solution)/shard_map/all_to_all | solution.py:206
  546.2 58.2 %collective-permute-start.2 = (f32[1024,256]{1,0:T(8,128)S(1)}, f32[1024,256]{1,0:T(8,128)S(1)}, u32[]{:S(2)}, u32[]{:S(2)}) collective-permute-start(f32[1024,256]{1,0:T(8,128)S(1)} %slice.60), channel_id=1, source_target_pairs={{8,0},{16,8},{24,16},{32,24},{40,32},{48,40},{56,48},{64,56},{72,6... | collective-permute-start | bytes 3145736 | tf_op jit(solution)/shard_map/ppermute | solution.py:156
  549.7 72.9 %collective-permute-start.3 = (f32[384,256]{1,0:T(8,128)S(1)}, f32[384,256]{1,0:T(8,128)S(1)}, u32[]{:S(2)}, u32[]{:S(2)}) collective-permute-start(f32[384,256]{1,0:T(8,128)S(1)} %slice.62), channel_id=1, source_target_pairs={{16,0},{24,8},{32,16},{40,24},{48,32},{56,40},{64,48},{72,56},{80,... | collective-permute-start | bytes 1179656 | tf_op jit(solution)/shard_map/ppermute | solution.py:156
  630.6 7.1 %copy-start.1 = (s32[16384]{0:T(1024)S(1)}, s32[16384]{0:T(1024)}, u32[]{:S(2)}) copy-start(s32[16384]{0:T(1024)} %param.16) | copy-start | bytes 196612
  (9 other events, 37.0 us)

commit v2 on v1

--- a/solution.py
+++ b/solution.py
@@ -2,6 +2,8 @@
 import jax.numpy as jnp
 from jax import lax
 from jax.sharding import PartitionSpec as P
+from jax.experimental import pallas as pl
+from jax.experimental.pallas import tpu as pltpu
 
 HEADS = 64
 KV_HEADS = 8
@@ -144,6 +146,82 @@
         advance, zero_grads, (query_blocks, grad_blocks, out_blocks, log_totals, local_ids)
     )
     return (dq_blocks, key_grad, value_grad)
+
+
+TRANS_B = (((1,), (1,)), ((), ()))
+TRANS_A = (((0,), (0,)), ((), ()))
+
+
+def fused_kernel(qdoc_ref, kdoc_ref, q_ref, do_ref, k_ref, v_ref, out_ref, dq_ref, dk_ref, dv_ref):
+    block = pl.program_id(0)
+    head = pl.program_id(1)
+    window_rows = BAND * BLOCK
+    scale = HEAD_DIM ** (-0.5)
+
+    @pl.when((block == 0) & (head == 0))
+    def _():
+        dk_ref[...] = jnp.zeros_like(dk_ref)
+        dv_ref[...] = jnp.zeros_like(dv_ref)
+
+    start = pl.multiple_of(block * BLOCK, BLOCK)
+    key_window = k_ref[pl.ds(start, window_rows), :]
+    value_window = v_ref[pl.ds(start, window_rows), :]
+    query = q_ref[0]
+    raw = lax.dot_general(query, key_window, TRANS_B, preferred_element_type=jnp.float32) * scale
+    rows = lax.broadcasted_iota(jnp.int32, raw.shape, 0) + (BAND - 1) * BLOCK
+    cols = lax.broadcasted_iota(jnp.int32, raw.shape, 1)
+    allowed = (qdoc_ref[0] == kdoc_ref[0]) & (cols <= rows)
+    scores = jnp.where(allowed, raw, -1e30)
+    row_max = jnp.max(scores, axis=1, keepdims=True)
+    log_total = row_max + jnp.log(jnp.sum(jnp.exp(scores - row_max), axis=1, keepdims=True))
+    weights = jnp.exp(scores - log_total)
+    soft_low = weights.astype(jnp.bfloat16)
+    out = jnp.dot(soft_low, value_window, preferred_element_type=jnp.float32).astype(jnp.bfloat16)
+    out_ref[0] = out
+    grad = do_ref[0]
+    row_dot = jnp.sum(grad.astype(jnp.float32) * out.astype(jnp.float32), axis=1, keepdims=True)
+    prob_grad = lax.dot_general(grad, value_window, TRANS_B, preferred_element_type=jnp.float32)
+    score_grad = (weights * (prob_grad - row_dot)).astype(jnp.bfloat16)
+    dq = jnp.dot(score_grad, key_window, preferred_element_type=jnp.float32) * scale
+    dq_ref[0] = dq.astype(jnp.bfloat16)
+    dk = lax.dot_general(score_grad, query, TRANS_A, preferred_element_type=jnp.float32) * scale
+    dv = lax.dot_general(soft_low, grad, TRANS_A, preferred_element_type=jnp.float32)
+    dk_ref[pl.ds(start, window_rows), :] += dk
+    dv_ref[pl.ds(start, window_rows), :] += dv
+
+
+def fused_attention(query_blocks, grad_blocks, halo_key, halo_value, halo_doc):
+    blocks, _, width = query_blocks.shape
+    heads_here = width // HEAD_DIM
+    window_rows = BAND * BLOCK
+    reach = (BAND - 1) * BLOCK
+    halo_rows = halo_key.shape[0]
+    query_doc = halo_doc[reach:].reshape(blocks, BLOCK, 1)
+    key_doc = jnp.stack(
+        [halo_doc[b * BLOCK : b * BLOCK + window_rows] for b in range(blocks)]
+    ).reshape(blocks, 1, window_rows)
+    head_spec = pl.BlockSpec((1, BLOCK, HEAD_DIM), lambda b, h: (b, 0, h))
+    whole = pl.BlockSpec((halo_rows, HEAD_DIM), lambda b, h: (0, 0))
+    return pl.pallas_call(
+        fused_kernel,
+        grid=(blocks, heads_here),
+        in_specs=[
+            pl.BlockSpec((1, BLOCK, 1), lambda b, h: (b, 0, 0)),
+            pl.BlockSpec((1, 1, window_rows), lambda b, h: (b, 0, 0)),
+            head_spec,
+            head_spec,
+            whole,
+            whole,
+        ],
+        out_specs=[head_spec, head_spec, whole, whole],
+        out_shape=[
+            jax.ShapeDtypeStruct(query_blocks.shape, jnp.bfloat16),
+            jax.ShapeDtypeStruct(query_blocks.shape, jnp.bfloat16),
+            jax.ShapeDtypeStruct((halo_rows, HEAD_DIM), jnp.float32),
+            jax.ShapeDtypeStruct((halo_rows, HEAD_DIM), jnp.float32),
+        ],
+        compiler_params=pltpu.CompilerParams(dimension_semantics=("arbitrary", "arbitrary")),
+    )(query_doc, key_doc, query_blocks, grad_blocks, halo_key, halo_value)
 
 
 def shift_from_below(x, ctx_count, distance):
@@ -193,9 +271,8 @@
     halo_key = halo[:, :kv_cols]
     halo_value = halo[:, kv_cols:]
     halo_doc = halo_docs(doc_ids, ctx_rank * tok_dev - reach, reach + tok_dev)
-    out_blocks, log_totals = attend_forward(query_blocks, halo_key, halo_value, halo_doc)
-    dq_blocks, key_grad, value_grad = attend_backward(
-        query_blocks, grad_blocks, out_blocks, log_totals, halo_key, halo_value, halo_doc
+    out_blocks, dq_blocks, key_grad, value_grad = fused_attention(
+        query_blocks, grad_blocks, halo_key, halo_value, halo_doc
     )
     kv_grad = jnp.concatenate([key_grad, value_grad], axis=1)
     grad_near = shift_to_below(kv_grad[far:reach], ctx_count, 1)

time: 643 us -> 346 us (0.54)
  matrix products: 209 us -> 14.2 us
  local copies, waits for them, and re-layouts: 220 us -> 48.6 us
  Pallas kernels: 0 us -> 88.7 us
  other arithmetic: 31.2 us -> 3.2 us
  waiting for transfers between devices: 130 us -> 155 us
  loops' own time: 11.5 us -> 0 us
    dot_general x56 -> x0, matrix products: 197 us -> none  [the longest x16 53.3 us: masked_scores(): jnp.einsum('qkgd,wkd->kgqw', query_heads, key_window, preferred_element_t...]
    dynamic_slice x104 -> x0, local copies, waits for them, and re-layouts: 96.8 us -> none  [the longest x16 35.2 us: advance(): old_values = lax.dynamic_slice_in_dim(value_grad, start, window_rows, 0)]
    pallas_call x0 -> x1, Pallas kernels: none -> 88.7 us  [fused_attention(): pl.pallas_call(fused_kernel, grid=(blocks, heads_here), in_specs=[pl.Bloc...]
    dynamic_update_slice x40 -> x0, local copies, waits for them, and re-layouts: 70.7 us -> none  [the longest x16 39.9 us: advance(): lax.dynamic_update_slice_in_dim(value_grad, old_values + value_part.resha...]
    all_to_all x1, waiting for transfers between devices: 3.25 us -> 24.9 us  [on_device(): lax.all_to_all(queries.reshape(local_rows, tp_count, head_cols), 'tp', sp...]
    another operation x2 -> x0, loops' own time: 11.5 us -> none  [the longest x1 5.92 us: attend_backward(): lax.scan(advance, zero_grads, (query_blocks, grad_blocks, out_blocks, log...]
    reduce_sum x16 -> x0, other arithmetic: 10.7 us -> none  [the longest x8 10.4 us: advance(): jnp.sum(jnp.exp(scores - row_max), axis=-1, keepdims=True)]
    and x16 -> x0, other arithmetic: 9.78 us -> none  [masked_scores(): (query_doc[:, None] == key_doc[None, :]) & (key_pos[None, :] <= query_pos...]
  transfers between devices with their start and end apart: 8 -> 8, of which waited for: 6 -> 5; matrix products, arithmetic and copies ran while one was open for 17% -> 13% of each run, Pallas kernels for 0% -> 0%
where the time goes in v2:
time: 346 us
  waiting for transfers between devices  155 us (45%)
  Pallas kernels  88.7 us (26%)
  local copies, waits for them, and re-layouts  48.6 us (14%)
  starting transfers between devices  34.6 us (10%)
  matrix products  14.2 us (4%)
    pallas_call x1, Pallas kernels, fused_attention(): pl.pallas_call(fused_kernel, grid=(blocks, heads_here), in_specs=[pl.Bloc...  88.7 us
    ppermute x2, waiting for transfers between devices, shift_to_below(): return lax.ppermute(x, 'ctx', pairs)  69.2 us
    all_to_all x1, waiting for transfers between devices, on_device(): lax.all_to_all(select_rows(send_pick, dq_blocks), 'ctx', split_axis=0, co...  53.1 us
    all_to_all x1, waiting for transfers between devices, on_device(): lax.all_to_all(queries.reshape(local_rows, tp_count, head_cols), 'tp', sp...  24.9 us
    dot_general x4, matrix products, select_rows(): jnp.einsum('ab,brh->arh', selector, blocks, preferred_element_type=jnp.fl...  14.2 us
    convert_element_type x4, local copies, waits for them, and re-layouts, select_rows(): return picked.astype(jnp.bfloat16)  13.6 us
    gather x1, local copies, waits for them, and re-layouts, halo_docs(): jnp.take(doc_ids, jnp.clip(positions, 0, doc_ids.shape[0] - 1), axis=0)  13 us
    unnamed x21, local copies, waits for them, and re-layouts  10.6 us
  transfers between devices with their start and end apart: 8, of which 5 were waited for; matrix products, arithmetic and copies ran while one was open for 13% of the time, Pallas kernels for 0%

profile of v2, /device:TPU:60, one launch (start us, length us, event | category | flops | bytes accessed | tf_op | source)
XLA Modules:
  0.0 345.6 jit_solution(298603599931894140)
XLA Ops:
  0.6 3.3 copy.23
  3.9 2.6 copy.24
  6.5 7.2 %all-to-all-start.1 = ((bf16[128,8,1024]{2,0,1:T(8,128)(2,1)}), bf16[128,8,1024]{2,0,1:T(8,128)(2,1)S(1)}, u32[]{:S(2)}, u32[]{:S(2)}) async-start(bf16[128,8,1024]{2,0,1:T(8,128)(2,1)} %copy.24), calls=%async_computation.1 | async-start | bytes 4194304 | tf_op jit(solution)/shard_map/all_to_all | solution.py:257
  13.9 1.9 collective-permute-start.1
  16.5 3.5 %collective-permute-start = (bf16[384,256]{1,0:T(8,128)(2,1)}, bf16[384,256]{1,0:T(8,128)(2,1)S(1)}, u32[]{:S(2)}, u32[]{:S(2)}) collective-permute-start(bf16[384,256]{1,0:T(8,128)(2,1)} %slice.104), channel_id=1, source_target_pairs={{0,16},{8,24},{16,32},{24,40},{32,48},{40,56},{48,64},{56,72},{64,... | collective-permute-start | bytes 589832 | tf_op jit(solution)/shard_map/ppermute | solution.py:229
  20.1 4.1 %copy.21 = bf16[128,8192]{0,1:T(8,128)(2,1)} copy(bf16[128,8192]{1,0:T(8,128)(2,1)} %param.8) | data formatting | bytes 4194304 | tf_op args[0]
  24.2 3.9 %copy.22 = bf16[128,8,1024]{2,0,1:T(8,128)(2,1)} copy(bf16[128,8,1024]{0,2,1:T(8,128)(2,1)} %bitcast.28) | data formatting | bytes 4194304 | tf_op jit(solution)/shard_map/reshape | solution.py:251
  28.1 13.0 %gather_fusion = s32[2432]{0:T(1024)S(1)} fusion(s32[16384]{0:T(1024)S(1)} %copy-done, s32[3072]{0:T(1024)S(1)} %pad_clamp_fusion), kind=kCustom, calls=%fused_computation | custom fusion | bytes 29184 | tf_op jit(solution)/shard_map/jit(_take)/gather | solution.py:37
  41.2 8.2 %all-to-all-done.1 = bf16[128,8,1024]{2,0,1:T(8,128)(2,1)S(1)} async-done(((bf16[128,8,1024]{2,0,1:T(8,128)(2,1)}), bf16[128,8,1024]{2,0,1:T(8,128)(2,1)S(1)}, u32[]{:S(2)}, u32[]{:S(2)}) %all-to-all-start.1) | async-done | bytes 2097184 | tf_op jit(solution)/shard_map/all_to_all | solution.py:257
  49.4 1.3 copy-done.2
  50.7 4.8 %all-to-all-start = ((bf16[128,8,1024]{2,0,1:T(8,128)(2,1)}), bf16[128,8,1024]{2,0,1:T(8,128)(2,1)}, u32[]{:S(2)}, u32[]{:S(2)}) async-start(bf16[128,8,1024]{2,0,1:T(8,128)(2,1)} %copy.22), calls=%async_computation | async-start | bytes 4194304 | tf_op jit(solution)/shard_map/all_to_all | solution.py:250
  58.1 1.1 fusion.31
  59.2 24.9 %all-to-all-done = bf16[128,8,1024]{2,0,1:T(8,128)(2,1)} async-done(((bf16[128,8,1024]{2,0,1:T(8,128)(2,1)}), bf16[128,8,1024]{2,0,1:T(8,128)(2,1)}, u32[]{:S(2)}, u32[]{:S(2)}) %all-to-all-start) | async-done | bytes 2097184 | tf_op jit(solution)/shard_map/all_to_all | solution.py:250
  84.1 88.7 %shard_map.93 = (bf16[8,128,1024]{2,1,0:T(8,128)(2,1)}, bf16[8,128,1024]{2,1,0:T(8,128)(2,1)}, f32[2432,128]{1,0:T(8,128)}, f32[2432,128]{1,0:T(8,128)}) custom-call(s32[8,128,1]{2,1,0:T(8,128)} %select_select_fusion.qdoc_ref, s32[8,1,1536]{2,1,0:T(1,128)} %reshape.173.kdoc_ref, bf16[8,128,1024]{2,1,0:T(8,128)(2,1)} %bitcast.8.q_ref, ...), custom_call_target="tpu_custom_call" | custom-call | tf_op jit(solution)/shard_map/pallas_call | solution.py:205
  172.8 3.2 convolution_convert_fusion
  176.0 4.3 %copy.30 = bf16[16,128,1024]{2,1,0:T(8,128)(2,1)} copy(bf16[16,128,1024]{2,0,1:T(8,128)(2,1)S(1)} %convolution_convert_fusion) | data formatting | bytes 8388608 | tf_op jit(solution)/shard_map/convert_element_type | solution.py:32
  180.3 5.9 %all-to-all-start.3 = ((bf16[16,128,1024]{2,1,0:T(8,128)(2,1)}), bf16[16,128,1024]{2,1,0:T(8,128)(2,1)}, u32[]{:S(2)}, u32[]{:S(2)}) async-start(bf16[16,128,1024]{2,1,0:T(8,128)(2,1)} %copy.30), calls=%async_computation.3 | async-start | bytes 8388608 | tf_op jit(solution)/shard_map/all_to_all | solution.py:286
  186.2 1.8 convolution_convert_fusion.1
  188.0 4.3 %copy.26 = bf16[16,128,1024]{2,1,0:T(8,128)(2,1)} copy(bf16[16,128,1024]{2,0,1:T(8,128)(2,1)S(1)} %convolution_convert_fusion.1) | data formatting | bytes 8388608 | tf_op jit(solution)/shard_map/convert_element_type | solution.py:32
  192.3 53.1 %all-to-all-done.3 = bf16[16,128,1024]{2,1,0:T(8,128)(2,1)} async-done(((bf16[16,128,1024]{2,1,0:T(8,128)(2,1)}), bf16[16,128,1024]{2,1,0:T(8,128)(2,1)}, u32[]{:S(2)}, u32[]{:S(2)}) %all-to-all-start.3) | async-done | bytes 4194336 | tf_op jit(solution)/shard_map/all_to_all | solution.py:286
  245.3 5.7 %all-to-all-start.2 = ((bf16[16,128,1024]{2,1,0:T(8,128)(2,1)}), bf16[16,128,1024]{2,1,0:T(8,128)(2,1)}, u32[]{:S(2)}, u32[]{:S(2)}) async-start(bf16[16,128,1024]{2,1,0:T(8,128)(2,1)} %copy.26), calls=%async_computation.2 | async-start | bytes 8388608 | tf_op jit(solution)/shard_map/all_to_all | solution.py:283
  251.1 1.5 constant_dynamic-update-slice_fusion.3
  252.8 1.0 slice.108
  253.9 2.2 collective-permute-start.2
  256.3 3.4 collective-permute-start.3
  259.8 52.4 %collective-permute-done.2 = f32[1024,256]{1,0:T(8,128)} collective-permute-done((f32[1024,256]{1,0:T(8,128)}, f32[1024,256]{1,0:T(8,128)}, u32[]{:S(2)}, u32[]{:S(2)}) %collective-permute-start.2) | collective-permute-done | bytes 1048608 | tf_op jit(solution)/shard_map/ppermute | solution.py:234
  312.3 1.4 slice_add_fusion
  313.6 16.7 %collective-permute-done.3 = f32[384,256]{1,0:T(8,128)S(1)} collective-permute-done((f32[384,256]{1,0:T(8,128)S(1)}, f32[384,256]{1,0:T(8,128)S(1)}, u32[]{:S(2)}, u32[]{:S(2)}) %collective-permute-start.3) | collective-permute-done | bytes 393248 | tf_op jit(solution)/shard_map/ppermute | solution.py:234
  331.4 4.6 %fusion.9 = bf16[8,128,1024]{2,0,1:T(8,128)(2,1)S(1)} fusion(bf16[16,128,1024]{2,1,0:T(8,128)(2,1)} %all-to-all-done.3, s32[16]{0:T(128)S(1)} %add_reduce_fusion, pred[16]{0:T(512)(128)(4,1)S(1)} %broadcast_compare_fusion), kind=kOutput, calls=%fused_computation.10 | convolution fusion | flops 34603264 | bytes 6291536 | tf_op jit(solution)/shard_map/ab,brh->arh/dot_general | solution.py:31
  336.0 2.5 copy.32
  338.4 4.6 %fusion.6 = bf16[8,128,1024]{2,0,1:T(8,128)(2,1)S(1)} fusion(bf16[16,128,1024]{2,1,0:T(8,128)(2,1)} %all-to-all-done.2, s32[16]{0:T(128)S(1)} %add_reduce_fusion, pred[16]{0:T(512)(128)(4,1)S(1)} %broadcast_compare_fusion), kind=kOutput, calls=%fused_computation.9 | convolution fusion | flops 34603264 | bytes 6291536 | tf_op jit(solution)/shard_map/ab,brh->arh/dot_general | solution.py:31
  343.1 2.5 copy.28
  (52 shorter events, 5.0 us)
Async XLA Ops:
  0.6 27.5 %copy-start = (s32[16384]{0:T(1024)S(1)}, s32[16384]{0:T(1024)}, u32[]{:S(2)}) copy-start(s32[16384]{0:T(1024)} %param.12) | copy-start | bytes 196612
  6.5 7.2 %copy-start.5 = (bf16[1024,128]{1,0:T(8,128)(2,1)S(1)}, bf16[1024,128]{1,0:T(8,128)(2,1)}, u32[]{:S(2)}) copy-start(bf16[1024,128]{1,0:T(8,128)(2,1)} %param.9) | copy-start | bytes 786436
  6.5 7.3 %copy-start.6 = (bf16[1024,128]{1,0:T(8,128)(2,1)S(1)}, bf16[1024,128]{1,0:T(8,128)(2,1)}, u32[]{:S(2)}) copy-start(bf16[1024,128]{1,0:T(8,128)(2,1)} %param.10) | copy-start | bytes 786436
  6.5 42.8 %all-to-all-start.1 = ((bf16[128,8,1024]{2,0,1:T(8,128)(2,1)}), bf16[128,8,1024]{2,0,1:T(8,128)(2,1)S(1)}, u32[]{:S(2)}, u32[]{:S(2)}) async-start(bf16[128,8,1024]{2,0,1:T(8,128)(2,1)} %copy.24), calls=%async_computation.1 | async-start | bytes 4194304 | tf_op jit(solution)/shard_map/all_to_all | solution.py:257
  13.9 44.1 %collective-permute-start.1 = (bf16[1024,256]{1,0:T(8,128)(2,1)S(1)}, bf16[1024,256]{1,0:T(8,128)(2,1)S(1)}, u32[]{:S(2)}, u32[]{:S(2)}) collective-permute-start(bf16[1024,256]{1,0:T(8,128)(2,1)S(1)} %constant_dynamic-update-slice_fusion), channel_id=1, source_target_pairs={{0,8},{8,16},{16,24},{24,32},{32,40},{40,48},{48,56},{56,64},{64,7... | collective-permute-start | bytes 1572872 | tf_op jit(solution)/shard_map/ppermute | solution.py:229
  16.5 41.5 %collective-permute-start = (bf16[384,256]{1,0:T(8,128)(2,1)}, bf16[384,256]{1,0:T(8,128)(2,1)S(1)}, u32[]{:S(2)}, u32[]{:S(2)}) collective-permute-start(bf16[384,256]{1,0:T(8,128)(2,1)} %slice.104), channel_id=1, source_target_pairs={{0,16},{8,24},{16,32},{24,40},{32,48},{40,56},{48,64},{56,72},{64,... | collective-permute-start | bytes 589832 | tf_op jit(solution)/shard_map/ppermute | solution.py:229
  41.2 15.4 %copy-start.7 = (s32[128]{0:T(128)S(1)}, s32[128]{0:T(128)}, u32[]{:S(2)}) copy-start(s32[128]{0:T(128)} %param.13) | copy-start | bytes 1540
  49.4 1.3 copy-start.2
  50.7 33.4 %all-to-all-start = ((bf16[128,8,1024]{2,0,1:T(8,128)(2,1)}), bf16[128,8,1024]{2,0,1:T(8,128)(2,1)}, u32[]{:S(2)}, u32[]{:S(2)}) async-start(bf16[128,8,1024]{2,0,1:T(8,128)(2,1)} %copy.22), calls=%async_computation | async-start | bytes 4194304 | tf_op jit(solution)/shard_map/all_to_all | solution.py:250
  180.3 5.9 %copy-start.3 = (bf16[8,128,1024]{2,1,0:T(8,128)(2,1)S(1)}, bf16[8,128,1024]{2,1,0:T(8,128)(2,1)}, u32[]{:S(2)}) copy-start(bf16[8,128,1024]{2,1,0:T(8,128)(2,1)} %get-tuple-element.20) | copy-start | bytes 6291460
  180.3 65.0 %all-to-all-start.3 = ((bf16[16,128,1024]{2,1,0:T(8,128)(2,1)}), bf16[16,128,1024]{2,1,0:T(8,128)(2,1)}, u32[]{:S(2)}, u32[]{:S(2)}) async-start(bf16[16,128,1024]{2,1,0:T(8,128)(2,1)} %copy.30), calls=%async_computation.3 | async-start | bytes 8388608 | tf_op jit(solution)/shard_map/all_to_all | solution.py:286
  245.3 93.1 %all-to-all-start.2 = ((bf16[16,128,1024]{2,1,0:T(8,128)(2,1)}), bf16[16,128,1024]{2,1,0:T(8,128)(2,1)}, u32[]{:S(2)}, u32[]{:S(2)}) async-start(bf16[16,128,1024]{2,1,0:T(8,128)(2,1)} %copy.26), calls=%async_computation.2 | async-start | bytes 8388608 | tf_op jit(solution)/shard_map/all_to_all | solution.py:283
  251.1 1.7 copy-start.4
  253.9 58.4 %collective-permute-start.2 = (f32[1024,256]{1,0:T(8,128)}, f32[1024,256]{1,0:T(8,128)}, u32[]{:S(2)}, u32[]{:S(2)}) collective-permute-start(f32[1024,256]{1,0:T(8,128)} %slice.108), channel_id=1, source_target_pairs={{8,0},{16,8},{24,16},{32,24},{40,32},{48,40},{56,48},{64,56},{72,6... | collective-permute-start | bytes 3145736 | tf_op jit(solution)/shard_map/ppermute | solution.py:234
  256.3 74.0 %collective-permute-start.3 = (f32[384,256]{1,0:T(8,128)S(1)}, f32[384,256]{1,0:T(8,128)S(1)}, u32[]{:S(2)}, u32[]{:S(2)}) collective-permute-start(f32[384,256]{1,0:T(8,128)S(1)} %slice.110), channel_id=1, source_target_pairs={{16,0},{24,8},{32,16},{40,24},{48,32},{56,40},{64,48},{72,56},{80,... | collective-permute-start | bytes 1179656 | tf_op jit(solution)/shard_map/ppermute | solution.py:234
  338.4 7.1 %copy-start.1 = (s32[16384]{0:T(1024)S(1)}, s32[16384]{0:T(1024)}, u32[]{:S(2)}) copy-start(s32[16384]{0:T(1024)} %param.12) | copy-start | bytes 196612

commit v3 on v2

--- a/solution.py
+++ b/solution.py
@@ -10,6 +10,7 @@
 HEAD_DIM = 128
 BLOCK = 128
 BAND = 12
+CHUNKS = 2
 
 
 def routing(block_owner, ctx_count, ctx_rank, blocks_here):
@@ -240,55 +241,49 @@
     ctx_rank = lax.axis_index("ctx")
     local_rows, width = queries.shape
     head_cols = width // tp_count
+    chunk_cols = head_cols // CHUNKS
     tok_dev = key_rows.shape[0]
     kv_cols = key_rows.shape[1]
     blocks_here = tok_dev // BLOCK
     reach = (BAND - 1) * BLOCK
     far = reach - tok_dev
     send_pick, recv_pick, _ = routing(block_owner, ctx_count, ctx_rank, blocks_here)
-    query_split, grad_split = (
-        lax.all_to_all(
-            queries.reshape(local_rows, tp_count, head_cols),
-            "tp",
-            split_axis=1,
-            concat_axis=0,
-            tiled=True,
-        ),
-        lax.all_to_all(
-            out_grad.reshape(local_rows, tp_count, head_cols),
-            "tp",
-            split_axis=1,
-            concat_axis=0,
-            tiled=True,
-        ),
-    )
-    query_blocks = query_split.reshape(blocks_here, BLOCK, head_cols)
-    grad_blocks = grad_split.reshape(blocks_here, BLOCK, head_cols)
     kv_here = jnp.concatenate([key_rows, value_rows], axis=1)
     kv_near = shift_from_below(kv_here, ctx_count, 1)
     kv_far = shift_from_below(kv_here[tok_dev - far :], ctx_count, 2)
     halo = jnp.concatenate([kv_far, kv_near, kv_here], axis=0)
     halo_key = halo[:, :kv_cols]
     halo_value = halo[:, kv_cols:]
-    halo_doc = halo_docs(doc_ids, ctx_rank * tok_dev - reach, reach + tok_dev)
-    out_blocks, dq_blocks, key_grad, value_grad = fused_attention(
-        query_blocks, grad_blocks, halo_key, halo_value, halo_doc
-    )
+    padded_doc = jnp.concatenate([jnp.full((reach,), -1, doc_ids.dtype), doc_ids])
+    halo_doc = lax.dynamic_slice_in_dim(padded_doc, ctx_rank * tok_dev, reach + tok_dev, 0)
+    query_parts = queries.reshape(local_rows, tp_count, CHUNKS, chunk_cols)
+    grad_parts = out_grad.reshape(local_rows, tp_count, CHUNKS, chunk_cols)
+    held_parts = []
+    key_grad = None
+    for chunk in range(CHUNKS):
+        both = jnp.concatenate([query_parts[:, :, chunk], grad_parts[:, :, chunk]], axis=-1)
+        both = lax.all_to_all(both, "tp", split_axis=1, concat_axis=0, tiled=True)
+        both = both.reshape(blocks_here, BLOCK, 2 * chunk_cols)
+        out_blocks, dq_blocks, chunk_key_grad, chunk_value_grad = fused_attention(
+            both[..., :chunk_cols], both[..., chunk_cols:], halo_key, halo_value, halo_doc
+        )
+        if key_grad is None:
+            key_grad, value_grad = chunk_key_grad, chunk_value_grad
+        else:
+            key_grad = key_grad + chunk_key_grad
+            value_grad = value_grad + chunk_value_grad
+        results = jnp.concatenate([out_blocks, dq_blocks], axis=-1)
+        sent = lax.all_to_all(
+            select_rows(send_pick, results), "ctx", split_axis=0, concat_axis=0, tiled=True
+        )
+        held_parts.append(select_rows(recv_pick, sent))
     kv_grad = jnp.concatenate([key_grad, value_grad], axis=1)
     grad_near = shift_to_below(kv_grad[far:reach], ctx_count, 1)
     grad_far = shift_to_below(kv_grad[:far], ctx_count, 2)
     kv_total = kv_grad[reach:] + grad_near
     kv_total = kv_total.at[tok_dev - far :].add(grad_far)
-    sent_out, sent_dq = (
-        lax.all_to_all(
-            select_rows(send_pick, out_blocks), "ctx", split_axis=0, concat_axis=0, tiled=True
-        ),
-        lax.all_to_all(
-            select_rows(send_pick, dq_blocks), "ctx", split_axis=0, concat_axis=0, tiled=True
-        ),
-    )
-    held_out = select_rows(recv_pick, sent_out)
-    held_dq = select_rows(recv_pick, sent_dq)
+    held_out = jnp.concatenate([part[..., :chunk_cols] for part in held_parts], axis=-1)
+    held_dq = jnp.concatenate([part[..., chunk_cols:] for part in held_parts], axis=-1)
     return (
         held_out.reshape(tok_dev, head_cols),
         held_dq.reshape(tok_dev, head_cols),

time: 346 us -> 289 us (0.84)
  waiting for transfers between devices: 155 us -> 88.2 us
  other arithmetic: 3.2 us -> 15.7 us
  local copies, waits for them, and re-layouts: 48.6 us -> 43.8 us
    all_to_all x4, waiting for transfers between devices: 86.1 us -> 19.8 us  [the longest x2 17.4 us: on_device(): both = lax.all_to_all(both, 'tp', split_axis=1, concat_axis=0, tiled=True)]
    gather x1 -> x0, local copies, waits for them, and re-layouts: 13 us -> none  [halo_docs(): jnp.take(doc_ids, jnp.clip(positions, 0, doc_ids.shape[0] - 1), axis=0)]
    concatenate x0 -> x7, other arithmetic: none -> 9.45 us  [the longest x2 4.4 us: on_device(): jnp.concatenate([query_parts[:, :, chunk], grad_parts[:, :, chunk]], axis...]
    reshape x2 -> x0, local copies, waits for them, and re-layouts: 6.54 us -> none  [the longest x1 3.91 us: on_device(): queries.reshape(local_rows, tp_count, head_cols)]
    slice x2 -> x6, local copies, waits for them, and re-layouts: 1.07 us -> 7.56 us  [the longest x2 4.66 us: on_device(): both[..., chunk_cols:]]
    convert_element_type x4 -> x2, local copies, waits for them, and re-layouts: 13.6 us -> 8.64 us  [select_rows(): return picked.astype(jnp.bfloat16)]
    concatenate x1 -> x2, local copies, waits for them, and re-layouts: 0.09 us -> 4.95 us  [the longest x1 2.48 us: on_device(): jnp.concatenate([part[..., :chunk_cols] for part in held_parts], axis=-1)]
    unnamed x21 -> x25, local copies, waits for them, and re-layouts: 10.6 us -> 15.2 us
  transfers between devices with their start and end apart: 8 -> 8, of which waited for: 5 -> 4; matrix products, arithmetic and copies ran while one was open for 13% -> 16% of each run, Pallas kernels for 0% -> 32%
where the time goes in v3:
time: 289 us; the launch traced here: 288 us
  Pallas kernels  91.6 us (32%)
  waiting for transfers between devices  88.2 us (31%)
  local copies, waits for them, and re-layouts  43.8 us (15%)
  starting transfers between devices  34.8 us (12%)
  other arithmetic  15.7 us (5%)
  matrix products  12.8 us (4%)
    pallas_call x2, Pallas kernels, fused_attention(): pl.pallas_call(fused_kernel, grid=(blocks, heads_here), in_specs=[pl.Bloc...  91.6 us
    ppermute x2, waiting for transfers between devices, shift_to_below(): return lax.ppermute(x, 'ctx', pairs)  68.4 us
    all_to_all x2, waiting for transfers between devices, on_device(): both = lax.all_to_all(both, 'tp', split_axis=1, concat_axis=0, tiled=True)  17.4 us
    unnamed x25, local copies, waits for them, and re-layouts  15.2 us
    dot_general x4, matrix products, select_rows(): jnp.einsum('ab,brh->arh', selector, blocks, preferred_element_type=jnp.fl...  12.8 us
    all_to_all x2, starting transfers between devices, on_device(): both = lax.all_to_all(both, 'tp', split_axis=1, concat_axis=0, tiled=True)  12.1 us
    all_to_all x2, starting transfers between devices, on_device(): lax.all_to_all(select_rows(send_pick, results), 'ctx', split_axis=0, conc...  11.4 us
    convert_element_type x2, local copies, waits for them, and re-layouts, select_rows(): return picked.astype(jnp.bfloat16)  8.64 us
  transfers between devices with their start and end apart: 8, of which 4 were waited for; matrix products, arithmetic and copies ran while one was open for 16% of the time, Pallas kernels for 32%

profile of v3, /device:TPU:60, one launch (start us, length us, event | category | flops | bytes accessed | tf_op | source)
XLA Modules:
  0.0 287.8 jit_solution(10678789034965882957)
XLA Ops:
  0.6 3.2 %copy.23 = bf16[128,8192]{0,1:T(8,128)(2,1)S(1)} copy(bf16[128,8192]{1,0:T(8,128)(2,1)} %param.8) | data formatting | bytes 4194304 | tf_op args[0]
  5.0 2.3 copy.39
  7.3 3.2 %copy.25 = bf16[128,8192]{0,1:T(8,128)(2,1)S(1)} copy(bf16[128,8192]{1,0:T(8,128)(2,1)} %param.11) | data formatting | bytes 4194304 | tf_op args[3]
  15.2 7.2 %all-to-all-start = ((bf16[128,8,1024]{2,0,1:T(8,128)(2,1)}), bf16[128,8,1024]{2,0,1:T(8,128)(2,1)S(1)}, u32[]{:S(2)}, u32[]{:S(2)}) async-start(bf16[128,8,1024]{2,0,1:T(8,128)(2,1)} %pad_maximum_fusion), calls=%async_computation | async-start | bytes 4194304 | tf_op jit(solution)/shard_map/all_to_all | solution.py:265
  23.2 1.7 constant_dynamic-update-slice_fusion
  24.9 1.9 collective-permute-start.1
  26.8 1.6 slice.162
  28.4 3.5 %collective-permute-start = (bf16[384,256]{1,0:T(8,128)(2,1)}, bf16[384,256]{1,0:T(8,128)(2,1)S(1)}, u32[]{:S(2)}, u32[]{:S(2)}) collective-permute-start(bf16[384,256]{1,0:T(8,128)(2,1)} %slice.162), channel_id=1, source_target_pairs={{0,16},{8,24},{16,32},{24,40},{32,48},{40,56},{48,64},{56,72},{64,... | collective-permute-start | bytes 589832 | tf_op jit(solution)/shard_map/ppermute | solution.py:230
  35.5 2.4 copy.42
  37.8 2.8 pad_maximum_fusion.2
  40.6 17.4 %all-to-all-done = bf16[128,8,1024]{2,0,1:T(8,128)(2,1)S(1)} async-done(((bf16[128,8,1024]{2,0,1:T(8,128)(2,1)}), bf16[128,8,1024]{2,0,1:T(8,128)(2,1)S(1)}, u32[]{:S(2)}, u32[]{:S(2)}) %all-to-all-start) | async-done | bytes 2097184 | tf_op jit(solution)/shard_map/all_to_all | solution.py:265
  58.0 4.9 %all-to-all-start.2 = ((bf16[128,8,1024]{2,0,1:T(8,128)(2,1)}), bf16[128,8,1024]{2,0,1:T(8,128)(2,1)}, u32[]{:S(2)}, u32[]{:S(2)}) async-start(bf16[128,8,1024]{2,0,1:T(8,128)(2,1)} %pad_maximum_fusion.2), calls=%async_computation.2 | async-start | bytes 4194304 | tf_op jit(solution)/shard_map/all_to_all | solution.py:265
  66.9 45.8 %shard_map.93 = (bf16[8,128,512]{2,1,0:T(8,128)(2,1)}, bf16[8,128,512]{2,1,0:T(8,128)(2,1)}, f32[2432,128]{1,0:T(8,128)}, f32[2432,128]{1,0:T(8,128)}) custom-call(s32[8,128,1]{2,1,0:T(8,128)} %copy.27.qdoc_ref, s32[8,1,1536]{2,1,0:T(1,128)} %reshape.104.kdoc_ref, bf16[8,128,512]{2,1,0:T(8,128)(2,1)} %get-tuple-element.37.q_ref, ...), custom_call_target="tpu_custom_call" | custom-call | tf_op jit(solution)/shard_map/pallas_call | solution.py:206
  112.7 1.8 pad_maximum_fusion.1
  114.5 1.8 convolution_convert_fusion.1
  116.3 4.3 %copy.29 = bf16[16,128,1024]{2,1,0:T(8,128)(2,1)} copy(bf16[16,128,1024]{2,0,1:T(8,128)(2,1)S(1)} %convolution_convert_fusion.1) | data formatting | bytes 8388608 | tf_op jit(solution)/shard_map/convert_element_type | solution.py:33
  120.7 5.7 %all-to-all-start.1 = ((bf16[16,128,1024]{2,1,0:T(8,128)(2,1)}), bf16[16,128,1024]{2,1,0:T(8,128)(2,1)}, u32[]{:S(2)}, u32[]{:S(2)}) async-start(bf16[16,128,1024]{2,1,0:T(8,128)(2,1)} %copy.29), calls=%async_computation.1 | async-start | bytes 8388608 | tf_op jit(solution)/shard_map/all_to_all | solution.py:276
  126.4 3.1 %fusion.35 = (bf16[8,128,512]{2,1,0:T(8,128)(2,1)}, bf16[8,128,512]{2,1,0:T(8,128)(2,1)}) fusion(bf16[8,128,1024]{2,1,0:T(8,128)(2,1)} %bitcast.18), kind=kLoop, calls=%fused_computation.59 | loop fusion | bytes 4194304 | tf_op jit(solution)/shard_map/slice | solution.py:268
  129.5 45.8 %shard_map.94 = (bf16[8,128,512]{2,1,0:T(8,128)(2,1)}, bf16[8,128,512]{2,1,0:T(8,128)(2,1)}, f32[2432,128]{1,0:T(8,128)}, f32[2432,128]{1,0:T(8,128)}) custom-call(s32[8,128,1]{2,1,0:T(8,128)} %copy.27.qdoc_ref, s32[8,1,1536]{2,1,0:T(1,128)} %reshape.104.kdoc_ref, bf16[8,128,512]{2,1,0:T(8,128)(2,1)} %get-tuple-element.43.q_ref, ...), custom_call_target="tpu_custom_call" | custom-call | tf_op jit(solution)/shard_map/pallas_call | solution.py:206
  175.2 1.8 pad_maximum_fusion.3
  177.0 1.8 convolution_convert_fusion
  178.8 4.3 %copy.35 = bf16[16,128,1024]{2,1,0:T(8,128)(2,1)} copy(bf16[16,128,1024]{2,0,1:T(8,128)(2,1)S(1)} %convolution_convert_fusion) | data formatting | bytes 8388608 | tf_op jit(solution)/shard_map/convert_element_type | solution.py:33
  183.2 2.4 all-to-all-done.1
  185.6 5.7 %all-to-all-start.3 = ((bf16[16,128,1024]{2,1,0:T(8,128)(2,1)}), bf16[16,128,1024]{2,1,0:T(8,128)(2,1)}, u32[]{:S(2)}, u32[]{:S(2)}) async-start(bf16[16,128,1024]{2,1,0:T(8,128)(2,1)} %copy.35), calls=%async_computation.3 | async-start | bytes 8388608 | tf_op jit(solution)/shard_map/all_to_all | solution.py:276
  193.5 2.2 collective-permute-start.2
  196.6 3.6 %collective-permute-start.3 = (f32[384,256]{1,0:T(8,128)}, f32[384,256]{1,0:T(8,128)}, u32[]{:S(2)}, u32[]{:S(2)}) collective-permute-start(f32[384,256]{1,0:T(8,128)} %pad_maximum_fusion.7), channel_id=1, source_target_pairs={{16,0},{24,8},{32,16},{40,24},{48,32},{56,40},{64,48},{72,56},{80,... | collective-permute-start | bytes 1179656 | tf_op jit(solution)/shard_map/ppermute | solution.py:235
  201.0 51.4 %collective-permute-done.2 = f32[1024,256]{1,0:T(8,128)} collective-permute-done((f32[1024,256]{1,0:T(8,128)S(1)}, f32[1024,256]{1,0:T(8,128)}, u32[]{:S(2)}, u32[]{:S(2)}) %collective-permute-start.2) | collective-permute-done | bytes 1048608 | tf_op jit(solution)/shard_map/ppermute | solution.py:235
  253.7 17.0 %collective-permute-done.3 = f32[384,256]{1,0:T(8,128)} collective-permute-done((f32[384,256]{1,0:T(8,128)}, f32[384,256]{1,0:T(8,128)}, u32[]{:S(2)}, u32[]{:S(2)}) %collective-permute-start.3) | collective-permute-done | bytes 393248 | tf_op jit(solution)/shard_map/ppermute | solution.py:235
  272.7 4.6 %fusion.6 = bf16[8,128,1024]{2,0,1:T(8,128)(2,1)S(1)} fusion(bf16[16,128,1024]{2,1,0:T(8,128)(2,1)} %all-to-all-done.1, s32[16]{0:T(128)S(1)} %add_reduce_fusion, pred[16]{0:T(512)(128)(4,1)S(1)} %copy-done.7), kind=kOutput, calls=%fused_computation.18 | convolution fusion | flops 34603264 | bytes 6291536 | tf_op jit(solution)/shard_map/ab,brh->arh/dot_general | solution.py:32
  277.5 4.6 %fusion.9 = bf16[8,128,1024]{2,0,1:T(8,128)(2,1)S(1)} fusion(bf16[16,128,1024]{2,1,0:T(8,128)(2,1)} %all-to-all-done.3, s32[16]{0:T(128)S(1)} %add_reduce_fusion, pred[16]{0:T(512)(128)(4,1)S(1)} %copy-done.7), kind=kOutput, calls=%fused_computation.19 | convolution fusion | flops 34603264 | bytes 6291536 | tf_op jit(solution)/shard_map/ab,brh->arh/dot_general | solution.py:32
  282.9 2.5 copy.37
  285.3 2.5 copy.38
  (62 shorter events, 22.1 us)
Async XLA Ops:
  12.0 1.6 copy-start
  15.2 7.2 %copy-start.5 = (bf16[1024,128]{1,0:T(8,128)(2,1)S(1)}, bf16[1024,128]{1,0:T(8,128)(2,1)}, u32[]{:S(2)}) copy-start(bf16[1024,128]{1,0:T(8,128)(2,1)} %param.9) | copy-start | bytes 786436
  15.2 16.8 %copy-start.8 = (s32[128]{0:T(128)S(1)}, s32[128]{0:T(128)}, u32[]{:S(2)}) copy-start(s32[128]{0:T(128)} %param.13) | copy-start | bytes 1540
  15.2 16.9 %copy-start.6 = (s32[16384]{0:T(1024)S(1)}, s32[16384]{0:T(1024)}, u32[]{:S(2)}) copy-start(s32[16384]{0:T(1024)} %param.12) | copy-start | bytes 196612
  15.2 42.8 %all-to-all-start = ((bf16[128,8,1024]{2,0,1:T(8,128)(2,1)}), bf16[128,8,1024]{2,0,1:T(8,128)(2,1)S(1)}, u32[]{:S(2)}, u32[]{:S(2)}) async-start(bf16[128,8,1024]{2,0,1:T(8,128)(2,1)} %pad_maximum_fusion), calls=%async_computation | async-start | bytes 4194304 | tf_op jit(solution)/shard_map/all_to_all | solution.py:265
  24.9 38.0 %collective-permute-start.1 = (bf16[1024,256]{1,0:T(8,128)(2,1)}, bf16[1024,256]{1,0:T(8,128)(2,1)}, u32[]{:S(2)}, u32[]{:S(2)}) collective-permute-start(bf16[1024,256]{1,0:T(8,128)(2,1)} %constant_dynamic-update-slice_fusion), channel_id=1, source_target_pairs={{0,8},{8,16},{16,24},{24,32},{32,40},{40,48},{48,56},{56,64},{64,7... | collective-permute-start | bytes 1572872 | tf_op jit(solution)/shard_map/ppermute | solution.py:230
  28.4 34.5 %collective-permute-start = (bf16[384,256]{1,0:T(8,128)(2,1)}, bf16[384,256]{1,0:T(8,128)(2,1)S(1)}, u32[]{:S(2)}, u32[]{:S(2)}) collective-permute-start(bf16[384,256]{1,0:T(8,128)(2,1)} %slice.162), channel_id=1, source_target_pairs={{0,16},{8,24},{16,32},{24,40},{32,48},{40,56},{48,64},{56,72},{64,... | collective-permute-start | bytes 589832 | tf_op jit(solution)/shard_map/ppermute | solution.py:230
  35.5 2.4 copy-start.1
  58.0 62.6 %all-to-all-start.2 = ((bf16[128,8,1024]{2,0,1:T(8,128)(2,1)}), bf16[128,8,1024]{2,0,1:T(8,128)(2,1)}, u32[]{:S(2)}, u32[]{:S(2)}) async-start(bf16[128,8,1024]{2,0,1:T(8,128)(2,1)} %pad_maximum_fusion.2), calls=%async_computation.2 | async-start | bytes 4194304 | tf_op jit(solution)/shard_map/all_to_all | solution.py:265
  120.7 64.9 %all-to-all-start.1 = ((bf16[16,128,1024]{2,1,0:T(8,128)(2,1)}), bf16[16,128,1024]{2,1,0:T(8,128)(2,1)}, u32[]{:S(2)}, u32[]{:S(2)}) async-start(bf16[16,128,1024]{2,1,0:T(8,128)(2,1)} %copy.29), calls=%async_computation.1 | async-start | bytes 8388608 | tf_op jit(solution)/shard_map/all_to_all | solution.py:276
  183.1 8.2 %copy-start.3 = (f32[2432,128]{1,0:T(8,128)S(1)}, f32[2432,128]{1,0:T(8,128)}, u32[]{:S(2)}) copy-start(f32[2432,128]{1,0:T(8,128)} %get-tuple-element.28) | copy-start | bytes 3735556
  185.6 91.9 %all-to-all-start.3 = ((bf16[16,128,1024]{2,1,0:T(8,128)(2,1)}), bf16[16,128,1024]{2,1,0:T(8,128)(2,1)}, u32[]{:S(2)}, u32[]{:S(2)}) async-start(bf16[16,128,1024]{2,1,0:T(8,128)(2,1)} %copy.35), calls=%async_computation.3 | async-start | bytes 8388608 | tf_op jit(solution)/shard_map/all_to_all | solution.py:276
  191.3 1.7 copy-start.2
  191.3 2.0 copy-start.4
  193.5 58.9 %collective-permute-start.2 = (f32[1024,256]{1,0:T(8,128)S(1)}, f32[1024,256]{1,0:T(8,128)}, u32[]{:S(2)}, u32[]{:S(2)}) collective-permute-start(f32[1024,256]{1,0:T(8,128)S(1)} %fusion.12), channel_id=1, source_target_pairs={{8,0},{16,8},{24,16},{32,24},{40,32},{48,40},{56,48},{64,56},{72,6... | collective-permute-start | bytes 3145736 | tf_op jit(solution)/shard_map/ppermute | solution.py:235
  196.6 74.1 %collective-permute-start.3 = (f32[384,256]{1,0:T(8,128)}, f32[384,256]{1,0:T(8,128)}, u32[]{:S(2)}, u32[]{:S(2)}) collective-permute-start(f32[384,256]{1,0:T(8,128)} %pad_maximum_fusion.7), channel_id=1, source_target_pairs={{16,0},{24,8},{32,16},{40,24},{48,32},{56,40},{64,48},{72,56},{80,... | collective-permute-start | bytes 1179656 | tf_op jit(solution)/shard_map/ppermute | solution.py:235
  253.7 19.0 %copy-start.7 = (pred[16]{0:T(512)(128)(4,1)S(1)}, pred[16]{0:T(512)(128)(4,1)}, u32[]{:S(2)}) copy-start(pred[16]{0:T(512)(128)(4,1)} %broadcast_compare_fusion) | copy-start | bytes 52

commit v4 on v3

--- a/solution.py
+++ b/solution.py
@@ -155,11 +155,11 @@
 
 def fused_kernel(qdoc_ref, kdoc_ref, q_ref, do_ref, k_ref, v_ref, out_ref, dq_ref, dk_ref, dv_ref):
     block = pl.program_id(0)
-    head = pl.program_id(1)
     window_rows = BAND * BLOCK
     scale = HEAD_DIM ** (-0.5)
-
-    @pl.when((block == 0) & (head == 0))
+    heads_here = q_ref.shape[2] // HEAD_DIM
+
+    @pl.when(block == 0)
     def _():
         dk_ref[...] = jnp.zeros_like(dk_ref)
         dv_ref[...] = jnp.zeros_like(dv_ref)
@@ -167,33 +167,41 @@
     start = pl.multiple_of(block * BLOCK, BLOCK)
     key_window = k_ref[pl.ds(start, window_rows), :]
     value_window = v_ref[pl.ds(start, window_rows), :]
-    query = q_ref[0]
-    raw = lax.dot_general(query, key_window, TRANS_B, preferred_element_type=jnp.float32) * scale
-    rows = lax.broadcasted_iota(jnp.int32, raw.shape, 0) + (BAND - 1) * BLOCK
-    cols = lax.broadcasted_iota(jnp.int32, raw.shape, 1)
+    shape = (BLOCK, window_rows)
+    rows = lax.broadcasted_iota(jnp.int32, shape, 0) + (BAND - 1) * BLOCK
+    cols = lax.broadcasted_iota(jnp.int32, shape, 1)
     allowed = (qdoc_ref[0] == kdoc_ref[0]) & (cols <= rows)
-    scores = jnp.where(allowed, raw, -1e30)
-    row_max = jnp.max(scores, axis=1, keepdims=True)
-    log_total = row_max + jnp.log(jnp.sum(jnp.exp(scores - row_max), axis=1, keepdims=True))
-    weights = jnp.exp(scores - log_total)
-    soft_low = weights.astype(jnp.bfloat16)
-    out = jnp.dot(soft_low, value_window, preferred_element_type=jnp.float32).astype(jnp.bfloat16)
-    out_ref[0] = out
-    grad = do_ref[0]
-    row_dot = jnp.sum(grad.astype(jnp.float32) * out.astype(jnp.float32), axis=1, keepdims=True)
-    prob_grad = lax.dot_general(grad, value_window, TRANS_B, preferred_element_type=jnp.float32)
-    score_grad = (weights * (prob_grad - row_dot)).astype(jnp.bfloat16)
-    dq = jnp.dot(score_grad, key_window, preferred_element_type=jnp.float32) * scale
-    dq_ref[0] = dq.astype(jnp.bfloat16)
-    dk = lax.dot_general(score_grad, query, TRANS_A, preferred_element_type=jnp.float32) * scale
-    dv = lax.dot_general(soft_low, grad, TRANS_A, preferred_element_type=jnp.float32)
-    dk_ref[pl.ds(start, window_rows), :] += dk
-    dv_ref[pl.ds(start, window_rows), :] += dv
+    bias = jnp.where(allowed, 0.0, -1e30).astype(jnp.float32)
+    dk_sum = None
+    for head in range(heads_here):
+        cols_of = slice(head * HEAD_DIM, (head + 1) * HEAD_DIM)
+        query = q_ref[0, :, cols_of]
+        raw = lax.dot_general(query, key_window, TRANS_B, preferred_element_type=jnp.float32) * scale
+        scores = raw + bias
+        row_max = jnp.max(scores, axis=1, keepdims=True)
+        log_total = row_max + jnp.log(jnp.sum(jnp.exp(scores - row_max), axis=1, keepdims=True))
+        weights = jnp.exp(scores - log_total)
+        soft_low = weights.astype(jnp.bfloat16)
+        out = jnp.dot(soft_low, value_window, preferred_element_type=jnp.float32).astype(jnp.bfloat16)
+        out_ref[0, :, cols_of] = out
+        grad = do_ref[0, :, cols_of]
+        row_dot = jnp.sum(grad.astype(jnp.float32) * out.astype(jnp.float32), axis=1, keepdims=True)
+        prob_grad = lax.dot_general(grad, value_window, TRANS_B, preferred_element_type=jnp.float32)
+        score_grad = (weights * (prob_grad - row_dot)).astype(jnp.bfloat16)
+        dq = jnp.dot(score_grad, key_window, preferred_element_type=jnp.float32) * scale
+        dq_ref[0, :, cols_of] = dq.astype(jnp.bfloat16)
+        dk = lax.dot_general(score_grad, query, TRANS_A, preferred_element_type=jnp.float32) * scale
+        dv = lax.dot_general(soft_low, grad, TRANS_A, preferred_element_type=jnp.float32)
+        if dk_sum is None:
+            dk_sum, dv_sum = dk, dv
+        else:
+            dk_sum, dv_sum = dk_sum + dk, dv_sum + dv
+    dk_ref[pl.ds(start, window_rows), :] += dk_sum
+    dv_ref[pl.ds(start, window_rows), :] += dv_sum
 
 
 def fused_attention(query_blocks, grad_blocks, halo_key, halo_value, halo_doc):
     blocks, _, width = query_blocks.shape
-    heads_here = width // HEAD_DIM
     window_rows = BAND * BLOCK
     reach = (BAND - 1) * BLOCK
     halo_rows = halo_key.shape[0]
@@ -201,27 +209,27 @@
     key_doc = jnp.stack(
         [halo_doc[b * BLOCK : b * BLOCK + window_rows] for b in range(blocks)]
     ).reshape(blocks, 1, window_rows)
-    head_spec = pl.BlockSpec((1, BLOCK, HEAD_DIM), lambda b, h: (b, 0, h))
-    whole = pl.BlockSpec((halo_rows, HEAD_DIM), lambda b, h: (0, 0))
+    block_spec = pl.BlockSpec((1, BLOCK, width), lambda b: (b, 0, 0))
+    whole = pl.BlockSpec((halo_rows, HEAD_DIM), lambda b: (0, 0))
     return pl.pallas_call(
         fused_kernel,
-        grid=(blocks, heads_here),
+        grid=(blocks,),
         in_specs=[
-            pl.BlockSpec((1, BLOCK, 1), lambda b, h: (b, 0, 0)),
-            pl.BlockSpec((1, 1, window_rows), lambda b, h: (b, 0, 0)),
-            head_spec,
-            head_spec,
+            pl.BlockSpec((1, BLOCK, 1), lambda b: (b, 0, 0)),
+            pl.BlockSpec((1, 1, window_rows), lambda b: (b, 0, 0)),
+            block_spec,
+            block_spec,
             whole,
             whole,
         ],
-        out_specs=[head_spec, head_spec, whole, whole],
+        out_specs=[block_spec, block_spec, whole, whole],
         out_shape=[
             jax.ShapeDtypeStruct(query_blocks.shape, jnp.bfloat16),
             jax.ShapeDtypeStruct(query_blocks.shape, jnp.bfloat16),
             jax.ShapeDtypeStruct((halo_rows, HEAD_DIM), jnp.float32),
             jax.ShapeDtypeStruct((halo_rows, HEAD_DIM), jnp.float32),
         ],
-        compiler_params=pltpu.CompilerParams(dimension_semantics=("arbitrary", "arbitrary")),
+        compiler_params=pltpu.CompilerParams(dimension_semantics=("arbitrary",)),
     )(query_doc, key_doc, query_blocks, grad_blocks, halo_key, halo_value)
 
 

time: 289 us -> 284 us (0.983)
  Pallas kernels: 91.6 us -> 81 us
  waiting for transfers between devices: 88.2 us -> 93.5 us
    pallas_call x2, Pallas kernels: 91.6 us -> 81 us  [fused_attention(): pl.pallas_call(fused_kernel, grid=(blocks,), in_specs=[pl.BlockSpec((1, B...]
    all_to_all x2, waiting for transfers between devices: 2.42 us -> 7.69 us  [on_device(): lax.all_to_all(select_rows(send_pick, results), 'ctx', split_axis=0, conc...]
  transfers between devices with their start and end apart: 8 -> 8, of which waited for: 4 -> 4; matrix products, arithmetic and copies ran while one was open for 16% -> 17% of each run, Pallas kernels for 32% -> 29%
where the time goes in v4:
time: 284 us; the launch traced here: 283 us
  waiting for transfers between devices  93.5 us (33%)
  Pallas kernels  81 us (29%)
  local copies, waits for them, and re-layouts  43.8 us (15%)
  starting transfers between devices  34.8 us (12%)
  other arithmetic  15.7 us (6%)
  matrix products  12.8 us (5%)
    pallas_call x2, Pallas kernels, fused_attention(): pl.pallas_call(fused_kernel, grid=(blocks,), in_specs=[pl.BlockSpec((1, B...  81 us
    ppermute x2, waiting for transfers between devices, shift_to_below(): return lax.ppermute(x, 'ctx', pairs)  68.4 us
    all_to_all x2, waiting for transfers between devices, on_device(): both = lax.all_to_all(both, 'tp', split_axis=1, concat_axis=0, tiled=True)  17.4 us
    unnamed x25, local copies, waits for them, and re-layouts  15.2 us
    dot_general x4, matrix products, select_rows(): jnp.einsum('ab,brh->arh', selector, blocks, preferred_element_type=jnp.fl...  12.8 us
    all_to_all x2, starting transfers between devices, on_device(): both = lax.all_to_all(both, 'tp', split_axis=1, concat_axis=0, tiled=True)  12.1 us
    all_to_all x2, starting transfers between devices, on_device(): lax.all_to_all(select_rows(send_pick, results), 'ctx', split_axis=0, conc...  11.4 us
    convert_element_type x2, local copies, waits for them, and re-layouts, select_rows(): return picked.astype(jnp.bfloat16)  8.64 us
  transfers between devices with their start and end apart: 8, of which 4 were waited for; matrix products, arithmetic and copies ran while one was open for 17% of the time, Pallas kernels for 29%

profile of v4, /device:TPU:60, one launch (start us, length us, event | category | flops | bytes accessed | tf_op | source)
XLA Modules:
  0.0 282.5 jit_solution(15781092830879026199)
XLA Ops:
  0.6 3.2 %copy.23 = bf16[128,8192]{0,1:T(8,128)(2,1)S(1)} copy(bf16[128,8192]{1,0:T(8,128)(2,1)} %param.8) | data formatting | bytes 4194304 | tf_op args[0]
  5.0 2.3 copy.39
  7.3 3.2 %copy.25 = bf16[128,8192]{0,1:T(8,128)(2,1)S(1)} copy(bf16[128,8192]{1,0:T(8,128)(2,1)} %param.11) | data formatting | bytes 4194304 | tf_op args[3]
  15.2 7.2 %all-to-all-start = ((bf16[128,8,1024]{2,0,1:T(8,128)(2,1)}), bf16[128,8,1024]{2,0,1:T(8,128)(2,1)S(1)}, u32[]{:S(2)}, u32[]{:S(2)}) async-start(bf16[128,8,1024]{2,0,1:T(8,128)(2,1)} %pad_maximum_fusion), calls=%async_computation | async-start | bytes 4194304 | tf_op jit(solution)/shard_map/all_to_all | solution.py:273
  23.2 1.7 constant_dynamic-update-slice_fusion
  24.9 1.9 collective-permute-start.1
  26.8 1.6 slice.162
  28.4 3.5 %collective-permute-start = (bf16[384,256]{1,0:T(8,128)(2,1)}, bf16[384,256]{1,0:T(8,128)(2,1)S(1)}, u32[]{:S(2)}, u32[]{:S(2)}) collective-permute-start(bf16[384,256]{1,0:T(8,128)(2,1)} %slice.162), channel_id=1, source_target_pairs={{0,16},{8,24},{16,32},{24,40},{32,48},{40,56},{48,64},{56,72},{64,... | collective-permute-start | bytes 589832 | tf_op jit(solution)/shard_map/ppermute | solution.py:238
  35.5 2.4 copy.42
  37.8 2.8 pad_maximum_fusion.2
  40.6 17.4 %all-to-all-done = bf16[128,8,1024]{2,0,1:T(8,128)(2,1)S(1)} async-done(((bf16[128,8,1024]{2,0,1:T(8,128)(2,1)}), bf16[128,8,1024]{2,0,1:T(8,128)(2,1)S(1)}, u32[]{:S(2)}, u32[]{:S(2)}) %all-to-all-start) | async-done | bytes 2097184 | tf_op jit(solution)/shard_map/all_to_all | solution.py:273
  58.0 4.9 %all-to-all-start.2 = ((bf16[128,8,1024]{2,0,1:T(8,128)(2,1)}), bf16[128,8,1024]{2,0,1:T(8,128)(2,1)}, u32[]{:S(2)}, u32[]{:S(2)}) async-start(bf16[128,8,1024]{2,0,1:T(8,128)(2,1)} %pad_maximum_fusion.2), calls=%async_computation.2 | async-start | bytes 4194304 | tf_op jit(solution)/shard_map/all_to_all | solution.py:273
  66.9 40.5 %shard_map.93 = (bf16[8,128,512]{2,1,0:T(8,128)(2,1)}, bf16[8,128,512]{2,1,0:T(8,128)(2,1)}, f32[2432,128]{1,0:T(8,128)}, f32[2432,128]{1,0:T(8,128)}) custom-call(s32[8,128,1]{2,1,0:T(8,128)} %copy.27.qdoc_ref, s32[8,1,1536]{2,1,0:T(1,128)} %reshape.104.kdoc_ref, bf16[8,128,512]{2,1,0:T(8,128)(2,1)} %get-tuple-element.37.q_ref, ...), custom_call_target="tpu_custom_call" | custom-call | tf_op jit(solution)/shard_map/pallas_call | solution.py:214
  107.5 1.8 pad_maximum_fusion.1
  109.3 1.8 convolution_convert_fusion.1
  111.1 4.3 %copy.29 = bf16[16,128,1024]{2,1,0:T(8,128)(2,1)} copy(bf16[16,128,1024]{2,0,1:T(8,128)(2,1)S(1)} %convolution_convert_fusion.1) | data formatting | bytes 8388608 | tf_op jit(solution)/shard_map/convert_element_type | solution.py:33
  115.4 5.7 %all-to-all-start.1 = ((bf16[16,128,1024]{2,1,0:T(8,128)(2,1)}), bf16[16,128,1024]{2,1,0:T(8,128)(2,1)}, u32[]{:S(2)}, u32[]{:S(2)}) async-start(bf16[16,128,1024]{2,1,0:T(8,128)(2,1)} %copy.29), calls=%async_computation.1 | async-start | bytes 8388608 | tf_op jit(solution)/shard_map/all_to_all | solution.py:284
  121.1 3.1 %fusion.35 = (bf16[8,128,512]{2,1,0:T(8,128)(2,1)}, bf16[8,128,512]{2,1,0:T(8,128)(2,1)}) fusion(bf16[8,128,1024]{2,1,0:T(8,128)(2,1)} %bitcast.18), kind=kLoop, calls=%fused_computation.59 | loop fusion | bytes 4194304 | tf_op jit(solution)/shard_map/slice | solution.py:276
  124.2 40.5 %shard_map.94 = (bf16[8,128,512]{2,1,0:T(8,128)(2,1)}, bf16[8,128,512]{2,1,0:T(8,128)(2,1)}, f32[2432,128]{1,0:T(8,128)}, f32[2432,128]{1,0:T(8,128)}) custom-call(s32[8,128,1]{2,1,0:T(8,128)} %copy.27.qdoc_ref, s32[8,1,1536]{2,1,0:T(1,128)} %reshape.104.kdoc_ref, bf16[8,128,512]{2,1,0:T(8,128)(2,1)} %get-tuple-element.43.q_ref, ...), custom_call_target="tpu_custom_call" | custom-call | tf_op jit(solution)/shard_map/pallas_call | solution.py:214
  164.7 1.8 pad_maximum_fusion.3
  166.5 1.8 convolution_convert_fusion
  168.3 4.3 %copy.35 = bf16[16,128,1024]{2,1,0:T(8,128)(2,1)} copy(bf16[16,128,1024]{2,0,1:T(8,128)(2,1)S(1)} %convolution_convert_fusion) | data formatting | bytes 8388608 | tf_op jit(solution)/shard_map/convert_element_type | solution.py:33
  172.6 7.7 %all-to-all-done.1 = bf16[16,128,1024]{2,1,0:T(8,128)(2,1)} async-done(((bf16[16,128,1024]{2,1,0:T(8,128)(2,1)}), bf16[16,128,1024]{2,1,0:T(8,128)(2,1)}, u32[]{:S(2)}, u32[]{:S(2)}) %all-to-all-start.1) | async-done | bytes 4194336 | tf_op jit(solution)/shard_map/all_to_all | solution.py:284
  180.3 5.7 %all-to-all-start.3 = ((bf16[16,128,1024]{2,1,0:T(8,128)(2,1)}), bf16[16,128,1024]{2,1,0:T(8,128)(2,1)}, u32[]{:S(2)}, u32[]{:S(2)}) async-start(bf16[16,128,1024]{2,1,0:T(8,128)(2,1)} %copy.35), calls=%async_computation.3 | async-start | bytes 8388608 | tf_op jit(solution)/shard_map/all_to_all | solution.py:284
  188.3 2.2 collective-permute-start.2
  191.4 3.6 %collective-permute-start.3 = (f32[384,256]{1,0:T(8,128)}, f32[384,256]{1,0:T(8,128)}, u32[]{:S(2)}, u32[]{:S(2)}) collective-permute-start(f32[384,256]{1,0:T(8,128)} %pad_maximum_fusion.7), channel_id=1, source_target_pairs={{16,0},{24,8},{32,16},{40,24},{48,32},{56,40},{64,48},{72,56},{80,... | collective-permute-start | bytes 1179656 | tf_op jit(solution)/shard_map/ppermute | solution.py:243
  195.7 51.4 %collective-permute-done.2 = f32[1024,256]{1,0:T(8,128)} collective-permute-done((f32[1024,256]{1,0:T(8,128)S(1)}, f32[1024,256]{1,0:T(8,128)}, u32[]{:S(2)}, u32[]{:S(2)}) %collective-permute-start.2) | collective-permute-done | bytes 1048608 | tf_op jit(solution)/shard_map/ppermute | solution.py:243
  248.5 17.0 %collective-permute-done.3 = f32[384,256]{1,0:T(8,128)} collective-permute-done((f32[384,256]{1,0:T(8,128)}, f32[384,256]{1,0:T(8,128)}, u32[]{:S(2)}, u32[]{:S(2)}) %collective-permute-start.3) | collective-permute-done | bytes 393248 | tf_op jit(solution)/shard_map/ppermute | solution.py:243
  267.4 4.6 %fusion.6 = bf16[8,128,1024]{2,0,1:T(8,128)(2,1)S(1)} fusion(bf16[16,128,1024]{2,1,0:T(8,128)(2,1)} %all-to-all-done.1, s32[16]{0:T(128)S(1)} %add_reduce_fusion, pred[16]{0:T(512)(128)(4,1)S(1)} %copy-done.7), kind=kOutput, calls=%fused_computation.18 | convolution fusion | flops 34603264 | bytes 6291536 | tf_op jit(solution)/shard_map/ab,brh->arh/dot_general | solution.py:32
  272.2 4.6 %fusion.9 = bf16[8,128,1024]{2,0,1:T(8,128)(2,1)S(1)} fusion(bf16[16,128,1024]{2,1,0:T(8,128)(2,1)} %all-to-all-done.3, s32[16]{0:T(128)S(1)} %add_reduce_fusion, pred[16]{0:T(512)(128)(4,1)S(1)} %copy-done.7), kind=kOutput, calls=%fused_computation.19 | convolution fusion | flops 34603264 | bytes 6291536 | tf_op jit(solution)/shard_map/ab,brh->arh/dot_general | solution.py:32
  277.6 2.5 copy.37
  280.1 2.5 copy.38
  (62 shorter events, 22.1 us)
Async XLA Ops:
  12.0 1.6 copy-start
  15.2 7.2 %copy-start.5 = (bf16[1024,128]{1,0:T(8,128)(2,1)S(1)}, bf16[1024,128]{1,0:T(8,128)(2,1)}, u32[]{:S(2)}) copy-start(bf16[1024,128]{1,0:T(8,128)(2,1)} %param.9) | copy-start | bytes 786436
  15.2 16.8 %copy-start.8 = (s32[128]{0:T(128)S(1)}, s32[128]{0:T(128)}, u32[]{:S(2)}) copy-start(s32[128]{0:T(128)} %param.13) | copy-start | bytes 1540
  15.2 16.9 %copy-start.6 = (s32[16384]{0:T(1024)S(1)}, s32[16384]{0:T(1024)}, u32[]{:S(2)}) copy-start(s32[16384]{0:T(1024)} %param.12) | copy-start | bytes 196612
  15.2 42.8 %all-to-all-start = ((bf16[128,8,1024]{2,0,1:T(8,128)(2,1)}), bf16[128,8,1024]{2,0,1:T(8,128)(2,1)S(1)}, u32[]{:S(2)}, u32[]{:S(2)}) async-start(bf16[128,8,1024]{2,0,1:T(8,128)(2,1)} %pad_maximum_fusion), calls=%async_computation | async-start | bytes 4194304 | tf_op jit(solution)/shard_map/all_to_all | solution.py:273
  24.9 38.0 %collective-permute-start.1 = (bf16[1024,256]{1,0:T(8,128)(2,1)}, bf16[1024,256]{1,0:T(8,128)(2,1)}, u32[]{:S(2)}, u32[]{:S(2)}) collective-permute-start(bf16[1024,256]{1,0:T(8,128)(2,1)} %constant_dynamic-update-slice_fusion), channel_id=1, source_target_pairs={{0,8},{8,16},{16,24},{24,32},{32,40},{40,48},{48,56},{56,64},{64,7... | collective-permute-start | bytes 1572872 | tf_op jit(solution)/shard_map/ppermute | solution.py:238
  28.4 34.5 %collective-permute-start = (bf16[384,256]{1,0:T(8,128)(2,1)}, bf16[384,256]{1,0:T(8,128)(2,1)S(1)}, u32[]{:S(2)}, u32[]{:S(2)}) collective-permute-start(bf16[384,256]{1,0:T(8,128)(2,1)} %slice.162), channel_id=1, source_target_pairs={{0,16},{8,24},{16,32},{24,40},{32,48},{40,56},{48,64},{56,72},{64,... | collective-permute-start | bytes 589832 | tf_op jit(solution)/shard_map/ppermute | solution.py:238
  35.5 2.4 copy-start.1
  58.0 57.4 %all-to-all-start.2 = ((bf16[128,8,1024]{2,0,1:T(8,128)(2,1)}), bf16[128,8,1024]{2,0,1:T(8,128)(2,1)}, u32[]{:S(2)}, u32[]{:S(2)}) async-start(bf16[128,8,1024]{2,0,1:T(8,128)(2,1)} %pad_maximum_fusion.2), calls=%async_computation.2 | async-start | bytes 4194304 | tf_op jit(solution)/shard_map/all_to_all | solution.py:273
  115.4 64.9 %all-to-all-start.1 = ((bf16[16,128,1024]{2,1,0:T(8,128)(2,1)}), bf16[16,128,1024]{2,1,0:T(8,128)(2,1)}, u32[]{:S(2)}, u32[]{:S(2)}) async-start(bf16[16,128,1024]{2,1,0:T(8,128)(2,1)} %copy.29), calls=%async_computation.1 | async-start | bytes 8388608 | tf_op jit(solution)/shard_map/all_to_all | solution.py:284
  172.6 13.4 %copy-start.3 = (f32[2432,128]{1,0:T(8,128)S(1)}, f32[2432,128]{1,0:T(8,128)}, u32[]{:S(2)}) copy-start(f32[2432,128]{1,0:T(8,128)} %get-tuple-element.28) | copy-start | bytes 3735556
  180.3 91.9 %all-to-all-start.3 = ((bf16[16,128,1024]{2,1,0:T(8,128)(2,1)}), bf16[16,128,1024]{2,1,0:T(8,128)(2,1)}, u32[]{:S(2)}, u32[]{:S(2)}) async-start(bf16[16,128,1024]{2,1,0:T(8,128)(2,1)} %copy.35), calls=%async_computation.3 | async-start | bytes 8388608 | tf_op jit(solution)/shard_map/all_to_all | solution.py:284
  186.0 1.7 copy-start.2
  186.0 2.0 copy-start.4
  188.3 58.9 %collective-permute-start.2 = (f32[1024,256]{1,0:T(8,128)S(1)}, f32[1024,256]{1,0:T(8,128)}, u32[]{:S(2)}, u32[]{:S(2)}) collective-permute-start(f32[1024,256]{1,0:T(8,128)S(1)} %fusion.12), channel_id=1, source_target_pairs={{8,0},{16,8},{24,16},{32,24},{40,32},{48,40},{56,48},{64,56},{72,6... | collective-permute-start | bytes 3145736 | tf_op jit(solution)/shard_map/ppermute | solution.py:243
  191.4 74.1 %collective-permute-start.3 = (f32[384,256]{1,0:T(8,128)}, f32[384,256]{1,0:T(8,128)}, u32[]{:S(2)}, u32[]{:S(2)}) collective-permute-start(f32[384,256]{1,0:T(8,128)} %pad_maximum_fusion.7), channel_id=1, source_target_pairs={{16,0},{24,8},{32,16},{40,24},{48,32},{56,40},{64,48},{72,56},{80,... | collective-permute-start | bytes 1179656 | tf_op jit(solution)/shard_map/ppermute | solution.py:243
  248.5 19.0 %copy-start.7 = (pred[16]{0:T(512)(128)(4,1)S(1)}, pred[16]{0:T(512)(128)(4,1)}, u32[]{:S(2)}) copy-start(pred[16]{0:T(512)(128)(4,1)} %broadcast_compare_fusion) | copy-start | bytes 52

commit v5 on v4

--- a/solution.py
+++ b/solution.py
@@ -16,16 +16,13 @@
 def routing(block_owner, ctx_count, ctx_rank, blocks_here):
     owner_grid = block_owner.reshape(ctx_count, blocks_here)
     own_targets = lax.dynamic_index_in_dim(owner_grid, ctx_rank, 0, keepdims=False)
-    targets = jnp.arange(ctx_count, dtype=jnp.int32)
-    send_pick = (own_targets[None, :] == targets[:, None]).astype(jnp.bfloat16)
-    arrivals = (owner_grid == ctx_rank).astype(jnp.int32)
-    present = jnp.sum(arrivals, axis=1)
+    sources = jnp.arange(ctx_count, dtype=jnp.int32)
+    present = jnp.sum((owner_grid == ctx_rank).astype(jnp.int32), axis=1)
     arrival_rank = jnp.cumsum(present) - 1
     slot_index = jnp.arange(blocks_here, dtype=jnp.int32)
     chosen = (present[None, :] == 1) & (arrival_rank[None, :] == slot_index[:, None])
-    source_block = targets * blocks_here + jnp.sum(arrivals * slot_index[None, :], axis=1)
-    held_ids = jnp.sum(chosen.astype(jnp.int32) * source_block[None, :], axis=1)
-    return (send_pick, chosen.astype(jnp.bfloat16), held_ids)
+    held_sources = jnp.sum(chosen.astype(jnp.int32) * sources[None, :], axis=1)
+    return (own_targets, held_sources)
 
 
 def select_rows(selector, blocks):
@@ -153,11 +150,12 @@
 TRANS_A = (((0,), (0,)), ((), ()))
 
 
-def fused_kernel(qdoc_ref, kdoc_ref, q_ref, do_ref, k_ref, v_ref, out_ref, dq_ref, dk_ref, dv_ref):
+def fused_kernel(slot_ref, qdoc_ref, kdoc_ref, q_ref, do_ref, k_ref, v_ref, res_ref, dk_ref, dv_ref):
     block = pl.program_id(0)
     window_rows = BAND * BLOCK
     scale = HEAD_DIM ** (-0.5)
-    heads_here = q_ref.shape[2] // HEAD_DIM
+    width = q_ref.shape[2]
+    heads_here = width // HEAD_DIM
 
     @pl.when(block == 0)
     def _():
@@ -183,13 +181,15 @@
         weights = jnp.exp(scores - log_total)
         soft_low = weights.astype(jnp.bfloat16)
         out = jnp.dot(soft_low, value_window, preferred_element_type=jnp.float32).astype(jnp.bfloat16)
-        out_ref[0, :, cols_of] = out
+        res_ref[0, :, cols_of] = out
         grad = do_ref[0, :, cols_of]
         row_dot = jnp.sum(grad.astype(jnp.float32) * out.astype(jnp.float32), axis=1, keepdims=True)
         prob_grad = lax.dot_general(grad, value_window, TRANS_B, preferred_element_type=jnp.float32)
         score_grad = (weights * (prob_grad - row_dot)).astype(jnp.bfloat16)
         dq = jnp.dot(score_grad, key_window, preferred_element_type=jnp.float32) * scale
-        dq_ref[0, :, cols_of] = dq.astype(jnp.bfloat16)
+        res_ref[0, :, width + head * HEAD_DIM : width + (head + 1) * HEAD_DIM] = dq.astype(
+            jnp.bfloat16
+        )
         dk = lax.dot_general(score_grad, query, TRANS_A, preferred_element_type=jnp.float32) * scale
         dv = lax.dot_general(soft_low, grad, TRANS_A, preferred_element_type=jnp.float32)
         if dk_sum is None:
@@ -200,7 +200,7 @@
     dv_ref[pl.ds(start, window_rows), :] += dv_sum
 
 
-def fused_attention(query_blocks, grad_blocks, halo_key, halo_value, halo_doc):
+def fused_attention(slots, query_blocks, grad_blocks, halo_key, halo_value, halo_doc, slot_count):
     blocks, _, width = query_blocks.shape
     window_rows = BAND * BLOCK
     reach = (BAND - 1) * BLOCK
@@ -209,28 +209,35 @@
     key_doc = jnp.stack(
         [halo_doc[b * BLOCK : b * BLOCK + window_rows] for b in range(blocks)]
     ).reshape(blocks, 1, window_rows)
-    block_spec = pl.BlockSpec((1, BLOCK, width), lambda b: (b, 0, 0))
-    whole = pl.BlockSpec((halo_rows, HEAD_DIM), lambda b: (0, 0))
-    return pl.pallas_call(
-        fused_kernel,
+    block_spec = pl.BlockSpec((1, BLOCK, width), lambda b, slot: (b, 0, 0))
+    whole = pl.BlockSpec((halo_rows, HEAD_DIM), lambda b, slot: (0, 0))
+    grid_spec = pltpu.PrefetchScalarGridSpec(
+        num_scalar_prefetch=1,
         grid=(blocks,),
         in_specs=[
-            pl.BlockSpec((1, BLOCK, 1), lambda b: (b, 0, 0)),
-            pl.BlockSpec((1, 1, window_rows), lambda b: (b, 0, 0)),
+            pl.BlockSpec((1, BLOCK, 1), lambda b, slot: (b, 0, 0)),
+            pl.BlockSpec((1, 1, window_rows), lambda b, slot: (b, 0, 0)),
             block_spec,
             block_spec,
             whole,
             whole,
         ],
-        out_specs=[block_spec, block_spec, whole, whole],
+        out_specs=[
+            pl.BlockSpec((1, BLOCK, 2 * width), lambda b, slot: (slot[b], 0, 0)),
+            whole,
+            whole,
+        ],
+    )
+    return pl.pallas_call(
+        fused_kernel,
+        grid_spec=grid_spec,
         out_shape=[
-            jax.ShapeDtypeStruct(query_blocks.shape, jnp.bfloat16),
-            jax.ShapeDtypeStruct(query_blocks.shape, jnp.bfloat16),
+            jax.ShapeDtypeStruct((slot_count, BLOCK, 2 * width), jnp.bfloat16),
             jax.ShapeDtypeStruct((halo_rows, HEAD_DIM), jnp.float32),
             jax.ShapeDtypeStruct((halo_rows, HEAD_DIM), jnp.float32),
         ],
         compiler_params=pltpu.CompilerParams(dimension_semantics=("arbitrary",)),
-    )(query_doc, key_doc, query_blocks, grad_blocks, halo_key, halo_value)
+    )(slots, query_doc, key_doc, query_blocks, grad_blocks, halo_key, halo_value)
 
 
 def shift_from_below(x, ctx_count, distance):
@@ -255,7 +262,7 @@
     blocks_here = tok_dev // BLOCK
     reach = (BAND - 1) * BLOCK
     far = reach - tok_dev
-    send_pick, recv_pick, _ = routing(block_owner, ctx_count, ctx_rank, blocks_here)
+    own_targets, held_sources = routing(block_owner, ctx_count, ctx_rank, blocks_here)
     kv_here = jnp.concatenate([key_rows, value_rows], axis=1)
     kv_near = shift_from_below(kv_here, ctx_count, 1)
     kv_far = shift_from_below(kv_here[tok_dev - far :], ctx_count, 2)
@@ -272,19 +279,22 @@
         both = jnp.concatenate([query_parts[:, :, chunk], grad_parts[:, :, chunk]], axis=-1)
         both = lax.all_to_all(both, "tp", split_axis=1, concat_axis=0, tiled=True)
         both = both.reshape(blocks_here, BLOCK, 2 * chunk_cols)
-        out_blocks, dq_blocks, chunk_key_grad, chunk_value_grad = fused_attention(
-            both[..., :chunk_cols], both[..., chunk_cols:], halo_key, halo_value, halo_doc
+        results, chunk_key_grad, chunk_value_grad = fused_attention(
+            own_targets,
+            both[..., :chunk_cols],
+            both[..., chunk_cols:],
+            halo_key,
+            halo_value,
+            halo_doc,
+            ctx_count,
         )
         if key_grad is None:
             key_grad, value_grad = chunk_key_grad, chunk_value_grad
         else:
             key_grad = key_grad + chunk_key_grad
             value_grad = value_grad + chunk_value_grad
-        results = jnp.concatenate([out_blocks, dq_blocks], axis=-1)
-        sent = lax.all_to_all(
-            select_rows(send_pick, results), "ctx", split_axis=0, concat_axis=0, tiled=True
-        )
-        held_parts.append(select_rows(recv_pick, sent))
+        sent = lax.all_to_all(results, "ctx", split_axis=0, concat_axis=0, tiled=True)
+        held_parts.append(jnp.take(sent, held_sources, axis=0))
     kv_grad = jnp.concatenate([key_grad, value_grad], axis=1)
     grad_near = shift_to_below(kv_grad[far:reach], ctx_count, 1)
     grad_far = shift_to_below(kv_grad[:far], ctx_count, 2)

time: 284 us -> 295 us (1.039)
  waiting for transfers between devices: 93.5 us -> 122 us
  matrix products: 12.8 us -> 0 us
  local copies, waits for them, and re-layouts: 43.8 us -> 36.9 us
    ppermute x2, waiting for transfers between devices: 0.01 us -> 16.6 us  [shift_from_below(): return lax.ppermute(x, 'ctx', pairs)]
    dot_general x4 -> x0, matrix products: 12.8 us -> none  [select_rows(): jnp.einsum('ab,brh->arh', selector, blocks, preferred_element_type=jnp.fl...]
    convert_element_type x2 -> x0, local copies, waits for them, and re-layouts: 8.64 us -> none  [select_rows(): return picked.astype(jnp.bfloat16)]
    all_to_all x2, waiting for transfers between devices: 7.69 us -> 14.9 us  [on_device(): lax.all_to_all(results, 'ctx', split_axis=0, concat_axis=0, tiled=True)]
    gather x0 -> x2, local copies, waits for them, and re-layouts: none -> 7.05 us  [on_device(): held_parts.append(jnp.take(sent, held_sources, axis=0))]
    concatenate x2 -> x0, local copies, waits for them, and re-layouts: 4.95 us -> none  [the longest x1 2.48 us: on_device(): jnp.concatenate([part[..., :chunk_cols] for part in held_parts], axis=-1)]
    all_to_all x2, waiting for transfers between devices: 17.4 us -> 21.3 us  [on_device(): both = lax.all_to_all(both, 'tp', split_axis=1, concat_axis=0, tiled=True)]
    unnamed x25 -> x19, local copies, waits for them, and re-layouts: 15.2 us -> 14.8 us
  transfers between devices with their start and end apart: 8 -> 8, of which waited for: 4 -> 5; matrix products, arithmetic and copies ran while one was open for 17% -> 9% of each run, Pallas kernels for 29% -> 28%
where the time goes in v5:
time: 295 us; the launch traced here: 293 us
  waiting for transfers between devices  122 us (41%)
  Pallas kernels  82.5 us (28%)
  local copies, waits for them, and re-layouts  36.9 us (13%)
  starting transfers between devices  35 us (12%)
  other arithmetic  15.1 us (5%)
    pallas_call x2, Pallas kernels, fused_attention(): pl.pallas_call(fused_kernel, grid_spec=grid_spec, out_shape=[jax.ShapeDty...  82.5 us
    ppermute x2, waiting for transfers between devices, shift_to_below(): return lax.ppermute(x, 'ctx', pairs)  69.6 us
    all_to_all x2, waiting for transfers between devices, on_device(): both = lax.all_to_all(both, 'tp', split_axis=1, concat_axis=0, tiled=True)  21.3 us
    ppermute x2, waiting for transfers between devices, shift_from_below(): return lax.ppermute(x, 'ctx', pairs)  16.6 us
    all_to_all x2, waiting for transfers between devices, on_device(): lax.all_to_all(results, 'ctx', split_axis=0, concat_axis=0, tiled=True)  14.9 us
    unnamed x19, local copies, waits for them, and re-layouts  14.8 us
    all_to_all x2, starting transfers between devices, on_device(): both = lax.all_to_all(both, 'tp', split_axis=1, concat_axis=0, tiled=True)  14.2 us
    all_to_all x2, starting transfers between devices, on_device(): lax.all_to_all(results, 'ctx', split_axis=0, concat_axis=0, tiled=True)  11.5 us
  transfers between devices with their start and end apart: 8, of which 5 were waited for; matrix products, arithmetic and copies ran while one was open for 9% of the time, Pallas kernels for 28%

profile of v5, /device:TPU:60, one launch (start us, length us, event | category | flops | bytes accessed | tf_op | source)
XLA Modules:
  0.0 292.8 jit_solution(3917109709264970204)
XLA Ops:
  0.6 3.2 %copy.21 = bf16[128,8192]{0,1:T(8,128)(2,1)S(1)} copy(bf16[128,8192]{1,0:T(8,128)(2,1)} %param.10) | data formatting | bytes 4194304 | tf_op args[0]
  5.0 2.3 copy.31
  7.3 3.2 %copy.23 = bf16[128,8192]{0,1:T(8,128)(2,1)S(1)} copy(bf16[128,8192]{1,0:T(8,128)(2,1)} %param.13) | data formatting | bytes 4194304 | tf_op args[3]
  10.5 1.5 fusion.10
  12.0 1.6 copy.32
  13.6 1.6 pad_maximum_fusion.1
  15.2 7.2 %all-to-all-start.2 = ((bf16[128,8,1024]{2,0,1:T(8,128)(2,1)}), bf16[128,8,1024]{2,0,1:T(8,128)(2,1)S(1)}, u32[]{:S(2)}, u32[]{:S(2)}) async-start(bf16[128,8,1024]{2,0,1:T(8,128)(2,1)} %pad_maximum_fusion.1), calls=%async_computation.2 | async-start | bytes 4194304 | tf_op jit(solution)/shard_map/all_to_all | solution.py:280
  23.2 1.7 constant_dynamic-update-slice_fusion
  24.9 1.9 collective-permute-start.1
  28.2 2.4 copy.30
  30.5 2.8 pad_maximum_fusion
  33.3 21.3 %all-to-all-done.2 = bf16[128,8,1024]{2,0,1:T(8,128)(2,1)S(1)} async-done(((bf16[128,8,1024]{2,0,1:T(8,128)(2,1)}), bf16[128,8,1024]{2,0,1:T(8,128)(2,1)S(1)}, u32[]{:S(2)}, u32[]{:S(2)}) %all-to-all-start.2) | async-done | bytes 2097184 | tf_op jit(solution)/shard_map/all_to_all | solution.py:280
  54.6 6.9 %all-to-all-start = ((bf16[128,8,1024]{2,0,1:T(8,128)(2,1)}), bf16[128,8,1024]{2,0,1:T(8,128)(2,1)}, u32[]{:S(2)}, u32[]{:S(2)}) async-start(bf16[128,8,1024]{2,0,1:T(8,128)(2,1)} %pad_maximum_fusion), calls=%async_computation | async-start | bytes 4194304 | tf_op jit(solution)/shard_map/all_to_all | solution.py:280
  62.5 1.9 collective-permute-start
  67.2 16.5 %collective-permute-done = bf16[384,256]{1,0:T(8,128)(2,1)S(1)} collective-permute-done((bf16[384,256]{1,0:T(8,128)(2,1)S(1)}, bf16[384,256]{1,0:T(8,128)(2,1)S(1)}, u32[]{:S(2)}, u32[]{:S(2)}) %collective-permute-start) | collective-permute-done | bytes 196640 | tf_op jit(solution)/shard_map/ppermute | solution.py:245
  86.2 1.6 fusion.11
  87.7 41.3 %shard_map.94 = (bf16[16,128,1024]{2,1,0:T(8,128)(2,1)}, f32[2432,128]{1,0:T(8,128)}, f32[2432,128]{1,0:T(8,128)}) custom-call(s32[8]{0:T(128)} %dynamic-slice_bitcast_fusion.slot_ref, s32[8,128,1]{2,1,0:T(8,128)} %copy.25.qdoc_ref, s32[8,1,1536]{2,1,0:T(1,128)} %reshape.108.kdoc_ref, bf16[8,128,512]{2,1,0:T(8,128)(2,1)} %get-tuple-element.40.q_ref, ...), custom_call_target="tpu_custom_call" | custom-call | tf_op jit(solution)/shard_map/pallas_call | solution.py:231
  129.0 5.7 %all-to-all-start.3 = ((bf16[16,128,1024]{2,1,0:T(8,128)(2,1)}), bf16[16,128,1024]{2,1,0:T(8,128)(2,1)}, u32[]{:S(2)}, u32[]{:S(2)}) async-start(bf16[16,128,1024]{2,1,0:T(8,128)(2,1)} %get-tuple-element.24), calls=%async_computation.3 | async-start | bytes 8388608 | tf_op jit(solution)/shard_map/all_to_all | solution.py:296
  134.8 3.0 %fusion.8 = (bf16[8,128,512]{2,1,0:T(8,128)(2,1)}, bf16[8,128,512]{2,1,0:T(8,128)(2,1)}) fusion(bf16[8,128,1024]{2,1,0:T(8,128)(2,1)} %bitcast.9), kind=kLoop, calls=%fused_computation.43 | loop fusion | bytes 4194304 | tf_op jit(solution)/shard_map/slice | solution.py:285
  137.8 41.2 %shard_map.93 = (bf16[16,128,1024]{2,1,0:T(8,128)(2,1)}, f32[2432,128]{1,0:T(8,128)}, f32[2432,128]{1,0:T(8,128)}) custom-call(s32[8]{0:T(128)} %dynamic-slice_bitcast_fusion.slot_ref, s32[8,128,1]{2,1,0:T(8,128)} %copy.25.qdoc_ref, s32[8,1,1536]{2,1,0:T(1,128)} %reshape.108.kdoc_ref, bf16[8,128,512]{2,1,0:T(8,128)(2,1)} %get-tuple-element.34.q_ref, ...), custom_call_target="tpu_custom_call" | custom-call | tf_op jit(solution)/shard_map/pallas_call | solution.py:231
  179.0 14.9 %all-to-all-done.3 = bf16[16,128,1024]{2,1,0:T(8,128)(2,1)} async-done(((bf16[16,128,1024]{2,1,0:T(8,128)(2,1)}), bf16[16,128,1024]{2,1,0:T(8,128)(2,1)}, u32[]{:S(2)}, u32[]{:S(2)}) %all-to-all-start.3) | async-done | bytes 4194336 | tf_op jit(solution)/shard_map/all_to_all | solution.py:296
  194.0 5.7 %all-to-all-start.1 = ((bf16[16,128,1024]{2,1,0:T(8,128)(2,1)}), bf16[16,128,1024]{2,1,0:T(8,128)(2,1)}, u32[]{:S(2)}, u32[]{:S(2)}) async-start(bf16[16,128,1024]{2,1,0:T(8,128)(2,1)} %get-tuple-element.23), calls=%async_computation.1 | async-start | bytes 8388608 | tf_op jit(solution)/shard_map/all_to_all | solution.py:296
  199.9 1.9 add.37
  203.4 2.2 collective-permute-start.2
  205.9 3.4 %collective-permute-start.3 = (f32[384,256]{1,0:T(8,128)S(1)}, f32[384,256]{1,0:T(8,128)S(1)}, u32[]{:S(2)}, u32[]{:S(2)}) collective-permute-start(f32[384,256]{1,0:T(8,128)S(1)} %pad_maximum_fusion.5), channel_id=1, source_target_pairs={{16,0},{24,8},{32,16},{40,24},{48,32},{56,40},{64,48},{72,56},{80,... | collective-permute-start | bytes 1179656 | tf_op jit(solution)/shard_map/ppermute | solution.py:250
  209.3 51.5 %collective-permute-done.2 = f32[1024,256]{1,0:T(8,128)S(1)} collective-permute-done((f32[1024,256]{1,0:T(8,128)S(1)}, f32[1024,256]{1,0:T(8,128)S(1)}, u32[]{:S(2)}, u32[]{:S(2)}) %collective-permute-start.2) | collective-permute-done | bytes 1048608 | tf_op jit(solution)/shard_map/ppermute | solution.py:250
  260.9 18.1 %collective-permute-done.3 = f32[384,256]{1,0:T(8,128)S(1)} collective-permute-done((f32[384,256]{1,0:T(8,128)S(1)}, f32[384,256]{1,0:T(8,128)S(1)}, u32[]{:S(2)}, u32[]{:S(2)}) %collective-permute-start.3) | collective-permute-done | bytes 393248 | tf_op jit(solution)/shard_map/ppermute | solution.py:250
  280.0 2.9 gather_fusion.1
  282.9 4.2 %gather_fusion = bf16[8,128,1024]{2,1,0:T(8,128)(2,1)} fusion(bf16[16,128,1024]{2,1,0:T(8,128)(2,1)} %all-to-all-done.1, s32[1024]{0:T(1024)S(1)} %pad_clamp_fusion), kind=kCustom, calls=%fused_computation.clone | custom fusion | bytes 4194336 | tf_op jit(solution)/shard_map/jit(_take)/gather | solution.py:297
  287.0 2.0 broadcast_select_fusion.1
  289.6 1.6 pad_maximum_fusion.3
  291.2 1.6 pad_maximum_fusion.2
  (53 shorter events, 12.9 us)
Async XLA Ops:
  12.0 1.6 copy-start
  15.2 7.2 %copy-start.3 = (bf16[1024,128]{1,0:T(8,128)(2,1)S(1)}, bf16[1024,128]{1,0:T(8,128)(2,1)}, u32[]{:S(2)}) copy-start(bf16[1024,128]{1,0:T(8,128)(2,1)} %param.11) | copy-start | bytes 786436
  15.2 39.4 %all-to-all-start.2 = ((bf16[128,8,1024]{2,0,1:T(8,128)(2,1)}), bf16[128,8,1024]{2,0,1:T(8,128)(2,1)S(1)}, u32[]{:S(2)}, u32[]{:S(2)}) async-start(bf16[128,8,1024]{2,0,1:T(8,128)(2,1)} %pad_maximum_fusion.1), calls=%async_computation.2 | async-start | bytes 4194304 | tf_op jit(solution)/shard_map/all_to_all | solution.py:280
  24.9 58.9 %collective-permute-start.1 = (bf16[1024,256]{1,0:T(8,128)(2,1)}, bf16[1024,256]{1,0:T(8,128)(2,1)}, u32[]{:S(2)}, u32[]{:S(2)}) collective-permute-start(bf16[1024,256]{1,0:T(8,128)(2,1)} %constant_dynamic-update-slice_fusion), channel_id=1, source_target_pairs={{0,8},{8,16},{16,24},{24,32},{32,40},{40,48},{48,56},{56,64},{64,7... | collective-permute-start | bytes 1572872 | tf_op jit(solution)/shard_map/ppermute | solution.py:245
  28.2 2.4 copy-start.1
  33.3 31.1 %copy-start.5 = (s32[128]{0:T(128)S(1)}, s32[128]{0:T(128)}, u32[]{:S(2)}) copy-start(s32[128]{0:T(128)} %param.15) | copy-start | bytes 1540
  33.3 31.2 %copy-start.4 = (s32[16384]{0:T(1024)S(1)}, s32[16384]{0:T(1024)}, u32[]{:S(2)}) copy-start(s32[16384]{0:T(1024)} %param.14) | copy-start | bytes 196612
  54.6 74.4 %all-to-all-start = ((bf16[128,8,1024]{2,0,1:T(8,128)(2,1)}), bf16[128,8,1024]{2,0,1:T(8,128)(2,1)}, u32[]{:S(2)}, u32[]{:S(2)}) async-start(bf16[128,8,1024]{2,0,1:T(8,128)(2,1)} %pad_maximum_fusion), calls=%async_computation | async-start | bytes 4194304 | tf_op jit(solution)/shard_map/all_to_all | solution.py:280
  62.5 21.2 %collective-permute-start = (bf16[384,256]{1,0:T(8,128)(2,1)S(1)}, bf16[384,256]{1,0:T(8,128)(2,1)S(1)}, u32[]{:S(2)}, u32[]{:S(2)}) collective-permute-start(bf16[384,256]{1,0:T(8,128)(2,1)S(1)} %slice.166), channel_id=1, source_target_pairs={{0,16},{8,24},{16,32},{24,40},{32,48},{40,56},{48,64},{56,72},{64,... | collective-permute-start | bytes 589832 | tf_op jit(solution)/shard_map/ppermute | solution.py:245
  129.0 64.9 %all-to-all-start.3 = ((bf16[16,128,1024]{2,1,0:T(8,128)(2,1)}), bf16[16,128,1024]{2,1,0:T(8,128)(2,1)}, u32[]{:S(2)}, u32[]{:S(2)}) async-start(bf16[16,128,1024]{2,1,0:T(8,128)(2,1)} %get-tuple-element.24), calls=%async_computation.3 | async-start | bytes 8388608 | tf_op jit(solution)/shard_map/all_to_all | solution.py:296
  194.0 88.9 %all-to-all-start.1 = ((bf16[16,128,1024]{2,1,0:T(8,128)(2,1)}), bf16[16,128,1024]{2,1,0:T(8,128)(2,1)}, u32[]{:S(2)}, u32[]{:S(2)}) async-start(bf16[16,128,1024]{2,1,0:T(8,128)(2,1)} %get-tuple-element.23), calls=%async_computation.1 | async-start | bytes 8388608 | tf_op jit(solution)/shard_map/all_to_all | solution.py:296
  199.7 2.2 copy-start.2
  203.4 57.4 %collective-permute-start.2 = (f32[1024,256]{1,0:T(8,128)S(1)}, f32[1024,256]{1,0:T(8,128)S(1)}, u32[]{:S(2)}, u32[]{:S(2)}) collective-permute-start(f32[1024,256]{1,0:T(8,128)S(1)} %fusion), channel_id=1, source_target_pairs={{8,0},{16,8},{24,16},{32,24},{40,32},{48,40},{56,48},{64,56},{72,6... | collective-permute-start | bytes 3145736 | tf_op jit(solution)/shard_map/ppermute | solution.py:250
  205.9 73.1 %collective-permute-start.3 = (f32[384,256]{1,0:T(8,128)S(1)}, f32[384,256]{1,0:T(8,128)S(1)}, u32[]{:S(2)}, u32[]{:S(2)}) collective-permute-start(f32[384,256]{1,0:T(8,128)S(1)} %pad_maximum_fusion.5), channel_id=1, source_target_pairs={{16,0},{24,8},{32,16},{40,24},{48,32},{56,40},{64,48},{72,56},{80,... | collective-permute-start | bytes 1179656 | tf_op jit(solution)/shard_map/ppermute | solution.py:250

commit v6 on v5

--- a/solution.py
+++ b/solution.py
@@ -277,6 +277,8 @@
     key_grad = None
     for chunk in range(CHUNKS):
         both = jnp.concatenate([query_parts[:, :, chunk], grad_parts[:, :, chunk]], axis=-1)
+        if chunk > 0:
+            both, _ = lax.optimization_barrier((both, halo))
         both = lax.all_to_all(both, "tp", split_axis=1, concat_axis=0, tiled=True)
         both = both.reshape(blocks_here, BLOCK, 2 * chunk_cols)
         results, chunk_key_grad, chunk_value_grad = fused_attention(

time: 295 us -> 275 us (0.932)
  waiting for transfers between devices: 122 us -> 105 us
    all_to_all x2, waiting for transfers between devices: 21.3 us -> 2.93 us  [on_device(): both = lax.all_to_all(both, 'tp', split_axis=1, concat_axis=0, tiled=True)]
    unnamed x19 -> x23, local copies, waits for them, and re-layouts: 14.8 us -> 15 us
  transfers between devices with their start and end apart: 8 -> 8, of which waited for: 5 -> 6; matrix products, arithmetic and copies ran while one was open for 9% -> 9% of each run, Pallas kernels for 28% -> 30%
where the time goes in v6:
time: 275 us; the launch traced here: 274 us
  waiting for transfers between devices  105 us (38%)
  Pallas kernels  82.5 us (30%)
  local copies, waits for them, and re-layouts  37.1 us (13%)
  starting transfers between devices  35 us (13%)
  other arithmetic  13.3 us (5%)
    pallas_call x2, Pallas kernels, fused_attention(): pl.pallas_call(fused_kernel, grid_spec=grid_spec, out_shape=[jax.ShapeDty...  82.5 us
    ppermute x2, waiting for transfers between devices, shift_to_below(): return lax.ppermute(x, 'ctx', pairs)  71 us
    ppermute x2, waiting for transfers between devices, shift_from_below(): return lax.ppermute(x, 'ctx', pairs)  16 us
    unnamed x23, local copies, waits for them, and re-layouts  15 us
    all_to_all x2, waiting for transfers between devices, on_device(): lax.all_to_all(results, 'ctx', split_axis=0, concat_axis=0, tiled=True)  14.9 us
    all_to_all x2, starting transfers between devices, on_device(): both = lax.all_to_all(both, 'tp', split_axis=1, concat_axis=0, tiled=True)  12.1 us
    all_to_all x2, starting transfers between devices, on_device(): lax.all_to_all(results, 'ctx', split_axis=0, concat_axis=0, tiled=True)  11.9 us
    gather x2, local copies, waits for them, and re-layouts, on_device(): held_parts.append(jnp.take(sent, held_sources, axis=0))  7.05 us
  transfers between devices with their start and end apart: 8, of which 6 were waited for; matrix products, arithmetic and copies ran while one was open for 9% of the time, Pallas kernels for 30%

profile of v6, /device:TPU:60, one launch (start us, length us, event | category | flops | bytes accessed | tf_op | source)
XLA Modules:
  0.0 273.7 jit_solution(17456979238304345064)
XLA Ops:
  0.6 3.2 %copy.21 = bf16[128,8192]{0,1:T(8,128)(2,1)S(1)} copy(bf16[128,8192]{1,0:T(8,128)(2,1)} %param.10) | data formatting | bytes 4194304 | tf_op args[0]
  5.0 2.3 copy.29
  7.3 3.2 %copy.23 = bf16[128,8192]{0,1:T(8,128)(2,1)S(1)} copy(bf16[128,8192]{1,0:T(8,128)(2,1)} %param.13) | data formatting | bytes 4194304 | tf_op args[3]
  12.0 1.6 copy.30
  13.5 1.6 pad_maximum_fusion
  15.2 7.2 %all-to-all-start = ((bf16[128,8,1024]{2,0,1:T(8,128)(2,1)}), bf16[128,8,1024]{2,0,1:T(8,128)(2,1)S(1)}, u32[]{:S(2)}, u32[]{:S(2)}) async-start(bf16[128,8,1024]{2,0,1:T(8,128)(2,1)} %pad_maximum_fusion), calls=%async_computation | async-start | bytes 4194304 | tf_op jit(solution)/shard_map/all_to_all | solution.py:282
  23.1 1.7 constant_dynamic-update-slice_fusion
  24.8 1.9 collective-permute-start.1
  27.7 3.5 %collective-permute-start = (bf16[384,256]{1,0:T(8,128)(2,1)S(1)}, bf16[384,256]{1,0:T(8,128)(2,1)S(1)}, u32[]{:S(2)}, u32[]{:S(2)}) collective-permute-start(bf16[384,256]{1,0:T(8,128)(2,1)S(1)} %slice.166), channel_id=1, source_target_pairs={{0,16},{8,24},{16,32},{24,40},{32,48},{40,56},{48,64},{56,72},{64,... | collective-permute-start | bytes 589832 | tf_op jit(solution)/shard_map/ppermute | solution.py:245
  32.6 2.4 copy.32
  35.0 2.8 %pad_maximum_fusion.1 = bf16[128,8,1024]{2,0,1:T(8,128)(2,1)} fusion(bf16[128,8,512]{2,0,1:T(8,128)(2,1)} %bitcast.29, bf16[128,8,512]{2,0,1:T(8,128)(2,1)S(1)} %bitcast.27), kind=kLoop, calls=%fused_computation.7 | loop fusion | flops 4194304 | bytes 4194304 | tf_op jit(solution)/shard_map/concatenate | solution.py:279
  37.7 12.5 %collective-permute-done = bf16[384,256]{1,0:T(8,128)(2,1)S(1)} collective-permute-done((bf16[384,256]{1,0:T(8,128)(2,1)S(1)}, bf16[384,256]{1,0:T(8,128)(2,1)S(1)}, u32[]{:S(2)}, u32[]{:S(2)}) %collective-permute-start) | collective-permute-done | bytes 196640 | tf_op jit(solution)/shard_map/ppermute | solution.py:245
  50.2 3.5 %collective-permute-done.1 = bf16[1024,256]{1,0:T(8,128)(2,1)} collective-permute-done((bf16[1024,256]{1,0:T(8,128)(2,1)}, bf16[1024,256]{1,0:T(8,128)(2,1)}, u32[]{:S(2)}, u32[]{:S(2)}) %collective-permute-start.1) | collective-permute-done | bytes 524320 | tf_op jit(solution)/shard_map/ppermute | solution.py:245
  55.1 2.9 %all-to-all-done = bf16[128,8,1024]{2,0,1:T(8,128)(2,1)S(1)} async-done(((bf16[128,8,1024]{2,0,1:T(8,128)(2,1)}), bf16[128,8,1024]{2,0,1:T(8,128)(2,1)S(1)}, u32[]{:S(2)}, u32[]{:S(2)}) %all-to-all-start) | async-done | bytes 2097184 | tf_op jit(solution)/shard_map/all_to_all | solution.py:282
  58.0 4.9 %all-to-all-start.2 = ((bf16[128,8,1024]{2,0,1:T(8,128)(2,1)}), bf16[128,8,1024]{2,0,1:T(8,128)(2,1)}, u32[]{:S(2)}, u32[]{:S(2)}) async-start(bf16[128,8,1024]{2,0,1:T(8,128)(2,1)} %pad_maximum_fusion.1), calls=%async_computation.2 | async-start | bytes 4194304 | tf_op jit(solution)/shard_map/all_to_all | solution.py:282
  66.7 1.6 fusion.8
  68.3 41.2 %shard_map.93 = (bf16[16,128,1024]{2,1,0:T(8,128)(2,1)}, f32[2432,128]{1,0:T(8,128)}, f32[2432,128]{1,0:T(8,128)}) custom-call(s32[8]{0:T(128)} %dynamic-slice_bitcast_fusion.slot_ref, s32[8,128,1]{2,1,0:T(8,128)} %copy.25.qdoc_ref, s32[8,1,1536]{2,1,0:T(1,128)} %reshape.108.kdoc_ref, bf16[8,128,512]{2,1,0:T(8,128)(2,1)} %get-tuple-element.36.q_ref, ...), custom_call_target="tpu_custom_call" | custom-call | tf_op jit(solution)/shard_map/pallas_call | solution.py:231
  109.6 6.0 %all-to-all-start.1 = ((bf16[16,128,1024]{2,1,0:T(8,128)(2,1)}), bf16[16,128,1024]{2,1,0:T(8,128)(2,1)}, u32[]{:S(2)}, u32[]{:S(2)}) async-start(bf16[16,128,1024]{2,1,0:T(8,128)(2,1)} %get-tuple-element.24), calls=%async_computation.1 | async-start | bytes 8388608 | tf_op jit(solution)/shard_map/all_to_all | solution.py:298
  115.6 3.0 %fusion.11 = (bf16[8,128,512]{2,1,0:T(8,128)(2,1)}, bf16[8,128,512]{2,1,0:T(8,128)(2,1)}) fusion(bf16[8,128,1024]{2,1,0:T(8,128)(2,1)} %bitcast.16), kind=kLoop, calls=%fused_computation.46 | loop fusion | bytes 4194304 | tf_op jit(solution)/shard_map/slice | solution.py:287
  118.6 41.2 %shard_map.94 = (bf16[16,128,1024]{2,1,0:T(8,128)(2,1)}, f32[2432,128]{1,0:T(8,128)}, f32[2432,128]{1,0:T(8,128)}) custom-call(s32[8]{0:T(128)} %dynamic-slice_bitcast_fusion.slot_ref, s32[8,128,1]{2,1,0:T(8,128)} %copy.25.qdoc_ref, s32[8,1,1536]{2,1,0:T(1,128)} %reshape.108.kdoc_ref, bf16[8,128,512]{2,1,0:T(8,128)(2,1)} %get-tuple-element.42.q_ref, ...), custom_call_target="tpu_custom_call" | custom-call | tf_op jit(solution)/shard_map/pallas_call | solution.py:231
  159.8 14.9 %all-to-all-done.1 = bf16[16,128,1024]{2,1,0:T(8,128)(2,1)} async-done(((bf16[16,128,1024]{2,1,0:T(8,128)(2,1)}), bf16[16,128,1024]{2,1,0:T(8,128)(2,1)}, u32[]{:S(2)}, u32[]{:S(2)}) %all-to-all-start.1) | async-done | bytes 4194336 | tf_op jit(solution)/shard_map/all_to_all | solution.py:298
  174.8 5.9 %all-to-all-start.3 = ((bf16[16,128,1024]{2,1,0:T(8,128)(2,1)}), bf16[16,128,1024]{2,1,0:T(8,128)(2,1)}, u32[]{:S(2)}, u32[]{:S(2)}) async-start(bf16[16,128,1024]{2,1,0:T(8,128)(2,1)} %get-tuple-element.26), calls=%async_computation.3 | async-start | bytes 8388608 | tf_op jit(solution)/shard_map/all_to_all | solution.py:298
  180.9 1.5 add.37
  182.9 2.2 collective-permute-start.2
  185.4 3.4 %collective-permute-start.3 = (f32[384,256]{1,0:T(8,128)S(1)}, f32[384,256]{1,0:T(8,128)S(1)}, u32[]{:S(2)}, u32[]{:S(2)}) collective-permute-start(f32[384,256]{1,0:T(8,128)S(1)} %pad_maximum_fusion.5), channel_id=1, source_target_pairs={{16,0},{24,8},{32,16},{40,24},{48,32},{56,40},{64,48},{72,56},{80,... | collective-permute-start | bytes 1179656 | tf_op jit(solution)/shard_map/ppermute | solution.py:250
  188.8 52.9 %collective-permute-done.2 = f32[1024,256]{1,0:T(8,128)S(1)} collective-permute-done((f32[1024,256]{1,0:T(8,128)S(1)}, f32[1024,256]{1,0:T(8,128)S(1)}, u32[]{:S(2)}, u32[]{:S(2)}) %collective-permute-start.2) | collective-permute-done | bytes 1048608 | tf_op jit(solution)/shard_map/ppermute | solution.py:250
  241.8 18.1 %collective-permute-done.3 = f32[384,256]{1,0:T(8,128)S(1)} collective-permute-done((f32[384,256]{1,0:T(8,128)S(1)}, f32[384,256]{1,0:T(8,128)S(1)}, u32[]{:S(2)}, u32[]{:S(2)}) %collective-permute-start.3) | collective-permute-done | bytes 393248 | tf_op jit(solution)/shard_map/ppermute | solution.py:250
  260.9 2.9 %gather_fusion = bf16[8,128,1024]{2,1,0:T(8,128)(2,1)S(1)} fusion(bf16[16,128,1024]{2,1,0:T(8,128)(2,1)} %all-to-all-done.1, s32[1024]{0:T(1024)S(1)} %pad_clamp_fusion), kind=kCustom, calls=%fused_computation.clone | custom fusion | bytes 4194336 | tf_op jit(solution)/shard_map/jit(_take)/gather | solution.py:299
  263.8 4.2 %gather_fusion.1 = bf16[8,128,1024]{2,1,0:T(8,128)(2,1)} fusion(bf16[16,128,1024]{2,1,0:T(8,128)(2,1)} %all-to-all-done.3, s32[1024]{0:T(1024)S(1)} %pad_clamp_fusion), kind=kCustom, calls=%fused_computation.1.clone | custom fusion | bytes 4194336 | tf_op jit(solution)/shard_map/jit(_take)/gather | solution.py:299
  268.0 2.0 broadcast_select_fusion.1
  270.5 1.6 pad_maximum_fusion.3
  272.0 1.6 pad_maximum_fusion.2
  (57 shorter events, 13.2 us)
Async XLA Ops:
  12.0 1.6 copy-start
  15.2 7.2 %copy-start.5 = (bf16[1024,128]{1,0:T(8,128)(2,1)S(1)}, bf16[1024,128]{1,0:T(8,128)(2,1)}, u32[]{:S(2)}) copy-start(bf16[1024,128]{1,0:T(8,128)(2,1)} %param.11) | copy-start | bytes 786436
  15.2 42.8 %all-to-all-start = ((bf16[128,8,1024]{2,0,1:T(8,128)(2,1)}), bf16[128,8,1024]{2,0,1:T(8,128)(2,1)S(1)}, u32[]{:S(2)}, u32[]{:S(2)}) async-start(bf16[128,8,1024]{2,0,1:T(8,128)(2,1)} %pad_maximum_fusion), calls=%async_computation | async-start | bytes 4194304 | tf_op jit(solution)/shard_map/all_to_all | solution.py:282
  24.8 28.9 %collective-permute-start.1 = (bf16[1024,256]{1,0:T(8,128)(2,1)}, bf16[1024,256]{1,0:T(8,128)(2,1)}, u32[]{:S(2)}, u32[]{:S(2)}) collective-permute-start(bf16[1024,256]{1,0:T(8,128)(2,1)} %constant_dynamic-update-slice_fusion), channel_id=1, source_target_pairs={{0,8},{8,16},{16,24},{24,32},{32,40},{40,48},{48,56},{56,64},{64,7... | collective-permute-start | bytes 1572872 | tf_op jit(solution)/shard_map/ppermute | solution.py:245
  27.7 22.5 %collective-permute-start = (bf16[384,256]{1,0:T(8,128)(2,1)S(1)}, bf16[384,256]{1,0:T(8,128)(2,1)S(1)}, u32[]{:S(2)}, u32[]{:S(2)}) collective-permute-start(bf16[384,256]{1,0:T(8,128)(2,1)S(1)} %slice.166), channel_id=1, source_target_pairs={{0,16},{8,24},{16,32},{24,40},{32,48},{40,56},{48,64},{56,72},{64,... | collective-permute-start | bytes 589832 | tf_op jit(solution)/shard_map/ppermute | solution.py:245
  32.6 2.4 copy-start.1
  55.0 7.8 %copy-start.7 = (s32[128]{0:T(128)S(1)}, s32[128]{0:T(128)}, u32[]{:S(2)}) copy-start(s32[128]{0:T(128)} %param.15) | copy-start | bytes 1540
  55.0 7.9 %copy-start.6 = (s32[16384]{0:T(1024)S(1)}, s32[16384]{0:T(1024)}, u32[]{:S(2)}) copy-start(s32[16384]{0:T(1024)} %param.14) | copy-start | bytes 196612
  58.0 51.6 %all-to-all-start.2 = ((bf16[128,8,1024]{2,0,1:T(8,128)(2,1)}), bf16[128,8,1024]{2,0,1:T(8,128)(2,1)}, u32[]{:S(2)}, u32[]{:S(2)}) async-start(bf16[128,8,1024]{2,0,1:T(8,128)(2,1)} %pad_maximum_fusion.1), calls=%async_computation.2 | async-start | bytes 4194304 | tf_op jit(solution)/shard_map/all_to_all | solution.py:282
  109.6 65.2 %all-to-all-start.1 = ((bf16[16,128,1024]{2,1,0:T(8,128)(2,1)}), bf16[16,128,1024]{2,1,0:T(8,128)(2,1)}, u32[]{:S(2)}, u32[]{:S(2)}) async-start(bf16[16,128,1024]{2,1,0:T(8,128)(2,1)} %get-tuple-element.24), calls=%async_computation.1 | async-start | bytes 8388608 | tf_op jit(solution)/shard_map/all_to_all | solution.py:298
  174.8 6.1 %copy-start.3 = (f32[2432,128]{1,0:T(8,128)S(1)}, f32[2432,128]{1,0:T(8,128)}, u32[]{:S(2)}) copy-start(f32[2432,128]{1,0:T(8,128)} %get-tuple-element.29) | copy-start | bytes 3735556
  174.8 89.0 %all-to-all-start.3 = ((bf16[16,128,1024]{2,1,0:T(8,128)(2,1)}), bf16[16,128,1024]{2,1,0:T(8,128)(2,1)}, u32[]{:S(2)}, u32[]{:S(2)}) async-start(bf16[16,128,1024]{2,1,0:T(8,128)(2,1)} %get-tuple-element.26), calls=%async_computation.3 | async-start | bytes 8388608 | tf_op jit(solution)/shard_map/all_to_all | solution.py:298
  180.6 1.8 copy-start.2
  180.9 1.9 copy-start.4
  182.9 58.8 %collective-permute-start.2 = (f32[1024,256]{1,0:T(8,128)S(1)}, f32[1024,256]{1,0:T(8,128)S(1)}, u32[]{:S(2)}, u32[]{:S(2)}) collective-permute-start(f32[1024,256]{1,0:T(8,128)S(1)} %fusion), channel_id=1, source_target_pairs={{8,0},{16,8},{24,16},{32,24},{40,32},{48,40},{56,48},{64,56},{72,6... | collective-permute-start | bytes 3145736 | tf_op jit(solution)/shard_map/ppermute | solution.py:250
  185.4 74.5 %collective-permute-start.3 = (f32[384,256]{1,0:T(8,128)S(1)}, f32[384,256]{1,0:T(8,128)S(1)}, u32[]{:S(2)}, u32[]{:S(2)}) collective-permute-start(f32[384,256]{1,0:T(8,128)S(1)} %pad_maximum_fusion.5), channel_id=1, source_target_pairs={{16,0},{24,8},{32,16},{40,24},{48,32},{56,40},{64,48},{72,56},{80,... | collective-permute-start | bytes 1179656 | tf_op jit(solution)/shard_map/ppermute | solution.py:250

commit v7 on v6

--- a/solution.py
+++ b/solution.py
@@ -10,7 +10,7 @@
 HEAD_DIM = 128
 BLOCK = 128
 BAND = 12
-CHUNKS = 2
+FIRST_SHARE = 3
 
 
 def routing(block_owner, ctx_count, ctx_rank, blocks_here):
@@ -256,7 +256,8 @@
     ctx_rank = lax.axis_index("ctx")
     local_rows, width = queries.shape
     head_cols = width // tp_count
-    chunk_cols = head_cols // CHUNKS
+    first_cols = (head_cols // HEAD_DIM) * FIRST_SHARE // 8 * HEAD_DIM
+    bounds = [(0, first_cols), (first_cols, head_cols)]
     tok_dev = key_rows.shape[0]
     kv_cols = key_rows.shape[1]
     blocks_here = tok_dev // BLOCK
@@ -271,12 +272,13 @@
     halo_value = halo[:, kv_cols:]
     padded_doc = jnp.concatenate([jnp.full((reach,), -1, doc_ids.dtype), doc_ids])
     halo_doc = lax.dynamic_slice_in_dim(padded_doc, ctx_rank * tok_dev, reach + tok_dev, 0)
-    query_parts = queries.reshape(local_rows, tp_count, CHUNKS, chunk_cols)
-    grad_parts = out_grad.reshape(local_rows, tp_count, CHUNKS, chunk_cols)
+    query_parts = queries.reshape(local_rows, tp_count, head_cols)
+    grad_parts = out_grad.reshape(local_rows, tp_count, head_cols)
     held_parts = []
     key_grad = None
-    for chunk in range(CHUNKS):
-        both = jnp.concatenate([query_parts[:, :, chunk], grad_parts[:, :, chunk]], axis=-1)
+    for chunk, (low, high) in enumerate(bounds):
+        chunk_cols = high - low
+        both = jnp.concatenate([query_parts[:, :, low:high], grad_parts[:, :, low:high]], axis=-1)
         if chunk > 0:
             both, _ = lax.optimization_barrier((both, halo))
         both = lax.all_to_all(both, "tp", split_axis=1, concat_axis=0, tiled=True)
@@ -302,8 +304,9 @@
     grad_far = shift_to_below(kv_grad[:far], ctx_count, 2)
     kv_total = kv_grad[reach:] + grad_near
     kv_total = kv_total.at[tok_dev - far :].add(grad_far)
-    held_out = jnp.concatenate([part[..., :chunk_cols] for part in held_parts], axis=-1)
-    held_dq = jnp.concatenate([part[..., chunk_cols:] for part in held_parts], axis=-1)
+    widths = [high - low for low, high in bounds]
+    held_out = jnp.concatenate([p[..., :w] for p, w in zip(held_parts, widths)], axis=-1)
+    held_dq = jnp.concatenate([p[..., w:] for p, w in zip(held_parts, widths)], axis=-1)
     return (
         held_out.reshape(tok_dev, head_cols),
         held_dq.reshape(tok_dev, head_cols),

time: 275 us -> 276 us (level)
    ppermute x2, waiting for transfers between devices: 71 us -> 92.8 us  [shift_to_below(): return lax.ppermute(x, 'ctx', pairs)]
    all_to_all x2, waiting for transfers between devices: 14.9 us -> 0.01 us  [on_device(): lax.all_to_all(results, 'ctx', split_axis=0, concat_axis=0, tiled=True)]
    ppermute x2, waiting for transfers between devices: 16 us -> 11.8 us  [shift_from_below(): return lax.ppermute(x, 'ctx', pairs)]
    unnamed x23 -> x25, local copies, waits for them, and re-layouts: 15 us -> 13.9 us
    concatenate x4 -> x3, other arithmetic: 7.59 us -> 6.96 us  [the longest x2 4.34 us: on_device(): jnp.concatenate([query_parts[:, :, low:high], grad_parts[:, :, low:high]]...]
  transfers between devices with their start and end apart: 8 -> 8, of which waited for: 6 -> 5; matrix products, arithmetic and copies ran while one was open for 9% -> 10% of each run, Pallas kernels for 30% -> 30%
where the time goes in v7:
time: 276 us; the launch traced here: 275 us
  waiting for transfers between devices  107 us (39%)
  Pallas kernels  82.7 us (30%)
  local copies, waits for them, and re-layouts  36.5 us (13%)
  starting transfers between devices  36 us (13%)
  other arithmetic  12.3 us (4%)
    ppermute x2, waiting for transfers between devices, shift_to_below(): return lax.ppermute(x, 'ctx', pairs)  92.8 us
    pallas_call x2, Pallas kernels, fused_attention(): pl.pallas_call(fused_kernel, grid_spec=grid_spec, out_shape=[jax.ShapeDty...  82.7 us
    unnamed x25, local copies, waits for them, and re-layouts  13.9 us
    all_to_all x2, starting transfers between devices, on_device(): lax.all_to_all(results, 'ctx', split_axis=0, concat_axis=0, tiled=True)  12.8 us
    all_to_all x2, starting transfers between devices, on_device(): both = lax.all_to_all(both, 'tp', split_axis=1, concat_axis=0, tiled=True)  12.3 us
    ppermute x2, waiting for transfers between devices, shift_from_below(): return lax.ppermute(x, 'ctx', pairs)  11.8 us
    gather x2, local copies, waits for them, and re-layouts, on_device(): held_parts.append(jnp.take(sent, held_sources, axis=0))  5.74 us
    ppermute x2, starting transfers between devices, shift_to_below(): return lax.ppermute(x, 'ctx', pairs)  5.56 us
  transfers between devices with their start and end apart: 8, of which 5 were waited for; matrix products, arithmetic and copies ran while one was open for 10% of the time, Pallas kernels for 30%

profile of v7, /device:TPU:60, one launch (start us, length us, event | category | flops | bytes accessed | tf_op | source)
XLA Modules:
  0.0 275.0 jit_solution(9517944744589859761)
XLA Ops:
  0.6 3.2 %copy.21 = bf16[128,8192]{0,1:T(8,128)(2,1)S(1)} copy(bf16[128,8192]{1,0:T(8,128)(2,1)} %param.8) | data formatting | bytes 4194304 | tf_op args[0]
  3.9 1.2 copy.29
  5.1 4.1 %copy.23 = bf16[128,8192]{0,1:T(8,128)(2,1)} copy(bf16[128,8192]{1,0:T(8,128)(2,1)} %param.11) | data formatting | bytes 4194304 | tf_op args[3]
  9.2 1.2 slice.163
  10.4 1.2 copy.30
  11.5 2.6 pad_maximum_fusion.3
  14.2 7.2 %all-to-all-start = ((bf16[128,8,768]{2,0,1:T(8,128)(2,1)}), bf16[128,8,768]{2,0,1:T(8,128)(2,1)}, u32[]{:S(2)}, u32[]{:S(2)}) async-start(bf16[128,8,768]{2,0,1:T(8,128)(2,1)} %pad_maximum_fusion.3), calls=%async_computation | async-start | bytes 3145728 | tf_op jit(solution)/shard_map/all_to_all | solution.py:284
  22.9 1.9 collective-permute-start.1
  24.8 1.6 slice.166
  26.4 3.5 %collective-permute-start = (bf16[384,256]{1,0:T(8,128)(2,1)}, bf16[384,256]{1,0:T(8,128)(2,1)}, u32[]{:S(2)}, u32[]{:S(2)}) collective-permute-start(bf16[384,256]{1,0:T(8,128)(2,1)} %slice.166), channel_id=1, source_target_pairs={{0,16},{8,24},{16,32},{24,40},{32,48},{40,56},{48,64},{56,72},{64,... | collective-permute-start | bytes 589832 | tf_op jit(solution)/shard_map/ppermute | solution.py:245
  31.9 1.7 copy.32
  33.7 1.7 pad_maximum_fusion
  35.4 8.4 %collective-permute-done = bf16[384,256]{1,0:T(8,128)(2,1)} collective-permute-done((bf16[384,256]{1,0:T(8,128)(2,1)}, bf16[384,256]{1,0:T(8,128)(2,1)}, u32[]{:S(2)}, u32[]{:S(2)}) %collective-permute-start) | collective-permute-done | bytes 196640 | tf_op jit(solution)/shard_map/ppermute | solution.py:245
  43.7 3.4 %collective-permute-done.1 = bf16[1024,256]{1,0:T(8,128)(2,1)} collective-permute-done((bf16[1024,256]{1,0:T(8,128)(2,1)}, bf16[1024,256]{1,0:T(8,128)(2,1)}, u32[]{:S(2)}, u32[]{:S(2)}) %collective-permute-start.1) | collective-permute-done | bytes 524320 | tf_op jit(solution)/shard_map/ppermute | solution.py:245
  47.2 2.4 pad_maximum_fusion.4
  49.5 2.0 all-to-all-done
  51.5 5.0 %all-to-all-start.2 = ((bf16[128,8,1280]{2,0,1:T(8,128)(2,1)}), bf16[128,8,1280]{2,0,1:T(8,128)(2,1)S(1)}, u32[]{:S(2)}, u32[]{:S(2)}) async-start(bf16[128,8,1280]{2,0,1:T(8,128)(2,1)} %pad_maximum_fusion), calls=%async_computation.2 | async-start | bytes 5242880 | tf_op jit(solution)/shard_map/all_to_all | solution.py:284
  59.3 2.5 fusion.11
  61.7 2.7 fusion.10
  64.5 32.4 %shard_map.93 = (bf16[16,128,768]{2,1,0:T(8,128)(2,1)}, f32[2432,128]{1,0:T(8,128)}, f32[2432,128]{1,0:T(8,128)}) custom-call(s32[8]{0:T(128)} %dynamic-slice_bitcast_fusion.slot_ref, s32[8,128,1]{2,1,0:T(8,128)} %copy.25.qdoc_ref, s32[8,1,1536]{2,1,0:T(1,128)} %reshape.122.kdoc_ref, bf16[8,128,384]{2,1,0:T(8,128)(2,1)} %get-tuple-element.37.q_ref, ...), custom_call_target="tpu_custom_call" | custom-call | tf_op jit(solution)/shard_map/pallas_call | solution.py:231
  96.8 6.9 %all-to-all-start.1 = ((bf16[16,128,768]{2,1,0:T(8,128)(2,1)}), bf16[16,128,768]{2,1,0:T(8,128)(2,1)}, u32[]{:S(2)}, u32[]{:S(2)}) async-start(bf16[16,128,768]{2,1,0:T(8,128)(2,1)} %get-tuple-element.23), calls=%async_computation.1 | async-start | bytes 6291456 | tf_op jit(solution)/shard_map/all_to_all | solution.py:300
  103.7 1.9 fusion.8
  105.6 50.3 %shard_map.94 = (bf16[16,128,1280]{2,1,0:T(8,128)(2,1)}, f32[2432,128]{1,0:T(8,128)}, f32[2432,128]{1,0:T(8,128)}) custom-call(s32[8]{0:T(128)} %dynamic-slice_bitcast_fusion.slot_ref, s32[8,128,1]{2,1,0:T(8,128)} %copy.25.qdoc_ref, s32[8,1,1536]{2,1,0:T(1,128)} %reshape.122.kdoc_ref, bf16[8,128,640]{2,1,0:T(8,128)(2,1)} %get-tuple-element.33.q_ref, ...), custom_call_target="tpu_custom_call" | custom-call | tf_op jit(solution)/shard_map/pallas_call | solution.py:231
  155.9 5.9 %all-to-all-start.3 = ((bf16[16,128,1280]{2,1,0:T(8,128)(2,1)}), bf16[16,128,1280]{2,1,0:T(8,128)(2,1)}, u32[]{:S(2)}, u32[]{:S(2)}) async-start(bf16[16,128,1280]{2,1,0:T(8,128)(2,1)} %get-tuple-element.25), calls=%async_computation.3 | async-start | bytes 10485760 | tf_op jit(solution)/shard_map/all_to_all | solution.py:300
  162.0 1.5 add.53
  164.1 2.2 collective-permute-start.2
  166.6 3.4 %collective-permute-start.3 = (f32[384,256]{1,0:T(8,128)S(1)}, f32[384,256]{1,0:T(8,128)S(1)}, u32[]{:S(2)}, u32[]{:S(2)}) collective-permute-start(f32[384,256]{1,0:T(8,128)S(1)} %pad_maximum_fusion.5), channel_id=1, source_target_pairs={{16,0},{24,8},{32,16},{40,24},{48,32},{56,40},{64,48},{72,56},{80,... | collective-permute-start | bytes 1179656 | tf_op jit(solution)/shard_map/ppermute | solution.py:250
  170.0 64.1 %collective-permute-done.2 = f32[1024,256]{1,0:T(8,128)S(1)} collective-permute-done((f32[1024,256]{1,0:T(8,128)S(1)}, f32[1024,256]{1,0:T(8,128)S(1)}, u32[]{:S(2)}, u32[]{:S(2)}) %collective-permute-start.2) | collective-permute-done | bytes 1048608 | tf_op jit(solution)/shard_map/ppermute | solution.py:250
  234.2 28.6 %collective-permute-done.3 = f32[384,256]{1,0:T(8,128)S(1)} collective-permute-done((f32[384,256]{1,0:T(8,128)S(1)}, f32[384,256]{1,0:T(8,128)S(1)}, u32[]{:S(2)}, u32[]{:S(2)}) %collective-permute-start.3) | collective-permute-done | bytes 393248 | tf_op jit(solution)/shard_map/ppermute | solution.py:250
  263.8 2.5 gather_fusion
  267.7 3.2 %gather_fusion.1 = bf16[8,128,1280]{2,1,0:T(8,128)(2,1)S(1)} fusion(bf16[16,128,1280]{2,1,0:T(8,128)(2,1)} %all-to-all-done.3, s32[1024]{0:T(1024)S(1)} %pad_clamp_fusion), kind=kCustom, calls=%fused_computation.1 | custom fusion | bytes 5242912 | tf_op jit(solution)/shard_map/jit(_take)/gather | solution.py:301
  272.4 2.6 pad_maximum_fusion.1
  (62 shorter events, 11.0 us)
Async XLA Ops:
  14.2 7.2 %copy-start.5 = (bf16[1024,128]{1,0:T(8,128)(2,1)S(1)}, bf16[1024,128]{1,0:T(8,128)(2,1)}, u32[]{:S(2)}) copy-start(bf16[1024,128]{1,0:T(8,128)(2,1)} %param.9) | copy-start | bytes 786436
  14.2 8.0 %copy-start.6 = (bf16[1024,128]{1,0:T(8,128)(2,1)S(1)}, bf16[1024,128]{1,0:T(8,128)(2,1)}, u32[]{:S(2)}) copy-start(bf16[1024,128]{1,0:T(8,128)(2,1)} %param.10) | copy-start | bytes 786436
  14.2 37.3 %all-to-all-start = ((bf16[128,8,768]{2,0,1:T(8,128)(2,1)}), bf16[128,8,768]{2,0,1:T(8,128)(2,1)}, u32[]{:S(2)}, u32[]{:S(2)}) async-start(bf16[128,8,768]{2,0,1:T(8,128)(2,1)} %pad_maximum_fusion.3), calls=%async_computation | async-start | bytes 3145728 | tf_op jit(solution)/shard_map/all_to_all | solution.py:284
  21.4 8.6 %copy-start = (bf16[128,8192]{0,1:T(8,128)(2,1)S(1)}, bf16[128,8192]{0,1:T(8,128)(2,1)}, u32[]{:S(2)}) copy-start(bf16[128,8192]{0,1:T(8,128)(2,1)} %copy.23) | copy-start | bytes 6291460
  22.9 24.3 %collective-permute-start.1 = (bf16[1024,256]{1,0:T(8,128)(2,1)}, bf16[1024,256]{1,0:T(8,128)(2,1)}, u32[]{:S(2)}, u32[]{:S(2)}) collective-permute-start(bf16[1024,256]{1,0:T(8,128)(2,1)} %constant_dynamic-update-slice_fusion), channel_id=1, source_target_pairs={{0,8},{8,16},{16,24},{24,32},{32,40},{40,48},{48,56},{56,64},{64,7... | collective-permute-start | bytes 1572872 | tf_op jit(solution)/shard_map/ppermute | solution.py:245
  26.4 17.3 %collective-permute-start = (bf16[384,256]{1,0:T(8,128)(2,1)}, bf16[384,256]{1,0:T(8,128)(2,1)}, u32[]{:S(2)}, u32[]{:S(2)}) collective-permute-start(bf16[384,256]{1,0:T(8,128)(2,1)} %slice.166), channel_id=1, source_target_pairs={{0,16},{8,24},{16,32},{24,40},{32,48},{40,56},{48,64},{56,72},{64,... | collective-permute-start | bytes 589832 | tf_op jit(solution)/shard_map/ppermute | solution.py:245
  49.5 7.0 %copy-start.8 = (s32[128]{0:T(128)S(1)}, s32[128]{0:T(128)}, u32[]{:S(2)}) copy-start(s32[128]{0:T(128)} %param.13) | copy-start | bytes 1540
  49.5 7.1 %copy-start.7 = (s32[16384]{0:T(1024)S(1)}, s32[16384]{0:T(1024)}, u32[]{:S(2)}) copy-start(s32[16384]{0:T(1024)} %param.12) | copy-start | bytes 196612
  51.5 45.3 %all-to-all-start.2 = ((bf16[128,8,1280]{2,0,1:T(8,128)(2,1)}), bf16[128,8,1280]{2,0,1:T(8,128)(2,1)S(1)}, u32[]{:S(2)}, u32[]{:S(2)}) async-start(bf16[128,8,1280]{2,0,1:T(8,128)(2,1)} %pad_maximum_fusion), calls=%async_computation.2 | async-start | bytes 5242880 | tf_op jit(solution)/shard_map/all_to_all | solution.py:284
  96.8 59.1 %all-to-all-start.1 = ((bf16[16,128,768]{2,1,0:T(8,128)(2,1)}), bf16[16,128,768]{2,1,0:T(8,128)(2,1)}, u32[]{:S(2)}, u32[]{:S(2)}) async-start(bf16[16,128,768]{2,1,0:T(8,128)(2,1)} %get-tuple-element.23), calls=%async_computation.1 | async-start | bytes 6291456 | tf_op jit(solution)/shard_map/all_to_all | solution.py:300
  155.9 6.1 %copy-start.3 = (f32[2432,128]{1,0:T(8,128)S(1)}, f32[2432,128]{1,0:T(8,128)}, u32[]{:S(2)}) copy-start(f32[2432,128]{1,0:T(8,128)} %get-tuple-element.28) | copy-start | bytes 3735556
  155.9 111.8 %all-to-all-start.3 = ((bf16[16,128,1280]{2,1,0:T(8,128)(2,1)}), bf16[16,128,1280]{2,1,0:T(8,128)(2,1)}, u32[]{:S(2)}, u32[]{:S(2)}) async-start(bf16[16,128,1280]{2,1,0:T(8,128)(2,1)} %get-tuple-element.25), calls=%async_computation.3 | async-start | bytes 10485760 | tf_op jit(solution)/shard_map/all_to_all | solution.py:300
  161.8 1.8 copy-start.2
  162.0 1.9 copy-start.4
  164.1 70.0 %collective-permute-start.2 = (f32[1024,256]{1,0:T(8,128)S(1)}, f32[1024,256]{1,0:T(8,128)S(1)}, u32[]{:S(2)}, u32[]{:S(2)}) collective-permute-start(f32[1024,256]{1,0:T(8,128)S(1)} %fusion), channel_id=1, source_target_pairs={{8,0},{16,8},{24,16},{32,24},{40,32},{48,40},{56,48},{64,56},{72,6... | collective-permute-start | bytes 3145736 | tf_op jit(solution)/shard_map/ppermute | solution.py:250
  166.6 96.3 %collective-permute-start.3 = (f32[384,256]{1,0:T(8,128)S(1)}, f32[384,256]{1,0:T(8,128)S(1)}, u32[]{:S(2)}, u32[]{:S(2)}) collective-permute-start(f32[384,256]{1,0:T(8,128)S(1)} %pad_maximum_fusion.5), channel_id=1, source_target_pairs={{16,0},{24,8},{32,16},{40,24},{48,32},{56,40},{64,48},{72,56},{80,... | collective-permute-start | bytes 1179656 | tf_op jit(solution)/shard_map/ppermute | solution.py:250
  271.3 1.1 copy-start.1

commit v8 on v7

--- a/solution.py
+++ b/solution.py
@@ -177,8 +177,8 @@
         raw = lax.dot_general(query, key_window, TRANS_B, preferred_element_type=jnp.float32) * scale
         scores = raw + bias
         row_max = jnp.max(scores, axis=1, keepdims=True)
-        log_total = row_max + jnp.log(jnp.sum(jnp.exp(scores - row_max), axis=1, keepdims=True))
-        weights = jnp.exp(scores - log_total)
+        shifted = jnp.exp(scores - row_max)
+        weights = shifted * (1.0 / jnp.sum(shifted, axis=1, keepdims=True))
         soft_low = weights.astype(jnp.bfloat16)
         out = jnp.dot(soft_low, value_window, preferred_element_type=jnp.float32).astype(jnp.bfloat16)
         res_ref[0, :, cols_of] = out
@@ -190,13 +190,13 @@
         res_ref[0, :, width + head * HEAD_DIM : width + (head + 1) * HEAD_DIM] = dq.astype(
             jnp.bfloat16
         )
-        dk = lax.dot_general(score_grad, query, TRANS_A, preferred_element_type=jnp.float32) * scale
+        dk = lax.dot_general(score_grad, query, TRANS_A, preferred_element_type=jnp.float32)
         dv = lax.dot_general(soft_low, grad, TRANS_A, preferred_element_type=jnp.float32)
         if dk_sum is None:
             dk_sum, dv_sum = dk, dv
         else:
             dk_sum, dv_sum = dk_sum + dk, dv_sum + dv
-    dk_ref[pl.ds(start, window_rows), :] += dk_sum
+    dk_ref[pl.ds(start, window_rows), :] += dk_sum * scale
     dv_ref[pl.ds(start, window_rows), :] += dv_sum
 
 

time: 276 us -> 274 us (level)
  no operation moved by 1% of the time
where the time goes in v8:
time: 274 us; the launch traced here: 273 us
  waiting for transfers between devices  107 us (39%)
  Pallas kernels  80.6 us (29%)
  local copies, waits for them, and re-layouts  36.5 us (13%)
  starting transfers between devices  36 us (13%)
  other arithmetic  12.3 us (4%)
    ppermute x2, waiting for transfers between devices, shift_to_below(): return lax.ppermute(x, 'ctx', pairs)  92.8 us
    pallas_call x2, Pallas kernels, fused_attention(): pl.pallas_call(fused_kernel, grid_spec=grid_spec, out_shape=[jax.ShapeDty...  80.6 us
    unnamed x25, local copies, waits for them, and re-layouts  13.9 us
    all_to_all x2, starting transfers between devices, on_device(): lax.all_to_all(results, 'ctx', split_axis=0, concat_axis=0, tiled=True)  12.8 us
    all_to_all x2, starting transfers between devices, on_device(): both = lax.all_to_all(both, 'tp', split_axis=1, concat_axis=0, tiled=True)  12.3 us
    ppermute x2, waiting for transfers between devices, shift_from_below(): return lax.ppermute(x, 'ctx', pairs)  11.8 us
    gather x2, local copies, waits for them, and re-layouts, on_device(): held_parts.append(jnp.take(sent, held_sources, axis=0))  5.74 us
    ppermute x2, starting transfers between devices, shift_to_below(): return lax.ppermute(x, 'ctx', pairs)  5.56 us
  transfers between devices with their start and end apart: 8, of which 5 were waited for; matrix products, arithmetic and copies ran while one was open for 10% of the time, Pallas kernels for 30%

profile of v8, /device:TPU:60, one launch (start us, length us, event | category | flops | bytes accessed | tf_op | source)
XLA Modules:
  0.0 272.9 jit_solution(930658204401528364)
XLA Ops:
  0.6 3.2 %copy.21 = bf16[128,8192]{0,1:T(8,128)(2,1)S(1)} copy(bf16[128,8192]{1,0:T(8,128)(2,1)} %param.8) | data formatting | bytes 4194304 | tf_op args[0]
  3.9 1.2 copy.29
  5.1 4.1 %copy.23 = bf16[128,8192]{0,1:T(8,128)(2,1)} copy(bf16[128,8192]{1,0:T(8,128)(2,1)} %param.11) | data formatting | bytes 4194304 | tf_op args[3]
  9.2 1.2 slice.163
  10.4 1.2 copy.30
  11.5 2.6 pad_maximum_fusion.3
  14.2 7.2 %all-to-all-start = ((bf16[128,8,768]{2,0,1:T(8,128)(2,1)}), bf16[128,8,768]{2,0,1:T(8,128)(2,1)}, u32[]{:S(2)}, u32[]{:S(2)}) async-start(bf16[128,8,768]{2,0,1:T(8,128)(2,1)} %pad_maximum_fusion.3), calls=%async_computation | async-start | bytes 3145728 | tf_op jit(solution)/shard_map/all_to_all | solution.py:284
  22.9 1.9 collective-permute-start.1
  24.8 1.6 slice.166
  26.4 3.5 %collective-permute-start = (bf16[384,256]{1,0:T(8,128)(2,1)}, bf16[384,256]{1,0:T(8,128)(2,1)}, u32[]{:S(2)}, u32[]{:S(2)}) collective-permute-start(bf16[384,256]{1,0:T(8,128)(2,1)} %slice.166), channel_id=1, source_target_pairs={{0,16},{8,24},{16,32},{24,40},{32,48},{40,56},{48,64},{56,72},{64,... | collective-permute-start | bytes 589832 | tf_op jit(solution)/shard_map/ppermute | solution.py:245
  31.9 1.7 copy.32
  33.7 1.7 pad_maximum_fusion
  35.4 8.4 %collective-permute-done = bf16[384,256]{1,0:T(8,128)(2,1)} collective-permute-done((bf16[384,256]{1,0:T(8,128)(2,1)}, bf16[384,256]{1,0:T(8,128)(2,1)}, u32[]{:S(2)}, u32[]{:S(2)}) %collective-permute-start) | collective-permute-done | bytes 196640 | tf_op jit(solution)/shard_map/ppermute | solution.py:245
  43.7 3.4 %collective-permute-done.1 = bf16[1024,256]{1,0:T(8,128)(2,1)} collective-permute-done((bf16[1024,256]{1,0:T(8,128)(2,1)}, bf16[1024,256]{1,0:T(8,128)(2,1)}, u32[]{:S(2)}, u32[]{:S(2)}) %collective-permute-start.1) | collective-permute-done | bytes 524320 | tf_op jit(solution)/shard_map/ppermute | solution.py:245
  47.2 2.4 pad_maximum_fusion.4
  49.5 2.0 all-to-all-done
  51.5 5.0 %all-to-all-start.2 = ((bf16[128,8,1280]{2,0,1:T(8,128)(2,1)}), bf16[128,8,1280]{2,0,1:T(8,128)(2,1)S(1)}, u32[]{:S(2)}, u32[]{:S(2)}) async-start(bf16[128,8,1280]{2,0,1:T(8,128)(2,1)} %pad_maximum_fusion), calls=%async_computation.2 | async-start | bytes 5242880 | tf_op jit(solution)/shard_map/all_to_all | solution.py:284
  59.3 2.5 fusion.11
  61.7 2.7 fusion.10
  64.5 31.5 %shard_map.93 = (bf16[16,128,768]{2,1,0:T(8,128)(2,1)}, f32[2432,128]{1,0:T(8,128)}, f32[2432,128]{1,0:T(8,128)}) custom-call(s32[8]{0:T(128)} %dynamic-slice_bitcast_fusion.slot_ref, s32[8,128,1]{2,1,0:T(8,128)} %copy.25.qdoc_ref, s32[8,1,1536]{2,1,0:T(1,128)} %reshape.122.kdoc_ref, bf16[8,128,384]{2,1,0:T(8,128)(2,1)} %get-tuple-element.37.q_ref, ...), custom_call_target="tpu_custom_call" | custom-call | tf_op jit(solution)/shard_map/pallas_call | solution.py:231
  96.0 6.9 %all-to-all-start.1 = ((bf16[16,128,768]{2,1,0:T(8,128)(2,1)}), bf16[16,128,768]{2,1,0:T(8,128)(2,1)}, u32[]{:S(2)}, u32[]{:S(2)}) async-start(bf16[16,128,768]{2,1,0:T(8,128)(2,1)} %get-tuple-element.23), calls=%async_computation.1 | async-start | bytes 6291456 | tf_op jit(solution)/shard_map/all_to_all | solution.py:300
  102.9 1.9 fusion.8
  104.8 49.0 %shard_map.94 = (bf16[16,128,1280]{2,1,0:T(8,128)(2,1)}, f32[2432,128]{1,0:T(8,128)}, f32[2432,128]{1,0:T(8,128)}) custom-call(s32[8]{0:T(128)} %dynamic-slice_bitcast_fusion.slot_ref, s32[8,128,1]{2,1,0:T(8,128)} %copy.25.qdoc_ref, s32[8,1,1536]{2,1,0:T(1,128)} %reshape.122.kdoc_ref, bf16[8,128,640]{2,1,0:T(8,128)(2,1)} %get-tuple-element.33.q_ref, ...), custom_call_target="tpu_custom_call" | custom-call | tf_op jit(solution)/shard_map/pallas_call | solution.py:231
  153.8 5.9 %all-to-all-start.3 = ((bf16[16,128,1280]{2,1,0:T(8,128)(2,1)}), bf16[16,128,1280]{2,1,0:T(8,128)(2,1)}, u32[]{:S(2)}, u32[]{:S(2)}) async-start(bf16[16,128,1280]{2,1,0:T(8,128)(2,1)} %get-tuple-element.25), calls=%async_computation.3 | async-start | bytes 10485760 | tf_op jit(solution)/shard_map/all_to_all | solution.py:300
  159.9 1.5 add.53
  162.0 2.2 collective-permute-start.2
  164.5 3.4 %collective-permute-start.3 = (f32[384,256]{1,0:T(8,128)S(1)}, f32[384,256]{1,0:T(8,128)S(1)}, u32[]{:S(2)}, u32[]{:S(2)}) collective-permute-start(f32[384,256]{1,0:T(8,128)S(1)} %pad_maximum_fusion.5), channel_id=1, source_target_pairs={{16,0},{24,8},{32,16},{40,24},{48,32},{56,40},{64,48},{72,56},{80,... | collective-permute-start | bytes 1179656 | tf_op jit(solution)/shard_map/ppermute | solution.py:250
  167.9 64.1 %collective-permute-done.2 = f32[1024,256]{1,0:T(8,128)S(1)} collective-permute-done((f32[1024,256]{1,0:T(8,128)S(1)}, f32[1024,256]{1,0:T(8,128)S(1)}, u32[]{:S(2)}, u32[]{:S(2)}) %collective-permute-start.2) | collective-permute-done | bytes 1048608 | tf_op jit(solution)/shard_map/ppermute | solution.py:250
  232.1 28.6 %collective-permute-done.3 = f32[384,256]{1,0:T(8,128)S(1)} collective-permute-done((f32[384,256]{1,0:T(8,128)S(1)}, f32[384,256]{1,0:T(8,128)S(1)}, u32[]{:S(2)}, u32[]{:S(2)}) %collective-permute-start.3) | collective-permute-done | bytes 393248 | tf_op jit(solution)/shard_map/ppermute | solution.py:250
  261.7 2.5 gather_fusion
  265.6 3.2 %gather_fusion.1 = bf16[8,128,1280]{2,1,0:T(8,128)(2,1)S(1)} fusion(bf16[16,128,1280]{2,1,0:T(8,128)(2,1)} %all-to-all-done.3, s32[1024]{0:T(1024)S(1)} %pad_clamp_fusion), kind=kCustom, calls=%fused_computation.1 | custom fusion | bytes 5242912 | tf_op jit(solution)/shard_map/jit(_take)/gather | solution.py:301
  270.3 2.6 pad_maximum_fusion.1
  (62 shorter events, 11.0 us)
Async XLA Ops:
  14.2 7.2 %copy-start.5 = (bf16[1024,128]{1,0:T(8,128)(2,1)S(1)}, bf16[1024,128]{1,0:T(8,128)(2,1)}, u32[]{:S(2)}) copy-start(bf16[1024,128]{1,0:T(8,128)(2,1)} %param.9) | copy-start | bytes 786436
  14.2 8.0 %copy-start.6 = (bf16[1024,128]{1,0:T(8,128)(2,1)S(1)}, bf16[1024,128]{1,0:T(8,128)(2,1)}, u32[]{:S(2)}) copy-start(bf16[1024,128]{1,0:T(8,128)(2,1)} %param.10) | copy-start | bytes 786436
  14.2 37.3 %all-to-all-start = ((bf16[128,8,768]{2,0,1:T(8,128)(2,1)}), bf16[128,8,768]{2,0,1:T(8,128)(2,1)}, u32[]{:S(2)}, u32[]{:S(2)}) async-start(bf16[128,8,768]{2,0,1:T(8,128)(2,1)} %pad_maximum_fusion.3), calls=%async_computation | async-start | bytes 3145728 | tf_op jit(solution)/shard_map/all_to_all | solution.py:284
  21.4 8.6 %copy-start = (bf16[128,8192]{0,1:T(8,128)(2,1)S(1)}, bf16[128,8192]{0,1:T(8,128)(2,1)}, u32[]{:S(2)}) copy-start(bf16[128,8192]{0,1:T(8,128)(2,1)} %copy.23) | copy-start | bytes 6291460
  22.9 24.3 %collective-permute-start.1 = (bf16[1024,256]{1,0:T(8,128)(2,1)}, bf16[1024,256]{1,0:T(8,128)(2,1)}, u32[]{:S(2)}, u32[]{:S(2)}) collective-permute-start(bf16[1024,256]{1,0:T(8,128)(2,1)} %constant_dynamic-update-slice_fusion), channel_id=1, source_target_pairs={{0,8},{8,16},{16,24},{24,32},{32,40},{40,48},{48,56},{56,64},{64,7... | collective-permute-start | bytes 1572872 | tf_op jit(solution)/shard_map/ppermute | solution.py:245
  26.4 17.3 %collective-permute-start = (bf16[384,256]{1,0:T(8,128)(2,1)}, bf16[384,256]{1,0:T(8,128)(2,1)}, u32[]{:S(2)}, u32[]{:S(2)}) collective-permute-start(bf16[384,256]{1,0:T(8,128)(2,1)} %slice.166), channel_id=1, source_target_pairs={{0,16},{8,24},{16,32},{24,40},{32,48},{40,56},{48,64},{56,72},{64,... | collective-permute-start | bytes 589832 | tf_op jit(solution)/shard_map/ppermute | solution.py:245
  49.5 7.0 %copy-start.8 = (s32[128]{0:T(128)S(1)}, s32[128]{0:T(128)}, u32[]{:S(2)}) copy-start(s32[128]{0:T(128)} %param.13) | copy-start | bytes 1540
  49.5 7.1 %copy-start.7 = (s32[16384]{0:T(1024)S(1)}, s32[16384]{0:T(1024)}, u32[]{:S(2)}) copy-start(s32[16384]{0:T(1024)} %param.12) | copy-start | bytes 196612
  51.5 44.5 %all-to-all-start.2 = ((bf16[128,8,1280]{2,0,1:T(8,128)(2,1)}), bf16[128,8,1280]{2,0,1:T(8,128)(2,1)S(1)}, u32[]{:S(2)}, u32[]{:S(2)}) async-start(bf16[128,8,1280]{2,0,1:T(8,128)(2,1)} %pad_maximum_fusion), calls=%async_computation.2 | async-start | bytes 5242880 | tf_op jit(solution)/shard_map/all_to_all | solution.py:284
  96.0 57.8 %all-to-all-start.1 = ((bf16[16,128,768]{2,1,0:T(8,128)(2,1)}), bf16[16,128,768]{2,1,0:T(8,128)(2,1)}, u32[]{:S(2)}, u32[]{:S(2)}) async-start(bf16[16,128,768]{2,1,0:T(8,128)(2,1)} %get-tuple-element.23), calls=%async_computation.1 | async-start | bytes 6291456 | tf_op jit(solution)/shard_map/all_to_all | solution.py:300
  153.8 6.1 %copy-start.3 = (f32[2432,128]{1,0:T(8,128)S(1)}, f32[2432,128]{1,0:T(8,128)}, u32[]{:S(2)}) copy-start(f32[2432,128]{1,0:T(8,128)} %get-tuple-element.28) | copy-start | bytes 3735556
  153.8 111.8 %all-to-all-start.3 = ((bf16[16,128,1280]{2,1,0:T(8,128)(2,1)}), bf16[16,128,1280]{2,1,0:T(8,128)(2,1)}, u32[]{:S(2)}, u32[]{:S(2)}) async-start(bf16[16,128,1280]{2,1,0:T(8,128)(2,1)} %get-tuple-element.25), calls=%async_computation.3 | async-start | bytes 10485760 | tf_op jit(solution)/shard_map/all_to_all | solution.py:300
  159.7 1.8 copy-start.2
  159.9 1.9 copy-start.4
  162.0 70.0 %collective-permute-start.2 = (f32[1024,256]{1,0:T(8,128)S(1)}, f32[1024,256]{1,0:T(8,128)S(1)}, u32[]{:S(2)}, u32[]{:S(2)}) collective-permute-start(f32[1024,256]{1,0:T(8,128)S(1)} %fusion), channel_id=1, source_target_pairs={{8,0},{16,8},{24,16},{32,24},{40,32},{48,40},{56,48},{64,56},{72,6... | collective-permute-start | bytes 3145736 | tf_op jit(solution)/shard_map/ppermute | solution.py:250
  164.5 96.3 %collective-permute-start.3 = (f32[384,256]{1,0:T(8,128)S(1)}, f32[384,256]{1,0:T(8,128)S(1)}, u32[]{:S(2)}, u32[]{:S(2)}) collective-permute-start(f32[384,256]{1,0:T(8,128)S(1)} %pad_maximum_fusion.5), channel_id=1, source_target_pairs={{16,0},{24,8},{32,16},{40,24},{48,32},{56,40},{64,48},{72,56},{80,... | collective-permute-start | bytes 1179656 | tf_op jit(solution)/shard_map/ppermute | solution.py:250
  269.2 1.1 copy-start.1

commit v9 on v8

--- a/solution.py
+++ b/solution.py
@@ -300,10 +300,10 @@
         sent = lax.all_to_all(results, "ctx", split_axis=0, concat_axis=0, tiled=True)
         held_parts.append(jnp.take(sent, held_sources, axis=0))
     kv_grad = jnp.concatenate([key_grad, value_grad], axis=1)
-    grad_near = shift_to_below(kv_grad[far:reach], ctx_count, 1)
-    grad_far = shift_to_below(kv_grad[:far], ctx_count, 2)
-    kv_total = kv_grad[reach:] + grad_near
-    kv_total = kv_total.at[tok_dev - far :].add(grad_far)
+    grad_near = shift_to_below(kv_grad[far:reach].astype(jnp.bfloat16), ctx_count, 1)
+    grad_far = shift_to_below(kv_grad[:far].astype(jnp.bfloat16), ctx_count, 2)
+    kv_total = kv_grad[reach:] + grad_near.astype(jnp.float32)
+    kv_total = kv_total.at[tok_dev - far :].add(grad_far.astype(jnp.float32))
     widths = [high - low for low, high in bounds]
     held_out = jnp.concatenate([p[..., :w] for p, w in zip(held_parts, widths)], axis=-1)
     held_dq = jnp.concatenate([p[..., w:] for p, w in zip(held_parts, widths)], axis=-1)

time: 274 us -> 264 us (0.964)
  waiting for transfers between devices: 107 us -> 96.7 us
    ppermute x2, waiting for transfers between devices: 92.8 us -> 82.9 us  [shift_to_below(): return lax.ppermute(x, 'ctx', pairs)]
  transfers between devices with their start and end apart: 8 -> 8, of which waited for: 5 -> 5; matrix products, arithmetic and copies ran while one was open for 10% -> 11% of each run, Pallas kernels for 30% -> 31%
where the time goes in v9:
time: 264 us; the launch traced here: 263 us
  waiting for transfers between devices  96.7 us (37%)
  Pallas kernels  80.6 us (31%)
  local copies, waits for them, and re-layouts  36.3 us (14%)
  starting transfers between devices  36 us (14%)
  other arithmetic  12.5 us (5%)
    ppermute x2, waiting for transfers between devices, shift_to_below(): return lax.ppermute(x, 'ctx', pairs)  82.9 us
    pallas_call x2, Pallas kernels, fused_attention(): pl.pallas_call(fused_kernel, grid_spec=grid_spec, out_shape=[jax.ShapeDty...  80.6 us
    unnamed x25, local copies, waits for them, and re-layouts  13.6 us
    all_to_all x2, starting transfers between devices, on_device(): lax.all_to_all(results, 'ctx', split_axis=0, concat_axis=0, tiled=True)  12.8 us
    all_to_all x2, starting transfers between devices, on_device(): both = lax.all_to_all(both, 'tp', split_axis=1, concat_axis=0, tiled=True)  12.3 us
    ppermute x2, waiting for transfers between devices, shift_from_below(): return lax.ppermute(x, 'ctx', pairs)  11.8 us
    gather x2, local copies, waits for them, and re-layouts, on_device(): held_parts.append(jnp.take(sent, held_sources, axis=0))  5.74 us
    ppermute x2, starting transfers between devices, shift_to_below(): return lax.ppermute(x, 'ctx', pairs)  5.56 us
  transfers between devices with their start and end apart: 8, of which 5 were waited for; matrix products, arithmetic and copies ran while one was open for 11% of the time, Pallas kernels for 31%

profile of v9, /device:TPU:60, one launch (start us, length us, event | category | flops | bytes accessed | tf_op | source)
XLA Modules:
  0.0 263.1 jit_solution(7152762463238081565)
XLA Ops:
  0.6 3.2 %copy.21 = bf16[128,8192]{0,1:T(8,128)(2,1)S(1)} copy(bf16[128,8192]{1,0:T(8,128)(2,1)} %param.8) | data formatting | bytes 4194304 | tf_op args[0]
  3.9 1.2 copy.29
  5.1 4.1 %copy.23 = bf16[128,8192]{0,1:T(8,128)(2,1)} copy(bf16[128,8192]{1,0:T(8,128)(2,1)} %param.11) | data formatting | bytes 4194304 | tf_op args[3]
  9.2 1.2 slice.165
  10.4 1.2 copy.30
  11.5 2.6 %pad_maximum_fusion.4 = bf16[128,8,768]{2,0,1:T(8,128)(2,1)} fusion(bf16[128,8,384]{2,0,1:T(8,128)(2,1)} %copy.30, bf16[128,8,384]{2,0,1:T(8,128)(2,1)} %copy.29), kind=kLoop, calls=%fused_computation.10 | loop fusion | flops 3145728 | bytes 3145728 | tf_op jit(solution)/shard_map/concatenate | solution.py:281
  14.2 7.2 %all-to-all-start = ((bf16[128,8,768]{2,0,1:T(8,128)(2,1)}), bf16[128,8,768]{2,0,1:T(8,128)(2,1)}, u32[]{:S(2)}, u32[]{:S(2)}) async-start(bf16[128,8,768]{2,0,1:T(8,128)(2,1)} %pad_maximum_fusion.4), calls=%async_computation | async-start | bytes 3145728 | tf_op jit(solution)/shard_map/all_to_all | solution.py:284
  22.9 1.9 collective-permute-start.1
  24.8 1.6 slice.168
  26.4 3.5 %collective-permute-start = (bf16[384,256]{1,0:T(8,128)(2,1)}, bf16[384,256]{1,0:T(8,128)(2,1)}, u32[]{:S(2)}, u32[]{:S(2)}) collective-permute-start(bf16[384,256]{1,0:T(8,128)(2,1)} %slice.168), channel_id=1, source_target_pairs={{0,16},{8,24},{16,32},{24,40},{32,48},{40,56},{48,64},{56,72},{64,... | collective-permute-start | bytes 589832 | tf_op jit(solution)/shard_map/ppermute | solution.py:245
  31.9 1.7 copy.32
  33.7 1.7 pad_maximum_fusion.1
  35.4 8.4 %collective-permute-done = bf16[384,256]{1,0:T(8,128)(2,1)} collective-permute-done((bf16[384,256]{1,0:T(8,128)(2,1)}, bf16[384,256]{1,0:T(8,128)(2,1)}, u32[]{:S(2)}, u32[]{:S(2)}) %collective-permute-start) | collective-permute-done | bytes 196640 | tf_op jit(solution)/shard_map/ppermute | solution.py:245
  43.7 3.4 %collective-permute-done.1 = bf16[1024,256]{1,0:T(8,128)(2,1)} collective-permute-done((bf16[1024,256]{1,0:T(8,128)(2,1)}, bf16[1024,256]{1,0:T(8,128)(2,1)}, u32[]{:S(2)}, u32[]{:S(2)}) %collective-permute-start.1) | collective-permute-done | bytes 524320 | tf_op jit(solution)/shard_map/ppermute | solution.py:245
  47.2 2.4 pad_maximum_fusion.5
  49.5 2.0 all-to-all-done
  51.5 5.0 %all-to-all-start.2 = ((bf16[128,8,1280]{2,0,1:T(8,128)(2,1)}), bf16[128,8,1280]{2,0,1:T(8,128)(2,1)S(1)}, u32[]{:S(2)}, u32[]{:S(2)}) async-start(bf16[128,8,1280]{2,0,1:T(8,128)(2,1)} %pad_maximum_fusion.1), calls=%async_computation.2 | async-start | bytes 5242880 | tf_op jit(solution)/shard_map/all_to_all | solution.py:284
  59.3 2.5 fusion.11
  61.7 2.7 %fusion.10 = (bf16[8,128,384]{2,1,0:T(8,128)(2,1)}, bf16[8,128,384]{2,1,0:T(8,128)(2,1)}) fusion(bf16[8,128,768]{2,1,0:T(8,128)(2,1)} %bitcast.7), kind=kLoop, calls=%fused_computation.44 | loop fusion | bytes 3145728 | tf_op jit(solution)/shard_map/slice | solution.py:289
  64.5 31.5 %shard_map.93 = (bf16[16,128,768]{2,1,0:T(8,128)(2,1)}, f32[2432,128]{1,0:T(8,128)}, f32[2432,128]{1,0:T(8,128)}) custom-call(s32[8]{0:T(128)} %dynamic-slice_bitcast_fusion.slot_ref, s32[8,128,1]{2,1,0:T(8,128)} %copy.25.qdoc_ref, s32[8,1,1536]{2,1,0:T(1,128)} %reshape.122.kdoc_ref, bf16[8,128,384]{2,1,0:T(8,128)(2,1)} %get-tuple-element.37.q_ref, ...), custom_call_target="tpu_custom_call" | custom-call | tf_op jit(solution)/shard_map/pallas_call | solution.py:231
  96.0 6.9 %all-to-all-start.1 = ((bf16[16,128,768]{2,1,0:T(8,128)(2,1)}), bf16[16,128,768]{2,1,0:T(8,128)(2,1)}, u32[]{:S(2)}, u32[]{:S(2)}) async-start(bf16[16,128,768]{2,1,0:T(8,128)(2,1)} %get-tuple-element.23), calls=%async_computation.1 | async-start | bytes 6291456 | tf_op jit(solution)/shard_map/all_to_all | solution.py:300
  102.9 1.9 fusion.8
  104.8 49.0 %shard_map.94 = (bf16[16,128,1280]{2,1,0:T(8,128)(2,1)}, f32[2432,128]{1,0:T(8,128)}, f32[2432,128]{1,0:T(8,128)}) custom-call(s32[8]{0:T(128)} %dynamic-slice_bitcast_fusion.slot_ref, s32[8,128,1]{2,1,0:T(8,128)} %copy.25.qdoc_ref, s32[8,1,1536]{2,1,0:T(1,128)} %reshape.122.kdoc_ref, bf16[8,128,640]{2,1,0:T(8,128)(2,1)} %get-tuple-element.33.q_ref, ...), custom_call_target="tpu_custom_call" | custom-call | tf_op jit(solution)/shard_map/pallas_call | solution.py:231
  153.8 5.9 %all-to-all-start.3 = ((bf16[16,128,1280]{2,1,0:T(8,128)(2,1)}), bf16[16,128,1280]{2,1,0:T(8,128)(2,1)}, u32[]{:S(2)}, u32[]{:S(2)}) async-start(bf16[16,128,1280]{2,1,0:T(8,128)(2,1)} %get-tuple-element.25), calls=%async_computation.3 | async-start | bytes 10485760 | tf_op jit(solution)/shard_map/all_to_all | solution.py:300
  160.2 1.7 add.53
  162.2 2.2 collective-permute-start.2
  164.5 3.4 %collective-permute-start.3 = (bf16[384,256]{1,0:T(8,128)(2,1)S(1)}, bf16[384,256]{1,0:T(8,128)(2,1)S(1)}, u32[]{:S(2)}, u32[]{:S(2)}) collective-permute-start(bf16[384,256]{1,0:T(8,128)(2,1)S(1)} %slice.183), channel_id=1, source_target_pairs={{16,0},{24,8},{32,16},{40,24},{48,32},{56,40},{64,48},{72,56},{80,... | collective-permute-start | bytes 589832 | tf_op jit(solution)/shard_map/ppermute | solution.py:250
  167.8 56.5 %collective-permute-done.2 = bf16[1024,256]{1,0:T(8,128)(2,1)S(1)} collective-permute-done((bf16[1024,256]{1,0:T(8,128)(2,1)S(1)}, bf16[1024,256]{1,0:T(8,128)(2,1)S(1)}, u32[]{:S(2)}, u32[]{:S(2)}) %collective-permute-start.2) | collective-permute-done | bytes 524320 | tf_op jit(solution)/shard_map/ppermute | solution.py:250
  224.5 26.5 %collective-permute-done.3 = bf16[384,256]{1,0:T(8,128)(2,1)S(1)} collective-permute-done((bf16[384,256]{1,0:T(8,128)(2,1)S(1)}, bf16[384,256]{1,0:T(8,128)(2,1)S(1)}, u32[]{:S(2)}, u32[]{:S(2)}) %collective-permute-start.3) | collective-permute-done | bytes 196640 | tf_op jit(solution)/shard_map/ppermute | solution.py:250
  251.9 2.5 gather_fusion
  255.8 3.2 %gather_fusion.1 = bf16[8,128,1280]{2,1,0:T(8,128)(2,1)S(1)} fusion(bf16[16,128,1280]{2,1,0:T(8,128)(2,1)} %all-to-all-done.3, s32[1024]{0:T(1024)S(1)} %pad_clamp_fusion), kind=kCustom, calls=%fused_computation.1 | custom fusion | bytes 5242912 | tf_op jit(solution)/shard_map/jit(_take)/gather | solution.py:301
  260.5 2.6 pad_maximum_fusion.2
  (63 shorter events, 10.8 us)
Async XLA Ops:
  14.2 7.2 %copy-start.5 = (bf16[1024,128]{1,0:T(8,128)(2,1)S(1)}, bf16[1024,128]{1,0:T(8,128)(2,1)}, u32[]{:S(2)}) copy-start(bf16[1024,128]{1,0:T(8,128)(2,1)} %param.9) | copy-start | bytes 786436
  14.2 8.0 %copy-start.6 = (bf16[1024,128]{1,0:T(8,128)(2,1)S(1)}, bf16[1024,128]{1,0:T(8,128)(2,1)}, u32[]{:S(2)}) copy-start(bf16[1024,128]{1,0:T(8,128)(2,1)} %param.10) | copy-start | bytes 786436
  14.2 37.3 %all-to-all-start = ((bf16[128,8,768]{2,0,1:T(8,128)(2,1)}), bf16[128,8,768]{2,0,1:T(8,128)(2,1)}, u32[]{:S(2)}, u32[]{:S(2)}) async-start(bf16[128,8,768]{2,0,1:T(8,128)(2,1)} %pad_maximum_fusion.4), calls=%async_computation | async-start | bytes 3145728 | tf_op jit(solution)/shard_map/all_to_all | solution.py:284
  21.4 8.6 %copy-start = (bf16[128,8192]{0,1:T(8,128)(2,1)S(1)}, bf16[128,8192]{0,1:T(8,128)(2,1)}, u32[]{:S(2)}) copy-start(bf16[128,8192]{0,1:T(8,128)(2,1)} %copy.23) | copy-start | bytes 6291460
  22.9 24.3 %collective-permute-start.1 = (bf16[1024,256]{1,0:T(8,128)(2,1)}, bf16[1024,256]{1,0:T(8,128)(2,1)}, u32[]{:S(2)}, u32[]{:S(2)}) collective-permute-start(bf16[1024,256]{1,0:T(8,128)(2,1)} %constant_dynamic-update-slice_fusion), channel_id=1, source_target_pairs={{0,8},{8,16},{16,24},{24,32},{32,40},{40,48},{48,56},{56,64},{64,7... | collective-permute-start | bytes 1572872 | tf_op jit(solution)/shard_map/ppermute | solution.py:245
  26.4 17.3 %collective-permute-start = (bf16[384,256]{1,0:T(8,128)(2,1)}, bf16[384,256]{1,0:T(8,128)(2,1)}, u32[]{:S(2)}, u32[]{:S(2)}) collective-permute-start(bf16[384,256]{1,0:T(8,128)(2,1)} %slice.168), channel_id=1, source_target_pairs={{0,16},{8,24},{16,32},{24,40},{32,48},{40,56},{48,64},{56,72},{64,... | collective-permute-start | bytes 589832 | tf_op jit(solution)/shard_map/ppermute | solution.py:245
  49.5 7.0 %copy-start.8 = (s32[128]{0:T(128)S(1)}, s32[128]{0:T(128)}, u32[]{:S(2)}) copy-start(s32[128]{0:T(128)} %param.13) | copy-start | bytes 1540
  49.5 7.1 %copy-start.7 = (s32[16384]{0:T(1024)S(1)}, s32[16384]{0:T(1024)}, u32[]{:S(2)}) copy-start(s32[16384]{0:T(1024)} %param.12) | copy-start | bytes 196612
  51.5 44.5 %all-to-all-start.2 = ((bf16[128,8,1280]{2,0,1:T(8,128)(2,1)}), bf16[128,8,1280]{2,0,1:T(8,128)(2,1)S(1)}, u32[]{:S(2)}, u32[]{:S(2)}) async-start(bf16[128,8,1280]{2,0,1:T(8,128)(2,1)} %pad_maximum_fusion.1), calls=%async_computation.2 | async-start | bytes 5242880 | tf_op jit(solution)/shard_map/all_to_all | solution.py:284
  96.0 57.8 %all-to-all-start.1 = ((bf16[16,128,768]{2,1,0:T(8,128)(2,1)}), bf16[16,128,768]{2,1,0:T(8,128)(2,1)}, u32[]{:S(2)}, u32[]{:S(2)}) async-start(bf16[16,128,768]{2,1,0:T(8,128)(2,1)} %get-tuple-element.23), calls=%async_computation.1 | async-start | bytes 6291456 | tf_op jit(solution)/shard_map/all_to_all | solution.py:300
  153.8 6.4 %copy-start.3 = (f32[2432,128]{1,0:T(8,128)S(1)}, f32[2432,128]{1,0:T(8,128)}, u32[]{:S(2)}) copy-start(f32[2432,128]{1,0:T(8,128)} %get-tuple-element.28) | copy-start | bytes 3735556
  153.8 102.0 %all-to-all-start.3 = ((bf16[16,128,1280]{2,1,0:T(8,128)(2,1)}), bf16[16,128,1280]{2,1,0:T(8,128)(2,1)}, u32[]{:S(2)}, u32[]{:S(2)}) async-start(bf16[16,128,1280]{2,1,0:T(8,128)(2,1)} %get-tuple-element.25), calls=%async_computation.3 | async-start | bytes 10485760 | tf_op jit(solution)/shard_map/all_to_all | solution.py:300
  159.7 2.2 copy-start.2
  159.9 1.9 copy-start.4
  162.2 62.1 %collective-permute-start.2 = (bf16[1024,256]{1,0:T(8,128)(2,1)S(1)}, bf16[1024,256]{1,0:T(8,128)(2,1)S(1)}, u32[]{:S(2)}, u32[]{:S(2)}) collective-permute-start(bf16[1024,256]{1,0:T(8,128)(2,1)S(1)} %slice.181), channel_id=1, source_target_pairs={{8,0},{16,8},{24,16},{32,24},{40,32},{48,40},{56,48},{64,56},{72,6... | collective-permute-start | bytes 1572872 | tf_op jit(solution)/shard_map/ppermute | solution.py:250
  164.5 86.5 %collective-permute-start.3 = (bf16[384,256]{1,0:T(8,128)(2,1)S(1)}, bf16[384,256]{1,0:T(8,128)(2,1)S(1)}, u32[]{:S(2)}, u32[]{:S(2)}) collective-permute-start(bf16[384,256]{1,0:T(8,128)(2,1)S(1)} %slice.183), channel_id=1, source_target_pairs={{16,0},{24,8},{32,16},{40,24},{48,32},{56,40},{64,48},{72,56},{80,... | collective-permute-start | bytes 589832 | tf_op jit(solution)/shard_map/ppermute | solution.py:250
  259.3 1.1 copy-start.1

commit v10 on v9

--- a/solution.py
+++ b/solution.py
@@ -297,11 +297,13 @@
         else:
             key_grad = key_grad + chunk_key_grad
             value_grad = value_grad + chunk_value_grad
+        if chunk == len(bounds) - 1:
+            kv_grad = jnp.concatenate([key_grad, value_grad], axis=1)
+            grad_near = shift_to_below(kv_grad[far:reach].astype(jnp.bfloat16), ctx_count, 1)
+            grad_far = shift_to_below(kv_grad[:far].astype(jnp.bfloat16), ctx_count, 2)
+            results, grad_near, grad_far = lax.optimization_barrier((results, grad_near, grad_far))
         sent = lax.all_to_all(results, "ctx", split_axis=0, concat_axis=0, tiled=True)
         held_parts.append(jnp.take(sent, held_sources, axis=0))
-    kv_grad = jnp.concatenate([key_grad, value_grad], axis=1)
-    grad_near = shift_to_below(kv_grad[far:reach].astype(jnp.bfloat16), ctx_count, 1)
-    grad_far = shift_to_below(kv_grad[:far].astype(jnp.bfloat16), ctx_count, 2)
     kv_total = kv_grad[reach:] + grad_near.astype(jnp.float32)
     kv_total = kv_total.at[tok_dev - far :].add(grad_far.astype(jnp.float32))
     widths = [high - low for low, high in bounds]

time: 264 us -> 267 us (1.011)
    all_to_all x2, waiting for transfers between devices: 0.01 us -> 74.8 us  [on_device(): lax.all_to_all(results, 'ctx', split_axis=0, concat_axis=0, tiled=True)]
    ppermute x2, waiting for transfers between devices: 82.9 us -> 10.3 us  [shift_to_below(): return lax.ppermute(x, 'ctx', pairs)]
  transfers between devices with their start and end apart: 8 -> 8, of which waited for: 5 -> 5; matrix products, arithmetic and copies ran while one was open for 11% -> 11% of each run, Pallas kernels for 31% -> 30%
where the time goes in v10:
time: 267 us; the launch traced here: 266 us
  waiting for transfers between devices  98.8 us (37%)
  Pallas kernels  80.7 us (30%)
  local copies, waits for them, and re-layouts  36.9 us (14%)
  starting transfers between devices  35.9 us (13%)
  other arithmetic  12.3 us (5%)
    pallas_call x2, Pallas kernels, fused_attention(): pl.pallas_call(fused_kernel, grid_spec=grid_spec, out_shape=[jax.ShapeDty...  80.7 us
    all_to_all x2, waiting for transfers between devices, on_device(): lax.all_to_all(results, 'ctx', split_axis=0, concat_axis=0, tiled=True)  74.8 us
    unnamed x25, local copies, waits for them, and re-layouts  14 us
    all_to_all x2, starting transfers between devices, on_device(): lax.all_to_all(results, 'ctx', split_axis=0, concat_axis=0, tiled=True)  12.6 us
    all_to_all x2, starting transfers between devices, on_device(): both = lax.all_to_all(both, 'tp', split_axis=1, concat_axis=0, tiled=True)  12.3 us
    ppermute x2, waiting for transfers between devices, shift_from_below(): return lax.ppermute(x, 'ctx', pairs)  11.7 us
    ppermute x2, waiting for transfers between devices, shift_to_below(): return lax.ppermute(x, 'ctx', pairs)  10.3 us
    gather x2, local copies, waits for them, and re-layouts, on_device(): held_parts.append(jnp.take(sent, held_sources, axis=0))  5.74 us
  transfers between devices with their start and end apart: 8, of which 5 were waited for; matrix products, arithmetic and copies ran while one was open for 11% of the time, Pallas kernels for 30%

profile of v10, /device:TPU:60, one launch (start us, length us, event | category | flops | bytes accessed | tf_op | source)
XLA Modules:
  0.0 265.5 jit_solution(3441588714444980101)
XLA Ops:
  0.6 3.2 %copy.21 = bf16[128,8192]{0,1:T(8,128)(2,1)S(1)} copy(bf16[128,8192]{1,0:T(8,128)(2,1)} %param.8) | data formatting | bytes 4194304 | tf_op args[0]
  3.9 1.2 copy.29
  5.1 4.1 %copy.23 = bf16[128,8192]{0,1:T(8,128)(2,1)} copy(bf16[128,8192]{1,0:T(8,128)(2,1)} %param.11) | data formatting | bytes 4194304 | tf_op args[3]
  9.2 1.2 slice.165
  10.4 1.2 copy.30
  11.5 2.6 pad_maximum_fusion.4
  14.2 7.2 %all-to-all-start = ((bf16[128,8,768]{2,0,1:T(8,128)(2,1)}), bf16[128,8,768]{2,0,1:T(8,128)(2,1)}, u32[]{:S(2)}, u32[]{:S(2)}) async-start(bf16[128,8,768]{2,0,1:T(8,128)(2,1)} %pad_maximum_fusion.4), calls=%async_computation | async-start | bytes 3145728 | tf_op jit(solution)/shard_map/all_to_all | solution.py:284
  22.9 1.9 collective-permute-start.1
  24.9 1.6 slice.168
  26.5 3.5 %collective-permute-start = (bf16[384,256]{1,0:T(8,128)(2,1)}, bf16[384,256]{1,0:T(8,128)(2,1)}, u32[]{:S(2)}, u32[]{:S(2)}) collective-permute-start(bf16[384,256]{1,0:T(8,128)(2,1)} %slice.168), channel_id=1, source_target_pairs={{0,16},{8,24},{16,32},{24,40},{32,48},{40,56},{48,64},{56,72},{64,... | collective-permute-start | bytes 589832 | tf_op jit(solution)/shard_map/ppermute | solution.py:245
  32.0 1.7 copy.32
  33.7 1.7 pad_maximum_fusion.1
  35.4 8.3 %collective-permute-done = bf16[384,256]{1,0:T(8,128)(2,1)} collective-permute-done((bf16[384,256]{1,0:T(8,128)(2,1)}, bf16[384,256]{1,0:T(8,128)(2,1)}, u32[]{:S(2)}, u32[]{:S(2)}) %collective-permute-start) | collective-permute-done | bytes 196640 | tf_op jit(solution)/shard_map/ppermute | solution.py:245
  43.7 3.4 %collective-permute-done.1 = bf16[1024,256]{1,0:T(8,128)(2,1)} collective-permute-done((bf16[1024,256]{1,0:T(8,128)(2,1)}, bf16[1024,256]{1,0:T(8,128)(2,1)}, u32[]{:S(2)}, u32[]{:S(2)}) %collective-permute-start.1) | collective-permute-done | bytes 524320 | tf_op jit(solution)/shard_map/ppermute | solution.py:245
  47.2 2.4 pad_maximum_fusion.5
  49.5 2.0 all-to-all-done
  51.5 5.0 %all-to-all-start.2 = ((bf16[128,8,1280]{2,0,1:T(8,128)(2,1)}), bf16[128,8,1280]{2,0,1:T(8,128)(2,1)S(1)}, u32[]{:S(2)}, u32[]{:S(2)}) async-start(bf16[128,8,1280]{2,0,1:T(8,128)(2,1)} %pad_maximum_fusion.1), calls=%async_computation.2 | async-start | bytes 5242880 | tf_op jit(solution)/shard_map/all_to_all | solution.py:284
  59.3 2.5 fusion.11
  61.8 2.7 %fusion.10 = (bf16[8,128,384]{2,1,0:T(8,128)(2,1)}, bf16[8,128,384]{2,1,0:T(8,128)(2,1)}) fusion(bf16[8,128,768]{2,1,0:T(8,128)(2,1)} %bitcast.7), kind=kLoop, calls=%fused_computation.44 | loop fusion | bytes 3145728 | tf_op jit(solution)/shard_map/slice | solution.py:289
  64.5 31.5 %shard_map.93 = (bf16[16,128,768]{2,1,0:T(8,128)(2,1)}, f32[2432,128]{1,0:T(8,128)}, f32[2432,128]{1,0:T(8,128)}) custom-call(s32[8]{0:T(128)} %dynamic-slice_bitcast_fusion.slot_ref, s32[8,128,1]{2,1,0:T(8,128)} %copy.25.qdoc_ref, s32[8,1,1536]{2,1,0:T(1,128)} %reshape.122.kdoc_ref, bf16[8,128,384]{2,1,0:T(8,128)(2,1)} %get-tuple-element.43.q_ref, ...), custom_call_target="tpu_custom_call" | custom-call | tf_op jit(solution)/shard_map/pallas_call | solution.py:231
  96.1 6.9 %all-to-all-start.1 = ((bf16[16,128,768]{2,1,0:T(8,128)(2,1)}), bf16[16,128,768]{2,1,0:T(8,128)(2,1)}, u32[]{:S(2)}, u32[]{:S(2)}) async-start(bf16[16,128,768]{2,1,0:T(8,128)(2,1)} %get-tuple-element.26), calls=%async_computation.1 | async-start | bytes 6291456 | tf_op jit(solution)/shard_map/all_to_all | solution.py:305
  103.0 1.9 fusion.8
  104.8 49.2 %shard_map.94 = (bf16[16,128,1280]{2,1,0:T(8,128)(2,1)}, f32[2432,128]{1,0:T(8,128)}, f32[2432,128]{1,0:T(8,128)}) custom-call(s32[8]{0:T(128)} %dynamic-slice_bitcast_fusion.slot_ref, s32[8,128,1]{2,1,0:T(8,128)} %copy.25.qdoc_ref, s32[8,1,1536]{2,1,0:T(1,128)} %reshape.122.kdoc_ref, bf16[8,128,640]{2,1,0:T(8,128)(2,1)} %get-tuple-element.39.q_ref, ...), custom_call_target="tpu_custom_call" | custom-call | tf_op jit(solution)/shard_map/pallas_call | solution.py:231
  154.0 1.6 add.53
  156.3 2.2 collective-permute-start.2
  158.6 3.4 %collective-permute-start.3 = (bf16[384,256]{1,0:T(8,128)(2,1)S(1)}, bf16[384,256]{1,0:T(8,128)(2,1)S(1)}, u32[]{:S(2)}, u32[]{:S(2)}) collective-permute-start(bf16[384,256]{1,0:T(8,128)(2,1)S(1)} %slice.177), channel_id=1, source_target_pairs={{16,0},{24,8},{32,16},{40,24},{48,32},{56,40},{64,48},{72,56},{80,... | collective-permute-start | bytes 589832 | tf_op jit(solution)/shard_map/ppermute | solution.py:250
  161.9 10.3 %collective-permute-done.3 = bf16[384,256]{1,0:T(8,128)(2,1)S(1)} collective-permute-done((bf16[384,256]{1,0:T(8,128)(2,1)S(1)}, bf16[384,256]{1,0:T(8,128)(2,1)S(1)}, u32[]{:S(2)}, u32[]{:S(2)}) %collective-permute-start.3) | collective-permute-done | bytes 196640 | tf_op jit(solution)/shard_map/ppermute | solution.py:250
  172.2 5.7 %all-to-all-start.3 = ((bf16[16,128,1280]{2,1,0:T(8,128)(2,1)}), bf16[16,128,1280]{2,1,0:T(8,128)(2,1)}, u32[]{:S(2)}, u32[]{:S(2)}) async-start(bf16[16,128,1280]{2,1,0:T(8,128)(2,1)} %get-tuple-element.33), calls=%async_computation.3 | async-start | bytes 10485760 | tf_op jit(solution)/shard_map/all_to_all | solution.py:305
  179.6 2.5 gather_fusion
  183.4 74.8 %all-to-all-done.3 = bf16[16,128,1280]{2,1,0:T(8,128)(2,1)} async-done(((bf16[16,128,1280]{2,1,0:T(8,128)(2,1)}), bf16[16,128,1280]{2,1,0:T(8,128)(2,1)}, u32[]{:S(2)}, u32[]{:S(2)}) %all-to-all-start.3) | async-done | bytes 5242912 | tf_op jit(solution)/shard_map/all_to_all | solution.py:305
  258.2 3.2 %gather_fusion.1 = bf16[8,128,1280]{2,1,0:T(8,128)(2,1)S(1)} fusion(bf16[16,128,1280]{2,1,0:T(8,128)(2,1)} %all-to-all-done.3, s32[1024]{0:T(1024)S(1)} %pad_clamp_fusion), kind=kCustom, calls=%fused_computation.1 | custom fusion | bytes 5242912 | tf_op jit(solution)/shard_map/jit(_take)/gather | solution.py:306
  262.9 2.6 pad_maximum_fusion.2
  (63 shorter events, 11.3 us)
Async XLA Ops:
  14.2 7.2 %copy-start.5 = (bf16[1024,128]{1,0:T(8,128)(2,1)S(1)}, bf16[1024,128]{1,0:T(8,128)(2,1)}, u32[]{:S(2)}) copy-start(bf16[1024,128]{1,0:T(8,128)(2,1)} %param.9) | copy-start | bytes 786436
  14.2 8.0 %copy-start.6 = (bf16[1024,128]{1,0:T(8,128)(2,1)S(1)}, bf16[1024,128]{1,0:T(8,128)(2,1)}, u32[]{:S(2)}) copy-start(bf16[1024,128]{1,0:T(8,128)(2,1)} %param.10) | copy-start | bytes 786436
  14.2 37.3 %all-to-all-start = ((bf16[128,8,768]{2,0,1:T(8,128)(2,1)}), bf16[128,8,768]{2,0,1:T(8,128)(2,1)}, u32[]{:S(2)}, u32[]{:S(2)}) async-start(bf16[128,8,768]{2,0,1:T(8,128)(2,1)} %pad_maximum_fusion.4), calls=%async_computation | async-start | bytes 3145728 | tf_op jit(solution)/shard_map/all_to_all | solution.py:284
  21.4 8.7 %copy-start = (bf16[128,8192]{0,1:T(8,128)(2,1)S(1)}, bf16[128,8192]{0,1:T(8,128)(2,1)}, u32[]{:S(2)}) copy-start(bf16[128,8192]{0,1:T(8,128)(2,1)} %copy.23) | copy-start | bytes 6291460
  22.9 24.2 %collective-permute-start.1 = (bf16[1024,256]{1,0:T(8,128)(2,1)}, bf16[1024,256]{1,0:T(8,128)(2,1)}, u32[]{:S(2)}, u32[]{:S(2)}) collective-permute-start(bf16[1024,256]{1,0:T(8,128)(2,1)} %constant_dynamic-update-slice_fusion), channel_id=1, source_target_pairs={{0,8},{8,16},{16,24},{24,32},{32,40},{40,48},{48,56},{56,64},{64,7... | collective-permute-start | bytes 1572872 | tf_op jit(solution)/shard_map/ppermute | solution.py:245
  26.5 17.3 %collective-permute-start = (bf16[384,256]{1,0:T(8,128)(2,1)}, bf16[384,256]{1,0:T(8,128)(2,1)}, u32[]{:S(2)}, u32[]{:S(2)}) collective-permute-start(bf16[384,256]{1,0:T(8,128)(2,1)} %slice.168), channel_id=1, source_target_pairs={{0,16},{8,24},{16,32},{24,40},{32,48},{40,56},{48,64},{56,72},{64,... | collective-permute-start | bytes 589832 | tf_op jit(solution)/shard_map/ppermute | solution.py:245
  49.5 7.0 %copy-start.8 = (s32[128]{0:T(128)S(1)}, s32[128]{0:T(128)}, u32[]{:S(2)}) copy-start(s32[128]{0:T(128)} %param.13) | copy-start | bytes 1540
  49.5 7.1 %copy-start.7 = (s32[16384]{0:T(1024)S(1)}, s32[16384]{0:T(1024)}, u32[]{:S(2)}) copy-start(s32[16384]{0:T(1024)} %param.12) | copy-start | bytes 196612
  51.5 44.6 %all-to-all-start.2 = ((bf16[128,8,1280]{2,0,1:T(8,128)(2,1)}), bf16[128,8,1280]{2,0,1:T(8,128)(2,1)S(1)}, u32[]{:S(2)}, u32[]{:S(2)}) async-start(bf16[128,8,1280]{2,0,1:T(8,128)(2,1)} %pad_maximum_fusion.1), calls=%async_computation.2 | async-start | bytes 5242880 | tf_op jit(solution)/shard_map/all_to_all | solution.py:284
  96.1 76.2 %all-to-all-start.1 = ((bf16[16,128,768]{2,1,0:T(8,128)(2,1)}), bf16[16,128,768]{2,1,0:T(8,128)(2,1)}, u32[]{:S(2)}, u32[]{:S(2)}) async-start(bf16[16,128,768]{2,1,0:T(8,128)(2,1)} %get-tuple-element.26), calls=%async_computation.1 | async-start | bytes 6291456 | tf_op jit(solution)/shard_map/all_to_all | solution.py:305
  104.8 49.2 %copy-start.3 = (f32[2432,128]{1,0:T(8,128)S(1)}, f32[2432,128]{1,0:T(8,128)}, u32[]{:S(2)}) copy-start(f32[2432,128]{1,0:T(8,128)} %get-tuple-element.31) | copy-start | bytes 3735556
  154.0 1.7 copy-start.2
  154.0 2.0 copy-start.4
  156.3 15.9 %collective-permute-start.2 = (bf16[1024,256]{1,0:T(8,128)(2,1)S(1)}, bf16[1024,256]{1,0:T(8,128)(2,1)S(1)}, u32[]{:S(2)}, u32[]{:S(2)}) collective-permute-start(bf16[1024,256]{1,0:T(8,128)(2,1)S(1)} %slice.176), channel_id=1, source_target_pairs={{8,0},{16,8},{24,16},{32,24},{40,32},{48,40},{56,48},{64,56},{72,6... | collective-permute-start | bytes 1572872 | tf_op jit(solution)/shard_map/ppermute | solution.py:250
  158.6 13.7 %collective-permute-start.3 = (bf16[384,256]{1,0:T(8,128)(2,1)S(1)}, bf16[384,256]{1,0:T(8,128)(2,1)S(1)}, u32[]{:S(2)}, u32[]{:S(2)}) collective-permute-start(bf16[384,256]{1,0:T(8,128)(2,1)S(1)} %slice.177), channel_id=1, source_target_pairs={{16,0},{24,8},{32,16},{40,24},{48,32},{56,40},{64,48},{72,56},{80,... | collective-permute-start | bytes 589832 | tf_op jit(solution)/shard_map/ppermute | solution.py:250
  172.2 86.0 %all-to-all-start.3 = ((bf16[16,128,1280]{2,1,0:T(8,128)(2,1)}), bf16[16,128,1280]{2,1,0:T(8,128)(2,1)}, u32[]{:S(2)}, u32[]{:S(2)}) async-start(bf16[16,128,1280]{2,1,0:T(8,128)(2,1)} %get-tuple-element.33), calls=%async_computation.3 | async-start | bytes 10485760 | tf_op jit(solution)/shard_map/all_to_all | solution.py:305
  261.8 1.1 copy-start.1

commit v11 on v9

--- a/solution.py
+++ b/solution.py
@@ -10,7 +10,7 @@
 HEAD_DIM = 128
 BLOCK = 128
 BAND = 12
-FIRST_SHARE = 3
+FIRST_SHARE = 2
 
 
 def routing(block_owner, ctx_count, ctx_rank, blocks_here):

time: 264 us -> 289 us (1.095)
  waiting for transfers between devices: 96.7 us -> 122 us
    ppermute x2, waiting for transfers between devices: 82.9 us -> 100 us  [shift_to_below(): return lax.ppermute(x, 'ctx', pairs)]
    all_to_all x2, waiting for transfers between devices: 1.99 us -> 18.3 us  [on_device(): both = lax.all_to_all(both, 'tp', split_axis=1, concat_axis=0, tiled=True)]
    ppermute x2, waiting for transfers between devices: 11.8 us -> 3.14 us  [shift_from_below(): return lax.ppermute(x, 'ctx', pairs)]
    unnamed x25 -> x33, local copies, waits for them, and re-layouts: 13.6 us -> 16 us
  transfers between devices with their start and end apart: 8 -> 8, of which waited for: 5 -> 5; matrix products, arithmetic and copies ran while one was open for 11% -> 10% of each run, Pallas kernels for 31% -> 28%
where the time goes in v11:
time: 289 us; the launch traced here: 288 us
  waiting for transfers between devices  122 us (42%)
  Pallas kernels  80.6 us (28%)
  local copies, waits for them, and re-layouts  37.7 us (13%)
  starting transfers between devices  35 us (12%)
  other arithmetic  11.9 us (4%)
    ppermute x2, waiting for transfers between devices, shift_to_below(): return lax.ppermute(x, 'ctx', pairs)  100 us
    pallas_call x2, Pallas kernels, fused_attention(): pl.pallas_call(fused_kernel, grid_spec=grid_spec, out_shape=[jax.ShapeDty...  80.6 us
    all_to_all x2, waiting for transfers between devices, on_device(): both = lax.all_to_all(both, 'tp', split_axis=1, concat_axis=0, tiled=True)  18.3 us
    unnamed x33, local copies, waits for them, and re-layouts  16 us
    all_to_all x2, starting transfers between devices, on_device(): both = lax.all_to_all(both, 'tp', split_axis=1, concat_axis=0, tiled=True)  12.1 us
    all_to_all x2, starting transfers between devices, on_device(): lax.all_to_all(results, 'ctx', split_axis=0, concat_axis=0, tiled=True)  11.9 us
  transfers between devices with their start and end apart: 8, of which 5 were waited for; matrix products, arithmetic and copies ran while one was open for 10% of the time, Pallas kernels for 28%

profile of v11, /device:TPU:60, one launch (start us, length us, event | category | flops | bytes accessed | tf_op | source)
XLA Modules:
  0.0 287.8 jit_solution(6181204192167135309)
XLA Ops:
  0.6 3.2 %copy.21 = bf16[128,8192]{0,1:T(8,128)(2,1)S(1)} copy(bf16[128,8192]{1,0:T(8,128)(2,1)} %param.8) | data formatting | bytes 4194304 | tf_op args[0]
  4.1 4.1 %copy.23 = bf16[128,8192]{0,1:T(8,128)(2,1)} copy(bf16[128,8192]{1,0:T(8,128)(2,1)} %param.11) | data formatting | bytes 4194304 | tf_op args[3]
  10.3 2.2 pad_maximum_fusion.5
  12.5 7.1 %all-to-all-start = ((bf16[128,8,512]{2,0,1:T(8,128)(2,1)}), bf16[128,8,512]{2,0,1:T(8,128)(2,1)}, u32[]{:S(2)}, u32[]{:S(2)}) async-start(bf16[128,8,512]{2,0,1:T(8,128)(2,1)} %pad_maximum_fusion.5), calls=%async_computation | async-start | bytes 2097152 | tf_op jit(solution)/shard_map/all_to_all | solution.py:284
  21.1 1.9 collective-permute-start.1
  23.9 3.5 %collective-permute-start = (bf16[384,256]{1,0:T(8,128)(2,1)S(1)}, bf16[384,256]{1,0:T(8,128)(2,1)S(1)}, u32[]{:S(2)}, u32[]{:S(2)}) collective-permute-start(bf16[384,256]{1,0:T(8,128)(2,1)S(1)} %slice.168), channel_id=1, source_target_pairs={{0,16},{8,24},{16,32},{24,40},{32,48},{40,56},{48,64},{56,72},{64,... | collective-permute-start | bytes 589832 | tf_op jit(solution)/shard_map/ppermute | solution.py:245
  27.5 1.3 slice.172
  28.8 1.3 copy-done.1
  30.1 1.6 copy.31
  31.7 1.6 copy.32
  33.3 3.3 %pad_maximum_fusion = bf16[128,8,1536]{2,0,1:T(8,128)(2,1)} fusion(bf16[128,8,768]{2,0,1:T(8,128)(2,1)} %copy.32, bf16[128,8,768]{2,0,1:T(8,128)(2,1)S(1)} %copy-done.2), kind=kLoop, calls=%fused_computation.2 | loop fusion | flops 6291456 | bytes 6291456 | tf_op jit(solution)/shard_map/concatenate | solution.py:281
  36.5 3.1 %collective-permute-done.1 = bf16[1024,256]{1,0:T(8,128)(2,1)} collective-permute-done((bf16[1024,256]{1,0:T(8,128)(2,1)}, bf16[1024,256]{1,0:T(8,128)(2,1)}, u32[]{:S(2)}, u32[]{:S(2)}) %collective-permute-start.1) | collective-permute-done | bytes 524320 | tf_op jit(solution)/shard_map/ppermute | solution.py:245
  39.7 2.3 pad_maximum_fusion.4
  42.0 2.0 all-to-all-done
  44.0 5.0 %all-to-all-start.2 = ((bf16[128,8,1536]{2,0,1:T(8,128)(2,1)}), bf16[128,8,1536]{2,0,1:T(8,128)(2,1)S(1)}, u32[]{:S(2)}, u32[]{:S(2)}) async-start(bf16[128,8,1536]{2,0,1:T(8,128)(2,1)} %pad_maximum_fusion), calls=%async_computation.2 | async-start | bytes 6291456 | tf_op jit(solution)/shard_map/all_to_all | solution.py:284
  51.7 2.5 fusion.9
  54.2 2.3 fusion.11
  56.5 22.8 %shard_map.93 = (bf16[16,128,512]{2,1,0:T(8,128)(2,1)}, f32[2432,128]{1,0:T(8,128)}, f32[2432,128]{1,0:T(8,128)}) custom-call(s32[8]{0:T(128)} %dynamic-slice_bitcast_fusion.slot_ref, s32[8,128,1]{2,1,0:T(8,128)} %copy.25.qdoc_ref, s32[8,1,1536]{2,1,0:T(1,128)} %reshape.122.kdoc_ref, bf16[8,128,256]{2,1,0:T(8,128)(2,1)} %get-tuple-element.39.q_ref, ...), custom_call_target="tpu_custom_call" | custom-call | tf_op jit(solution)/shard_map/pallas_call | solution.py:231
  79.3 16.3 %all-to-all-done.2 = bf16[128,8,1536]{2,0,1:T(8,128)(2,1)S(1)} async-done(((bf16[128,8,1536]{2,0,1:T(8,128)(2,1)}), bf16[128,8,1536]{2,0,1:T(8,128)(2,1)S(1)}, u32[]{:S(2)}, u32[]{:S(2)}) %all-to-all-start.2) | async-done | bytes 3145760 | tf_op jit(solution)/shard_map/all_to_all | solution.py:284
  95.6 6.0 %all-to-all-start.1 = ((bf16[16,128,512]{2,1,0:T(8,128)(2,1)}), bf16[16,128,512]{2,1,0:T(8,128)(2,1)}, u32[]{:S(2)}, u32[]{:S(2)}) async-start(bf16[16,128,512]{2,1,0:T(8,128)(2,1)} %get-tuple-element.23), calls=%async_computation.1 | async-start | bytes 4194304 | tf_op jit(solution)/shard_map/all_to_all | solution.py:300
  101.6 2.0 fusion.8
  103.6 57.8 %shard_map.94 = (bf16[16,128,1536]{2,1,0:T(8,128)(2,1)}, f32[2432,128]{1,0:T(8,128)}, f32[2432,128]{1,0:T(8,128)}) custom-call(s32[8]{0:T(128)} %dynamic-slice_bitcast_fusion.slot_ref, s32[8,128,1]{2,1,0:T(8,128)} %copy.25.qdoc_ref, s32[8,1,1536]{2,1,0:T(1,128)} %reshape.122.kdoc_ref, bf16[8,128,768]{2,1,0:T(8,128)(2,1)} %get-tuple-element.33.q_ref, ...), custom_call_target="tpu_custom_call" | custom-call | tf_op jit(solution)/shard_map/pallas_call | solution.py:231
  161.5 5.9 %all-to-all-start.3 = ((bf16[16,128,1536]{2,1,0:T(8,128)(2,1)}), bf16[16,128,1536]{2,1,0:T(8,128)(2,1)}, u32[]{:S(2)}, u32[]{:S(2)}) async-start(bf16[16,128,1536]{2,1,0:T(8,128)(2,1)} %get-tuple-element.25), calls=%async_computation.3 | async-start | bytes 12582912 | tf_op jit(solution)/shard_map/all_to_all | solution.py:300
  167.8 2.2 gather_fusion
  170.2 1.1 copy-done.5
  172.0 2.2 collective-permute-start.2
  174.4 1.1 fusion.10
  175.5 3.4 %collective-permute-start.3 = (bf16[384,256]{1,0:T(8,128)(2,1)S(1)}, bf16[384,256]{1,0:T(8,128)(2,1)S(1)}, u32[]{:S(2)}, u32[]{:S(2)}) collective-permute-start(bf16[384,256]{1,0:T(8,128)(2,1)S(1)} %slice.183), channel_id=1, source_target_pairs={{16,0},{24,8},{32,16},{40,24},{48,32},{56,40},{64,48},{72,56},{80,... | collective-permute-start | bytes 589832 | tf_op jit(solution)/shard_map/ppermute | solution.py:250
  178.9 64.3 %collective-permute-done.2 = bf16[1024,256]{1,0:T(8,128)(2,1)S(1)} collective-permute-done((bf16[1024,256]{1,0:T(8,128)(2,1)S(1)}, bf16[1024,256]{1,0:T(8,128)(2,1)S(1)}, u32[]{:S(2)}, u32[]{:S(2)}) %collective-permute-start.2) | collective-permute-done | bytes 524320 | tf_op jit(solution)/shard_map/ppermute | solution.py:250
  243.3 35.8 %collective-permute-done.3 = bf16[384,256]{1,0:T(8,128)(2,1)S(1)} collective-permute-done((bf16[384,256]{1,0:T(8,128)(2,1)S(1)}, bf16[384,256]{1,0:T(8,128)(2,1)S(1)}, u32[]{:S(2)}, u32[]{:S(2)}) %collective-permute-start.3) | collective-permute-done | bytes 196640 | tf_op jit(solution)/shard_map/ppermute | solution.py:250
  280.1 3.5 %gather_fusion.1 = bf16[8,128,1536]{2,1,0:T(8,128)(2,1)S(1)} fusion(bf16[16,128,1536]{2,1,0:T(8,128)(2,1)} %all-to-all-done.3, s32[1024]{0:T(1024)S(1)} %pad_clamp_fusion), kind=kCustom, calls=%fused_computation.1 | custom fusion | bytes 6291488 | tf_op jit(solution)/shard_map/jit(_take)/gather | solution.py:301
  285.3 2.6 pad_maximum_fusion.2
  (71 shorter events, 11.7 us)
Async XLA Ops:
  10.3 9.3 %copy-start.9 = (bf16[1024,128]{1,0:T(8,128)(2,1)S(1)}, bf16[1024,128]{1,0:T(8,128)(2,1)}, u32[]{:S(2)}) copy-start(bf16[1024,128]{1,0:T(8,128)(2,1)} %param.9) | copy-start | bytes 786436
  10.3 10.0 %copy-start.10 = (bf16[1024,128]{1,0:T(8,128)(2,1)S(1)}, bf16[1024,128]{1,0:T(8,128)(2,1)}, u32[]{:S(2)}) copy-start(bf16[1024,128]{1,0:T(8,128)(2,1)} %param.10) | copy-start | bytes 786436
  12.5 31.6 %all-to-all-start = ((bf16[128,8,512]{2,0,1:T(8,128)(2,1)}), bf16[128,8,512]{2,0,1:T(8,128)(2,1)}, u32[]{:S(2)}, u32[]{:S(2)}) async-start(bf16[128,8,512]{2,0,1:T(8,128)(2,1)} %pad_maximum_fusion.5), calls=%async_computation | async-start | bytes 2097152 | tf_op jit(solution)/shard_map/all_to_all | solution.py:284
  20.3 8.4 %copy-start = (bf16[128,8192]{0,1:T(8,128)(2,1)S(1)}, bf16[128,8192]{0,1:T(8,128)(2,1)}, u32[]{:S(2)}) copy-start(bf16[128,8192]{0,1:T(8,128)(2,1)} %copy.23) | copy-start | bytes 6291460
  21.1 18.6 %collective-permute-start.1 = (bf16[1024,256]{1,0:T(8,128)(2,1)}, bf16[1024,256]{1,0:T(8,128)(2,1)}, u32[]{:S(2)}, u32[]{:S(2)}) collective-permute-start(bf16[1024,256]{1,0:T(8,128)(2,1)} %constant_dynamic-update-slice_fusion), channel_id=1, source_target_pairs={{0,8},{8,16},{16,24},{24,32},{32,40},{40,48},{48,56},{56,64},{64,7... | collective-permute-start | bytes 1572872 | tf_op jit(solution)/shard_map/ppermute | solution.py:245
  23.9 12.6 %collective-permute-start = (bf16[384,256]{1,0:T(8,128)(2,1)S(1)}, bf16[384,256]{1,0:T(8,128)(2,1)S(1)}, u32[]{:S(2)}, u32[]{:S(2)}) collective-permute-start(bf16[384,256]{1,0:T(8,128)(2,1)S(1)} %slice.168), channel_id=1, source_target_pairs={{0,16},{8,24},{16,32},{24,40},{32,48},{40,56},{48,64},{56,72},{64,... | collective-permute-start | bytes 589832 | tf_op jit(solution)/shard_map/ppermute | solution.py:245
  28.7 1.4 copy-start.1
  31.7 1.6 copy-start.2
  42.0 7.0 %copy-start.12 = (s32[128]{0:T(128)S(1)}, s32[128]{0:T(128)}, u32[]{:S(2)}) copy-start(s32[128]{0:T(128)} %param.13) | copy-start | bytes 1540
  42.0 7.1 %copy-start.11 = (s32[16384]{0:T(1024)S(1)}, s32[16384]{0:T(1024)}, u32[]{:S(2)}) copy-start(s32[16384]{0:T(1024)} %param.12) | copy-start | bytes 196612
  44.0 51.6 %all-to-all-start.2 = ((bf16[128,8,1536]{2,0,1:T(8,128)(2,1)}), bf16[128,8,1536]{2,0,1:T(8,128)(2,1)S(1)}, u32[]{:S(2)}, u32[]{:S(2)}) async-start(bf16[128,8,1536]{2,0,1:T(8,128)(2,1)} %pad_maximum_fusion), calls=%async_computation.2 | async-start | bytes 6291456 | tf_op jit(solution)/shard_map/all_to_all | solution.py:284
  95.6 65.8 %all-to-all-start.1 = ((bf16[16,128,512]{2,1,0:T(8,128)(2,1)}), bf16[16,128,512]{2,1,0:T(8,128)(2,1)}, u32[]{:S(2)}, u32[]{:S(2)}) async-start(bf16[16,128,512]{2,1,0:T(8,128)(2,1)} %get-tuple-element.23), calls=%async_computation.1 | async-start | bytes 4194304 | tf_op jit(solution)/shard_map/all_to_all | solution.py:300
  161.4 8.6 %copy-start.8 = (f32[2432,128]{1,0:T(8,128)S(1)}, f32[2432,128]{1,0:T(8,128)}, u32[]{:S(2)}) copy-start(f32[2432,128]{1,0:T(8,128)} %get-tuple-element.29) | copy-start | bytes 3735556
  161.5 118.7 %all-to-all-start.3 = ((bf16[16,128,1536]{2,1,0:T(8,128)(2,1)}), bf16[16,128,1536]{2,1,0:T(8,128)(2,1)}, u32[]{:S(2)}, u32[]{:S(2)}) async-start(bf16[16,128,1536]{2,1,0:T(8,128)(2,1)} %get-tuple-element.25), calls=%async_computation.3 | async-start | bytes 12582912 | tf_op jit(solution)/shard_map/all_to_all | solution.py:300
  167.3 2.8 copy-start.6
  170.1 1.3 copy-start.5
  170.1 1.7 copy-start.7
  172.0 71.1 %collective-permute-start.2 = (bf16[1024,256]{1,0:T(8,128)(2,1)S(1)}, bf16[1024,256]{1,0:T(8,128)(2,1)S(1)}, u32[]{:S(2)}, u32[]{:S(2)}) collective-permute-start(bf16[1024,256]{1,0:T(8,128)(2,1)S(1)} %slice.181), channel_id=1, source_target_pairs={{8,0},{16,8},{24,16},{32,24},{40,32},{48,40},{56,48},{64,56},{72,6... | collective-permute-start | bytes 1572872 | tf_op jit(solution)/shard_map/ppermute | solution.py:250
  175.5 103.7 %collective-permute-start.3 = (bf16[384,256]{1,0:T(8,128)(2,1)S(1)}, bf16[384,256]{1,0:T(8,128)(2,1)S(1)}, u32[]{:S(2)}, u32[]{:S(2)}) collective-permute-start(bf16[384,256]{1,0:T(8,128)(2,1)S(1)} %slice.183), channel_id=1, source_target_pairs={{16,0},{24,8},{32,16},{40,24},{48,32},{56,40},{64,48},{72,56},{80,... | collective-permute-start | bytes 589832 | tf_op jit(solution)/shard_map/ppermute | solution.py:250
  284.1 1.0 copy-start.3
  284.1 1.2 copy-start.4

commit v12 on v9

--- a/solution.py
+++ b/solution.py
@@ -200,8 +200,9 @@
     dv_ref[pl.ds(start, window_rows), :] += dv_sum
 
 
-def fused_attention(slots, query_blocks, grad_blocks, halo_key, halo_value, halo_doc, slot_count):
-    blocks, _, width = query_blocks.shape
+def fused_attention(slots, both_blocks, halo_key, halo_value, halo_doc, slot_count):
+    blocks, _, both_width = both_blocks.shape
+    width = both_width // 2
     window_rows = BAND * BLOCK
     reach = (BAND - 1) * BLOCK
     halo_rows = halo_key.shape[0]
@@ -209,7 +210,8 @@
     key_doc = jnp.stack(
         [halo_doc[b * BLOCK : b * BLOCK + window_rows] for b in range(blocks)]
     ).reshape(blocks, 1, window_rows)
-    block_spec = pl.BlockSpec((1, BLOCK, width), lambda b, slot: (b, 0, 0))
+    query_spec = pl.BlockSpec((1, BLOCK, width), lambda b, slot: (b, 0, 0))
+    grad_spec = pl.BlockSpec((1, BLOCK, width), lambda b, slot: (b, 0, 1))
     whole = pl.BlockSpec((halo_rows, HEAD_DIM), lambda b, slot: (0, 0))
     grid_spec = pltpu.PrefetchScalarGridSpec(
         num_scalar_prefetch=1,
@@ -217,8 +219,8 @@
         in_specs=[
             pl.BlockSpec((1, BLOCK, 1), lambda b, slot: (b, 0, 0)),
             pl.BlockSpec((1, 1, window_rows), lambda b, slot: (b, 0, 0)),
-            block_spec,
-            block_spec,
+            query_spec,
+            grad_spec,
             whole,
             whole,
         ],
@@ -237,7 +239,7 @@
             jax.ShapeDtypeStruct((halo_rows, HEAD_DIM), jnp.float32),
         ],
         compiler_params=pltpu.CompilerParams(dimension_semantics=("arbitrary",)),
-    )(slots, query_doc, key_doc, query_blocks, grad_blocks, halo_key, halo_value)
+    )(slots, query_doc, key_doc, both_blocks, both_blocks, halo_key, halo_value)
 
 
 def shift_from_below(x, ctx_count, distance):
@@ -285,8 +287,7 @@
         both = both.reshape(blocks_here, BLOCK, 2 * chunk_cols)
         results, chunk_key_grad, chunk_value_grad = fused_attention(
             own_targets,
-            both[..., :chunk_cols],
-            both[..., chunk_cols:],
+            both,
             halo_key,
             halo_value,
             halo_doc,

time: 264 us -> 261 us (0.989)
    slice x2 -> x0, local copies, waits for them, and re-layouts: 4.58 us -> none  [on_device(): both[..., chunk_cols:]]
    ppermute x2, waiting for transfers between devices: 11.8 us -> 8.49 us  [shift_from_below(): return lax.ppermute(x, 'ctx', pairs)]
    unnamed x25 -> x33, local copies, waits for them, and re-layouts: 13.6 us -> 16.7 us
  transfers between devices with their start and end apart: 8 -> 8, of which waited for: 5 -> 6; matrix products, arithmetic and copies ran while one was open for 11% -> 10% of each run, Pallas kernels for 31% -> 31%
where the time goes in v12:
time: 261 us; the launch traced here: 260 us
  waiting for transfers between devices  95.7 us (37%)
  Pallas kernels  80.6 us (31%)
  local copies, waits for them, and re-layouts  35.7 us (14%)
  starting transfers between devices  35 us (13%)
  other arithmetic  12.3 us (5%)
    ppermute x2, waiting for transfers between devices, shift_to_below(): return lax.ppermute(x, 'ctx', pairs)  82.9 us
    pallas_call x2, Pallas kernels, fused_attention(): pl.pallas_call(fused_kernel, grid_spec=grid_spec, out_shape=[jax.ShapeDty...  80.6 us
    unnamed x33, local copies, waits for them, and re-layouts  16.7 us
    all_to_all x2, starting transfers between devices, on_device(): both = lax.all_to_all(both, 'tp', split_axis=1, concat_axis=0, tiled=True)  12.1 us
    all_to_all x2, starting transfers between devices, on_device(): lax.all_to_all(results, 'ctx', split_axis=0, concat_axis=0, tiled=True)  11.8 us
    ppermute x2, waiting for transfers between devices, shift_from_below(): return lax.ppermute(x, 'ctx', pairs)  8.49 us
    gather x2, local copies, waits for them, and re-layouts, on_device(): held_parts.append(jnp.take(sent, held_sources, axis=0))  5.74 us
    ppermute x2, starting transfers between devices, shift_from_below(): return lax.ppermute(x, 'ctx', pairs)  5.59 us
  transfers between devices with their start and end apart: 8, of which 6 were waited for; matrix products, arithmetic and copies ran while one was open for 10% of the time, Pallas kernels for 31%

profile of v12, /device:TPU:60, one launch (start us, length us, event | category | flops | bytes accessed | tf_op | source)
XLA Modules:
  0.0 260.3 jit_solution(13241921742679537150)
XLA Ops:
  0.6 3.2 %copy.21 = bf16[128,8192]{0,1:T(8,128)(2,1)S(1)} copy(bf16[128,8192]{1,0:T(8,128)(2,1)} %param.8) | data formatting | bytes 4194304 | tf_op args[0]
  3.9 1.5 copy.29
  5.4 4.1 %copy.23 = bf16[128,8192]{0,1:T(8,128)(2,1)} copy(bf16[128,8192]{1,0:T(8,128)(2,1)} %param.11) | data formatting | bytes 4194304 | tf_op args[3]
  9.5 1.3 slice.149
  11.1 1.3 pad_maximum_fusion.4
  12.4 7.2 %all-to-all-start = ((bf16[128,8,768]{2,0,1:T(8,128)(2,1)}), bf16[128,8,768]{2,0,1:T(8,128)(2,1)S(1)}, u32[]{:S(2)}, u32[]{:S(2)}) async-start(bf16[128,8,768]{2,0,1:T(8,128)(2,1)} %pad_maximum_fusion.4), calls=%async_computation | async-start | bytes 3145728 | tf_op jit(solution)/shard_map/all_to_all | solution.py:286
  19.8 2.1 collective-permute-start.1
  22.6 3.5 %collective-permute-start = (bf16[384,256]{1,0:T(8,128)(2,1)}, bf16[384,256]{1,0:T(8,128)(2,1)}, u32[]{:S(2)}, u32[]{:S(2)}) collective-permute-start(bf16[384,256]{1,0:T(8,128)(2,1)} %slice.150), channel_id=1, source_target_pairs={{0,16},{8,24},{16,32},{24,40},{32,48},{40,56},{48,64},{56,72},{64,... | collective-permute-start | bytes 589832 | tf_op jit(solution)/shard_map/ppermute | solution.py:247
  26.1 2.5 slice.154
  29.7 1.7 copy.31
  31.5 2.4 copy.32
  33.9 3.0 %pad_maximum_fusion.1 = bf16[128,8,1280]{2,0,1:T(8,128)(2,1)} fusion(bf16[128,8,640]{2,0,1:T(8,128)(2,1)} %copy.32, bf16[128,8,640]{2,0,1:T(8,128)(2,1)S(1)} %copy.31), kind=kLoop, calls=%fused_computation.5 | loop fusion | flops 5242880 | bytes 5242880 | tf_op jit(solution)/shard_map/concatenate | solution.py:283
  36.9 5.1 %collective-permute-done = bf16[384,256]{1,0:T(8,128)(2,1)} collective-permute-done((bf16[384,256]{1,0:T(8,128)(2,1)}, bf16[384,256]{1,0:T(8,128)(2,1)}, u32[]{:S(2)}, u32[]{:S(2)}) %collective-permute-start) | collective-permute-done | bytes 196640 | tf_op jit(solution)/shard_map/ppermute | solution.py:247
  42.0 3.4 %collective-permute-done.1 = bf16[1024,256]{1,0:T(8,128)(2,1)} collective-permute-done((bf16[1024,256]{1,0:T(8,128)(2,1)S(1)}, bf16[1024,256]{1,0:T(8,128)(2,1)}, u32[]{:S(2)}, u32[]{:S(2)}) %collective-permute-start.1) | collective-permute-done | bytes 524320 | tf_op jit(solution)/shard_map/ppermute | solution.py:247
  45.4 2.2 pad_maximum_fusion.5
  47.6 2.0 all-to-all-done
  50.8 4.9 %all-to-all-start.2 = ((bf16[128,8,1280]{2,0,1:T(8,128)(2,1)}), bf16[128,8,1280]{2,0,1:T(8,128)(2,1)S(1)}, u32[]{:S(2)}, u32[]{:S(2)}) async-start(bf16[128,8,1280]{2,0,1:T(8,128)(2,1)} %pad_maximum_fusion.1), calls=%async_computation.2 | async-start | bytes 5242880 | tf_op jit(solution)/shard_map/all_to_all | solution.py:286
  58.4 2.5 fusion.9
  60.8 31.5 %shard_map.93 = (bf16[16,128,768]{2,1,0:T(8,128)(2,1)}, f32[2432,128]{1,0:T(8,128)}, f32[2432,128]{1,0:T(8,128)}) custom-call(s32[8]{0:T(128)} %dynamic-slice_bitcast_fusion.slot_ref, s32[8,128,1]{2,1,0:T(8,128)} %copy.25.qdoc_ref, s32[8,1,1536]{2,1,0:T(1,128)} %reshape.122.kdoc_ref, bf16[8,128,768]{2,1,0:T(8,128)(2,1)} %bitcast.25, ...), custom_call_target="tpu_custom_call" | custom-call | tf_op jit(solution)/shard_map/pallas_call | solution.py:233
  92.3 2.2 all-to-all-done.2
  94.6 1.5 copy-done
  96.0 5.9 %all-to-all-start.1 = ((bf16[16,128,768]{2,1,0:T(8,128)(2,1)}), bf16[16,128,768]{2,1,0:T(8,128)(2,1)}, u32[]{:S(2)}, u32[]{:S(2)}) async-start(bf16[16,128,768]{2,1,0:T(8,128)(2,1)} %get-tuple-element.23), calls=%async_computation.1 | async-start | bytes 6291456 | tf_op jit(solution)/shard_map/all_to_all | solution.py:301
  101.9 49.1 %shard_map.94 = (bf16[16,128,1280]{2,1,0:T(8,128)(2,1)}, f32[2432,128]{1,0:T(8,128)}, f32[2432,128]{1,0:T(8,128)}) custom-call(s32[8]{0:T(128)} %dynamic-slice_bitcast_fusion.slot_ref, s32[8,128,1]{2,1,0:T(8,128)} %copy.25.qdoc_ref, s32[8,1,1536]{2,1,0:T(1,128)} %reshape.122.kdoc_ref, bf16[8,128,1280]{2,1,0:T(8,128)(2,1)} %bitcast.23, ...), custom_call_target="tpu_custom_call" | custom-call | tf_op jit(solution)/shard_map/pallas_call | solution.py:233
  151.0 5.9 %all-to-all-start.3 = ((bf16[16,128,1280]{2,1,0:T(8,128)(2,1)}), bf16[16,128,1280]{2,1,0:T(8,128)(2,1)}, u32[]{:S(2)}, u32[]{:S(2)}) async-start(bf16[16,128,1280]{2,1,0:T(8,128)(2,1)} %get-tuple-element.25), calls=%async_computation.3 | async-start | bytes 10485760 | tf_op jit(solution)/shard_map/all_to_all | solution.py:301
  157.4 1.7 add.53
  159.4 2.2 collective-permute-start.2
  161.6 3.4 %collective-permute-start.3 = (bf16[384,256]{1,0:T(8,128)(2,1)S(1)}, bf16[384,256]{1,0:T(8,128)(2,1)S(1)}, u32[]{:S(2)}, u32[]{:S(2)}) collective-permute-start(bf16[384,256]{1,0:T(8,128)(2,1)S(1)} %slice.163), channel_id=1, source_target_pairs={{16,0},{24,8},{32,16},{40,24},{48,32},{56,40},{64,48},{72,56},{80,... | collective-permute-start | bytes 589832 | tf_op jit(solution)/shard_map/ppermute | solution.py:252
  165.0 56.5 %collective-permute-done.2 = bf16[1024,256]{1,0:T(8,128)(2,1)S(1)} collective-permute-done((bf16[1024,256]{1,0:T(8,128)(2,1)S(1)}, bf16[1024,256]{1,0:T(8,128)(2,1)S(1)}, u32[]{:S(2)}, u32[]{:S(2)}) %collective-permute-start.2) | collective-permute-done | bytes 524320 | tf_op jit(solution)/shard_map/ppermute | solution.py:252
  221.6 26.5 %collective-permute-done.3 = bf16[384,256]{1,0:T(8,128)(2,1)S(1)} collective-permute-done((bf16[384,256]{1,0:T(8,128)(2,1)S(1)}, bf16[384,256]{1,0:T(8,128)(2,1)S(1)}, u32[]{:S(2)}, u32[]{:S(2)}) %collective-permute-start.3) | collective-permute-done | bytes 196640 | tf_op jit(solution)/shard_map/ppermute | solution.py:252
  249.1 2.5 gather_fusion
  253.0 3.2 %gather_fusion.1 = bf16[8,128,1280]{2,1,0:T(8,128)(2,1)S(1)} fusion(bf16[16,128,1280]{2,1,0:T(8,128)(2,1)} %all-to-all-done.3, s32[1024]{0:T(1024)S(1)} %pad_clamp_fusion), kind=kCustom, calls=%fused_computation.1 | custom fusion | bytes 5242912 | tf_op jit(solution)/shard_map/jit(_take)/gather | solution.py:302
  257.6 2.6 %pad_maximum_fusion.2 = (bf16[8,128,1024]{2,1,0:T(8,128)(2,1)}, bf16[8,128,1024]{2,1,0:T(8,128)(2,1)}) fusion(bf16[8,128,640]{2,1,0:T(8,128)(2,1)S(1)} %get-tuple-element.31, bf16[8,128,384]{2,1,0:T(8,128)(2,1)S(1)} %copy-done.4, bf16[8,128,640]{2,1,0:T(8,128)(2,1)S(1)} %get-tuple-element.30, bf16[8,128,384]{2,1,0:T(8,128)(2,1)S(1)} %get-tuple-element.32), kind=kLoop, calls=%fused_computation.8 | loop fusion | flops 8388608 | bytes 8388608 | tf_op jit(solution)/shard_map/concatenate | solution.py:309
  (69 shorter events, 10.9 us)
Async XLA Ops:
  3.9 5.6 %copy-start.2 = (bf16[128,8192]{0,1:T(8,128)(2,1)}, bf16[128,8192]{0,1:T(8,128)(2,1)S(1)}, u32[]{:S(2)}) copy-start(bf16[128,8192]{0,1:T(8,128)(2,1)S(1)} %copy.21) | copy-start | bytes 6291460
  9.5 1.6 copy-start.5
  12.4 7.2 %copy-start.9 = (bf16[1024,128]{1,0:T(8,128)(2,1)S(1)}, bf16[1024,128]{1,0:T(8,128)(2,1)}, u32[]{:S(2)}) copy-start(bf16[1024,128]{1,0:T(8,128)(2,1)} %param.9) | copy-start | bytes 786436
  12.4 7.3 %copy-start.10 = (bf16[1024,128]{1,0:T(8,128)(2,1)S(1)}, bf16[1024,128]{1,0:T(8,128)(2,1)}, u32[]{:S(2)}) copy-start(bf16[1024,128]{1,0:T(8,128)(2,1)} %param.10) | copy-start | bytes 786436
  12.4 37.2 %all-to-all-start = ((bf16[128,8,768]{2,0,1:T(8,128)(2,1)}), bf16[128,8,768]{2,0,1:T(8,128)(2,1)S(1)}, u32[]{:S(2)}, u32[]{:S(2)}) async-start(bf16[128,8,768]{2,0,1:T(8,128)(2,1)} %pad_maximum_fusion.4), calls=%async_computation | async-start | bytes 3145728 | tf_op jit(solution)/shard_map/all_to_all | solution.py:286
  19.7 8.9 %copy-start.3 = (bf16[128,8192]{0,1:T(8,128)(2,1)S(1)}, bf16[128,8192]{0,1:T(8,128)(2,1)}, u32[]{:S(2)}) copy-start(bf16[128,8192]{0,1:T(8,128)(2,1)} %copy.23) | copy-start | bytes 6291460
  19.8 25.6 %collective-permute-start.1 = (bf16[1024,256]{1,0:T(8,128)(2,1)S(1)}, bf16[1024,256]{1,0:T(8,128)(2,1)}, u32[]{:S(2)}, u32[]{:S(2)}) collective-permute-start(bf16[1024,256]{1,0:T(8,128)(2,1)S(1)} %constant_dynamic-update-slice_fusion), channel_id=1, source_target_pairs={{0,8},{8,16},{16,24},{24,32},{32,40},{40,48},{48,56},{56,64},{64,7... | collective-permute-start | bytes 1572872 | tf_op jit(solution)/shard_map/ppermute | solution.py:247
  22.6 19.4 %collective-permute-start = (bf16[384,256]{1,0:T(8,128)(2,1)}, bf16[384,256]{1,0:T(8,128)(2,1)}, u32[]{:S(2)}, u32[]{:S(2)}) collective-permute-start(bf16[384,256]{1,0:T(8,128)(2,1)} %slice.150), channel_id=1, source_target_pairs={{0,16},{8,24},{16,32},{24,40},{32,48},{40,56},{48,64},{56,72},{64,... | collective-permute-start | bytes 589832 | tf_op jit(solution)/shard_map/ppermute | solution.py:247
  47.6 8.0 %copy-start.12 = (s32[128]{0:T(128)S(1)}, s32[128]{0:T(128)}, u32[]{:S(2)}) copy-start(s32[128]{0:T(128)} %param.13) | copy-start | bytes 1540
  47.6 8.1 %copy-start.11 = (s32[16384]{0:T(1024)S(1)}, s32[16384]{0:T(1024)}, u32[]{:S(2)}) copy-start(s32[16384]{0:T(1024)} %param.12) | copy-start | bytes 196612
  49.6 1.1 copy-start.1
  50.8 43.8 %all-to-all-start.2 = ((bf16[128,8,1280]{2,0,1:T(8,128)(2,1)}), bf16[128,8,1280]{2,0,1:T(8,128)(2,1)S(1)}, u32[]{:S(2)}, u32[]{:S(2)}) async-start(bf16[128,8,1280]{2,0,1:T(8,128)(2,1)} %pad_maximum_fusion.1), calls=%async_computation.2 | async-start | bytes 5242880 | tf_op jit(solution)/shard_map/all_to_all | solution.py:286
  94.6 1.5 copy-start
  96.0 55.0 %all-to-all-start.1 = ((bf16[16,128,768]{2,1,0:T(8,128)(2,1)}), bf16[16,128,768]{2,1,0:T(8,128)(2,1)}, u32[]{:S(2)}, u32[]{:S(2)}) async-start(bf16[16,128,768]{2,1,0:T(8,128)(2,1)} %get-tuple-element.23), calls=%async_computation.1 | async-start | bytes 6291456 | tf_op jit(solution)/shard_map/all_to_all | solution.py:301
  151.0 6.4 %copy-start.7 = (f32[2432,128]{1,0:T(8,128)S(1)}, f32[2432,128]{1,0:T(8,128)}, u32[]{:S(2)}) copy-start(f32[2432,128]{1,0:T(8,128)} %get-tuple-element.28) | copy-start | bytes 3735556
  151.0 102.0 %all-to-all-start.3 = ((bf16[16,128,1280]{2,1,0:T(8,128)(2,1)}), bf16[16,128,1280]{2,1,0:T(8,128)(2,1)}, u32[]{:S(2)}, u32[]{:S(2)}) async-start(bf16[16,128,1280]{2,1,0:T(8,128)(2,1)} %get-tuple-element.25), calls=%async_computation.3 | async-start | bytes 10485760 | tf_op jit(solution)/shard_map/all_to_all | solution.py:301
  156.9 2.2 copy-start.6
  157.1 1.9 copy-start.8
  159.4 62.1 %collective-permute-start.2 = (bf16[1024,256]{1,0:T(8,128)(2,1)S(1)}, bf16[1024,256]{1,0:T(8,128)(2,1)S(1)}, u32[]{:S(2)}, u32[]{:S(2)}) collective-permute-start(bf16[1024,256]{1,0:T(8,128)(2,1)S(1)} %slice.161), channel_id=1, source_target_pairs={{8,0},{16,8},{24,16},{32,24},{40,32},{48,40},{56,48},{64,56},{72,6... | collective-permute-start | bytes 1572872 | tf_op jit(solution)/shard_map/ppermute | solution.py:252
  161.6 86.5 %collective-permute-start.3 = (bf16[384,256]{1,0:T(8,128)(2,1)S(1)}, bf16[384,256]{1,0:T(8,128)(2,1)S(1)}, u32[]{:S(2)}, u32[]{:S(2)}) collective-permute-start(bf16[384,256]{1,0:T(8,128)(2,1)S(1)} %slice.163), channel_id=1, source_target_pairs={{16,0},{24,8},{32,16},{40,24},{48,32},{56,40},{64,48},{72,56},{80,... | collective-permute-start | bytes 589832 | tf_op jit(solution)/shard_map/ppermute | solution.py:252
  256.5 1.1 copy-start.4
